TPU v7x, 256 devices: a whole 4x4x8 slice. The times are simulated.
256 devices in a mesh: hyp: 32 (over y, x, core), head: 8 (over z).
Axes of the slice: x: 4, y: 4, z: 8, core: 2. Of those that a mesh axis runs over, the one named last changes fastest.
Arguments:
- step_embeds: bfloat16 [3, 512, 4096], P(None, 'hyp'), may hold values from -6 to 6
- lang_table: bfloat16 [8, 4096], replicated, may hold values from -3 to 3
- lang_ids: int32 [32, 4], replicated, may hold values from 0 to 7
- self_gain: float32 [4096], replicated, may hold values from 0.1 to 1.9
- self_wq: bfloat16 [4096, 2048], P(None, 'head'), may hold values from -0.09375 to 0.09375
- self_wk: bfloat16 [4096, 2048], P(None, 'head'), may hold values from -0.09375 to 0.09375
- self_wv: bfloat16 [4096, 2048], P(None, 'head'), may hold values from -0.09375 to 0.09375
- self_wo: bfloat16 [2048, 4096], P('head'), may hold values from -0.125 to 0.125
- cross_gain: float32 [4096], replicated, may hold values from 0.1 to 1.9
- cross_wq: bfloat16 [4096, 2048], P(None, 'head'), may hold values from -0.09375 to 0.09375
- cross_wkv: bfloat16 [4096, 4096], P('hyp', 'head'), may hold values from -0.09375 to 0.09375
- encoder_rows: bfloat16 [24576, 4096], P('hyp', 'head'), may hold values from -200 to 200
- doc_lengths: int32 [32], P('hyp'), may hold values from 192 to 768, as said below
- past_keys: bfloat16 [512, 32, 2048], P('hyp', None, 'head'), may hold values from -200 to 200
- past_values: bfloat16 [512, 32, 2048], P('hyp', None, 'head'), may hold values from -6 to 6
- parents: int32 [3, 512], replicated, may hold values from 0 to 3
Outputs:
- cross_context: bfloat16 [3, 512, 2048], P(None, 'hyp', 'head')
- final_keys: bfloat16 [512, 35, 2048], P('hyp', None, 'head')
- final_values: bfloat16 [512, 35, 2048], P('hyp', None, 'head')
Inputs may be any that keep to these rules, and one draw needn't show every extreme that they name: `doc_lengths`: some document has exactly 768 live rows. `parents`: A parent is a beam of the same document and target.
All inputs are finite; a program needn't handle non-finite values.
Results may differ from a plain program's by a relative error of at most 0.03.
Values may be sent and summed in bfloat16 or wider, within the bound.
No kernel may reach another device: no remote copies, remote signals or barrier semaphores. Data moves between devices by JAX's collectives and lax.ppermute only.
A program may use at most 128 MiB of HBM per device.

v0:
```python
import jax
import jax.numpy as jnp
from jax import lax
from jax.sharding import PartitionSpec as P

HEAD = 256
BEAMS = 4
TARGETS = 4
STEPS = 3


EPSILON = 1e-06


def shifted(block, axis, distance):
    devices = range(lax.axis_size(axis))
    route = [((i - distance) % len(devices), i) for i in devices]
    return lax.ppermute(block, axis, route)


def rms_scaled(values_in, gain):
    mean_square = jnp.mean(values_in * values_in, axis=-1, keepdims=True)
    return values_in * lax.rsqrt(mean_square + EPSILON) * gain


def pick_rows(candidates, selector, row_axis):
    shape_list = [1] * candidates[0].ndim
    shape_list[row_axis] = selector.shape[0]
    chosen = candidates[0]
    for position in range(1, len(candidates)):
        chosen = jnp.where((selector == position).reshape(shape_list), candidates[position], chosen)
    return chosen


def partial_attend(queries, cache_stack, scaling):
    row_count = cache_stack.shape[1]
    cached = cache_stack.shape[2]
    heads_here = cache_stack.shape[3] // HEAD
    key_part = cache_stack[0].reshape(row_count, cached, heads_here, HEAD)
    value_part = cache_stack[1].reshape(row_count, cached, heads_here, HEAD).astype(jnp.float32)
    scores = (
        jnp.einsum(
            "rhd,rphd->rhp",
            queries.reshape(row_count, heads_here, HEAD),
            key_part,
            preferred_element_type=jnp.float32,
        )
        * scaling
    )
    highest = jnp.max(scores, axis=2)
    raw_weights = jnp.exp(scores - highest[:, :, None])
    totals = jnp.sum(raw_weights, axis=2)
    summed = jnp.einsum("rhp,rphd->rhd", raw_weights, value_part)
    return (highest, totals, summed)


def cross_attend(queries, cross_keys, cross_values, doc_length, scaling):
    query_rows = queries.shape[0]
    heads_here = cross_keys.shape[1]
    scores = (
        jnp.einsum(
            "qhd,jhd->hqj",
            queries.reshape(query_rows, heads_here, HEAD),
            cross_keys,
            preferred_element_type=jnp.float32,
        )
        * scaling
    )
    live_mask = lax.broadcasted_iota(jnp.int32, (1, 1, cross_keys.shape[0]), 2) < doc_length
    scores = jnp.where(live_mask, scores, -jnp.inf)
    highest = jnp.max(scores, axis=2, keepdims=True)
    raw_weights = jnp.exp(scores - highest)
    totals = jnp.sum(raw_weights, axis=2, keepdims=True)
    weights = (raw_weights / totals).astype(jnp.bfloat16)
    output = jnp.einsum("hqj,jhd->qhd", weights, cross_values, preferred_element_type=jnp.float32)
    return output.reshape(query_rows, heads_here * HEAD).astype(jnp.bfloat16)


def shards(
    step_embeds,
    lang_table,
    lang_ids,
    self_gain,
    self_wq,
    self_wk,
    self_wv,
    self_wo,
    cross_gain,
    cross_wq,
    cross_wkv,
    encoder_rows,
    doc_lengths,
    past_keys,
    past_values,
    parents,
):
    hyp_count = lax.axis_size("hyp")
    group_size = hyp_count // BEAMS
    my_index = lax.axis_index("hyp")
    my_beam = my_index // group_size
    my_slot = my_index % group_size
    row_count = step_embeds.shape[1]
    head_width = self_wq.shape[1]
    heads_here = head_width // HEAD
    doc_count = lang_ids.shape[0]
    scaling = HEAD ** (-0.5)
    my_langs = lax.dynamic_slice_in_dim(lang_ids, my_slot * BEAMS, BEAMS, 0).reshape(row_count)
    one_hot = (
        my_langs[:, None] == lax.broadcasted_iota(jnp.int32, (1, lang_table.shape[0]), 1)
    ).astype(jnp.bfloat16)
    lang_rows = jnp.dot(one_hot, lang_table, preferred_element_type=jnp.float32)
    full_weights = lax.all_gather(cross_wkv, "hyp", axis=0, tiled=True)
    cross_kv = jnp.dot(
        lax.all_gather(encoder_rows, "head", axis=1, tiled=True),
        full_weights,
        preferred_element_type=jnp.float32,
    ).astype(jnp.bfloat16)
    cross_kv = cross_kv.reshape(encoder_rows.shape[0], heads_here, 2, HEAD)
    cross_keys = cross_kv[:, :, 0, :]
    cross_values = cross_kv[:, :, 1, :]
    doc_length = doc_lengths[0]
    parent_view = parents.reshape(parents.shape[0], BEAMS, -1)
    my_parents = lax.dynamic_slice_in_dim(parent_view, my_slot * row_count, row_count, 2)
    own_parents = lax.dynamic_index_in_dim(my_parents, my_beam, 1, keepdims=False)
    contexts = []
    cache_stack = jnp.stack([past_keys, past_values])
    for step_idx in range(STEPS):
        offsets = (my_beam - own_parents[step_idx]) % BEAMS
        moved_list = [cache_stack]
        for peer_hop in range(1, BEAMS):
            moved_list.append(shifted(cache_stack, "hyp", peer_hop * group_size))
        cache_stack = pick_rows(moved_list, offsets, 1)
        start_hidden_in = step_embeds[step_idx].astype(jnp.float32) + lang_rows
        normed = rms_scaled(start_hidden_in, self_gain).astype(jnp.bfloat16)
        new_query = jnp.dot(normed, self_wq, preferred_element_type=jnp.float32).astype(
            jnp.bfloat16
        )
        new_key = jnp.dot(normed, self_wk, preferred_element_type=jnp.float32).astype(jnp.bfloat16)
        new_value = jnp.dot(normed, self_wv, preferred_element_type=jnp.float32).astype(
            jnp.bfloat16
        )
        fresh_rows = jnp.stack([new_key, new_value])[:, :, None, :]
        hidden_in, new_query, fresh_rows = (start_hidden_in, new_query, fresh_rows)
        cache_stack = jnp.concatenate([cache_stack, fresh_rows], axis=2)
        attn_parts = partial_attend(new_query, cache_stack, scaling)
        rows_here = hidden_in.shape[0]
        self_context = (
            (attn_parts[2] / attn_parts[1][:, :, None])
            .reshape(rows_here, head_width)
            .astype(jnp.bfloat16)
        )
        partial_out = jnp.dot(self_context, self_wo, preferred_element_type=jnp.float32)
        residual = hidden_in + lax.psum(partial_out.astype(jnp.bfloat16), "head").astype(
            jnp.float32
        )
        normed_cross = rms_scaled(residual, cross_gain).astype(jnp.bfloat16)
        cross_query = jnp.dot(normed_cross, cross_wq, preferred_element_type=jnp.float32).astype(
            jnp.bfloat16
        )
        every_query = lax.all_gather(cross_query, "hyp", axis=0, tiled=True)
        arranged = every_query.reshape(BEAMS, doc_count, TARGETS, head_width)
        doc_queries = lax.dynamic_index_in_dim(arranged, my_index, 1, keepdims=False)
        answer = cross_attend(
            doc_queries.reshape(BEAMS * TARGETS, head_width),
            cross_keys,
            cross_values,
            doc_length,
            scaling,
        )
        every_answer = lax.all_gather(answer, "hyp", axis=0, tiled=True)
        by_owner = every_answer.reshape(doc_count, BEAMS, TARGETS, head_width)
        my_block = lax.dynamic_slice_in_dim(by_owner, my_slot * BEAMS, BEAMS, 0)
        contexts.append(
            lax.dynamic_index_in_dim(my_block, my_beam, 1, keepdims=False).reshape(
                row_count, head_width
            )
        )
    return (jnp.stack(contexts), cache_stack[0], cache_stack[1])


def solution(mesh):
    return jax.shard_map(
        shards,
        mesh=mesh,
        in_specs=(
            P(None, "hyp", None),
            P(),
            P(),
            P(),
            P(None, "head"),
            P(None, "head"),
            P(None, "head"),
            P("head", None),
            P(),
            P(None, "head"),
            P("hyp", "head"),
            P("hyp", "head"),
            P("hyp"),
            P("hyp", None, "head"),
            P("hyp", None, "head"),
            P(),
        ),
        out_specs=(P(None, "hyp", "head"), P("hyp", None, "head"), P("hyp", None, "head")),
        check_vma=False,
    )
```

profile of v0, /device:TPU:1, one launch (start us, length us, event | category | flops | bytes accessed | tf_op | source)
XLA Modules:
  0.0 360.1 jit_solution(13073119696567710992)
XLA Ops:
  8.1 1.5 copy_bitcast_fusion
  10.4 3.6 collective-permute-start
  15.9 2.7 fusion.11
  20.4 1.0 fusion.5
  21.4 1.0 fusion.4
  22.4 2.8 fusion.9
  25.2 1.0 fusion.3
  27.1 8.9 %collective-permute-done = bf16[2,16,32,256]{3,1,2,0:T(8,128)(2,1)} collective-permute-done((bf16[2,16,32,256]{3,1,2,0:T(8,128)(2,1)}, bf16[2,16,32,256]{3,1,2,0:T(8,128)(2,1)}, u32[]{:S(2)}, u32[]{:S(2)}) %collective-permute-start) | collective-permute-done | bytes 524320 | tf_op jit(solution)/shard_map/ppermute | solution.py:18
  36.0 4.9 %collective-permute-done.2 = bf16[2,16,32,256]{3,1,2,0:T(8,128)(2,1)} collective-permute-done((bf16[2,16,32,256]{3,1,2,0:T(8,128)(2,1)}, bf16[2,16,32,256]{3,1,2,0:T(8,128)(2,1)}, u32[]{:S(2)}, u32[]{:S(2)}) %collective-permute-start.2) | collective-permute-done | bytes 524320 | tf_op jit(solution)/shard_map/ppermute | solution.py:18
  40.9 1.5 select_select_fusion.2
  43.0 1.0 collective-permute-start.5
  44.8 1.1 convolution_convert_fusion.2
  45.9 10.0 %collective-permute-done.3 = bf16[2,16,33,256]{3,1,2,0:T(8,128)(2,1)S(1)} collective-permute-done((bf16[2,16,33,256]{3,1,2,0:T(8,128)(2,1)S(1)}, bf16[2,16,33,256]{3,1,2,0:T(8,128)(2,1)S(1)}, u32[]{:S(2)}, u32[]{:S(2)}) %collective-permute-start.3) | collective-permute-done | bytes 540704 | tf_op jit(solution)/shard_map/ppermute | solution.py:18
  55.9 1.1 collective-permute-done.4
  57.0 12.9 %collective-permute-done.5 = bf16[2,16,33,256]{3,1,2,0:T(8,128)(2,1)S(1)} collective-permute-done((bf16[2,16,33,256]{3,1,2,0:T(8,128)(2,1)S(1)}, bf16[2,16,33,256]{3,1,2,0:T(8,128)(2,1)S(1)}, u32[]{:S(2)}, u32[]{:S(2)}) %collective-permute-start.5) | collective-permute-done | bytes 540704 | tf_op jit(solution)/shard_map/ppermute | solution.py:18
  70.7 1.0 collective-permute-start.8
  72.5 1.1 convolution_convert_fusion.1
  73.6 10.3 %collective-permute-done.6 = bf16[2,16,34,256]{3,1,2,0:T(8,128)(2,1)S(1)} collective-permute-done((bf16[2,16,34,256]{3,1,2,0:T(8,128)(2,1)S(1)}, bf16[2,16,34,256]{3,1,2,0:T(8,128)(2,1)S(1)}, u32[]{:S(2)}, u32[]{:S(2)}) %collective-permute-start.6) | collective-permute-done | bytes 557088 | tf_op jit(solution)/shard_map/ppermute | solution.py:18
  84.6 13.7 %collective-permute-done.8 = bf16[2,16,34,256]{3,1,2,0:T(8,128)(2,1)S(1)} collective-permute-done((bf16[2,16,34,256]{3,1,2,0:T(8,128)(2,1)S(1)}, bf16[2,16,34,256]{3,1,2,0:T(8,128)(2,1)S(1)}, u32[]{:S(2)}, u32[]{:S(2)}) %collective-permute-start.8) | collective-permute-done | bytes 557088 | tf_op jit(solution)/shard_map/ppermute | solution.py:18
  99.5 1.1 convolution_convert_fusion
  103.0 72.8 %all-reduce.3.cloned.1.call-done = (bf16[16,4096]{1,0:T(8,128)(2,1)}, bf16[16,4096]{1,0:T(8,128)(2,1)}, bf16[16,4096]{1,0:T(8,128)(2,1)}) async-done(((bf16[16,4096]{1,0:T(8,128)(2,1)}, bf16[16,4096]{1,0:T(8,128)(2,1)}, bf16[16,4096]{1,0:T(8,128)(2,1)}), (bf16[16,4096]{1,0:T(8,128)(2,1)}, bf16[16,4096]{1,0:T(8,128)(2,1)}, bf16[16,4096]{1,0:T(8,128)(2,1)})) %all-reduce.3.cloned.1.call-update) | async-done | bytes 393232 | tf_op jit(solution)/shard_map/psum | solution.py:153
  175.8 1.8 multiply_reduce_fusion.4
  177.6 2.1 convolution_convert_fusion.4
  179.7 37.9 %all_gather.30 = bf16[512,256]{1,0:T(8,128)(2,1)S(1)} all-gather(bf16[16,256]{1,0:T(8,128)(2,1)S(1)} %convolution_convert_fusion.4), channel_id=1, replica_groups=mesh['hyp'=32,'head'=8] {'hyp'}, dimensions={0}, use_global_device_ids=true | all-gather | bytes 270336 | tf_op jit(solution)/shard_map/all_gather | solution.py:160
  218.9 2.0 convolution_convert_fusion.8
  220.9 24.2 %all_gather.28 = bf16[512,256]{1,0:T(8,128)(2,1)S(1)} all-gather(bf16[16,256]{1,0:T(8,128)(2,1)S(1)} %convolution_convert_fusion.8), channel_id=1, replica_groups=mesh['hyp'=32,'head'=8] {'hyp'}, dimensions={0}, use_global_device_ids=true | all-gather | bytes 270336 | tf_op jit(solution)/shard_map/all_gather | solution.py:160
  245.8 2.0 convolution_convert_fusion.12
  247.8 22.6 %all_gather.26 = bf16[512,256]{1,0:T(8,128)(2,1)S(1)} all-gather(bf16[16,256]{1,0:T(8,128)(2,1)S(1)} %convolution_convert_fusion.12), channel_id=1, replica_groups=mesh['hyp'=32,'head'=8] {'hyp'}, dimensions={0}, use_global_device_ids=true | all-gather | bytes 270336 | tf_op jit(solution)/shard_map/all_gather | solution.py:160
  270.7 7.5 %convolution_convert_fusion.3 = bf16[768,512]{0,1:T(8,128)(2,1)S(1)} fusion(bf16[768,4096]{1,0:T(8,128)(2,1)} %all-gather.6.cloned.1.call-done, bf16[4096,512]{1,0:T(8,128)(2,1)} %all-gather.8.cloned.1.call-done), kind=kOutput, calls=%fused_computation.3 | convolution fusion | flops 3221618688 | bytes 11272192 | tf_op jit(solution)/shard_map/dot_general | solution.py:113
  278.9 24.5 %all-gather.2 = bf16[512,1,256]{2,0,1:T(8,128)(2,1)S(1)} all-gather(bf16[16,1,256]{2,0,1:T(8,128)(2,1)S(1)} %fusion.14), channel_id=4, replica_groups=mesh['hyp'=32,'head'=8] {'hyp'}, dimensions={0}, use_global_device_ids=true | all-gather | bytes 270336 | tf_op jit(solution)/shard_map/all_gather | solution.py:170
  304.2 22.7 %all-gather.1 = bf16[512,1,256]{2,0,1:T(8,128)(2,1)S(1)} all-gather(bf16[16,1,256]{2,0,1:T(8,128)(2,1)S(1)} %fusion.13), channel_id=3, replica_groups=mesh['hyp'=32,'head'=8] {'hyp'}, dimensions={0}, use_global_device_ids=true | all-gather | bytes 270336 | tf_op jit(solution)/shard_map/all_gather | solution.py:170
  327.7 24.3 %all-gather = bf16[512,1,256]{2,0,1:T(8,128)(2,1)S(1)} all-gather(bf16[16,1,256]{2,0,1:T(8,128)(2,1)S(1)} %fusion.12), channel_id=2, replica_groups=mesh['hyp'=32,'head'=8] {'hyp'}, dimensions={0}, use_global_device_ids=true | all-gather | bytes 270336 | tf_op jit(solution)/shard_map/all_gather | solution.py:170
  (137 shorter events, 16.9 us)
Async XLA Ops:
  8.0 36.8 %copy-start = (bf16[256,4096]{1,0:T(8,128)(2,1)S(1)}, bf16[256,4096]{1,0:T(8,128)(2,1)}, u32[]{:S(2)}) copy-start(bf16[256,4096]{1,0:T(8,128)(2,1)} %param.23) | copy-start | bytes 6291460
  8.0 7.0 %copy-start.22 = (s32[32,4]{0,1:T(4,128)S(1)}, s32[32,4]{0,1:T(4,128)}, u32[]{:S(2)}) copy-start(s32[32,4]{0,1:T(4,128)} %param.18) | copy-start | bytes 1540
  8.0 7.2 %copy-start.4 = (bf16[3,16,4096]{2,1,0:T(8,128)(2,1)S(1)}, bf16[3,16,4096]{2,1,0:T(8,128)(2,1)}, u32[]{:S(2)}) copy-start(bf16[3,16,4096]{2,1,0:T(8,128)(2,1)} %param.16) | copy-start | bytes 1179652
  8.0 7.2 %copy-start.24 = (bf16[8,4096]{1,0:T(8,128)(2,1)S(1)}, bf16[8,4096]{1,0:T(8,128)(2,1)}, u32[]{:S(2)}) copy-start(bf16[8,4096]{1,0:T(8,128)(2,1)} %param.17) | copy-start | bytes 196612
  8.0 7.7 %copy-start.17 = (f32[4096]{0:T(1024)S(1)}, f32[4096]{0:T(1024)}, u32[]{:S(2)}) copy-start(f32[4096]{0:T(1024)} %param.19) | copy-start | bytes 49156
  8.1 167.7 %all-reduce.3.cloned.1.call-start = ((), (), s32[]{:S(2)}) async-start(), calls=%async_computation.2 | async-start | bytes 786432 | tf_op jit(solution)/shard_map/psum | solution.py:153
  10.4 25.6 %collective-permute-start = (bf16[2,16,32,256]{3,1,2,0:T(8,128)(2,1)}, bf16[2,16,32,256]{3,1,2,0:T(8,128)(2,1)}, u32[]{:S(2)}, u32[]{:S(2)}) collective-permute-start(bf16[2,16,32,256]{3,1,2,0:T(8,128)(2,1)} %pad_maximum_fusion.2), channel_id=1, source_target_pairs={{64,0},{72,8},{80,16},{88,24},{96,32},{104,40},{112,48},{120,56},{... | collective-permute-start | bytes 1572872 | tf_op jit(solution)/shard_map/ppermute | solution.py:18
  14.0 22.0 %collective-permute-start.1 = (bf16[2,16,32,256]{3,1,2,0:T(8,128)(2,1)}, bf16[2,16,32,256]{3,1,2,0:T(8,128)(2,1)}, u32[]{:S(2)}, u32[]{:S(2)}) collective-permute-start(bf16[2,16,32,256]{3,1,2,0:T(8,128)(2,1)} %pad_maximum_fusion.2), channel_id=1, source_target_pairs={{128,0},{136,8},{144,16},{152,24},{160,32},{168,40},{176,48},{184,... | collective-permute-start | bytes 1572872 | tf_op jit(solution)/shard_map/ppermute | solution.py:18
  14.3 26.6 %collective-permute-start.2 = (bf16[2,16,32,256]{3,1,2,0:T(8,128)(2,1)}, bf16[2,16,32,256]{3,1,2,0:T(8,128)(2,1)}, u32[]{:S(2)}, u32[]{:S(2)}) collective-permute-start(bf16[2,16,32,256]{3,1,2,0:T(8,128)(2,1)} %pad_maximum_fusion.2), channel_id=1, source_target_pairs={{192,0},{200,8},{208,16},{216,24},{224,32},{232,40},{240,48},{248,... | collective-permute-start | bytes 1572872 | tf_op jit(solution)/shard_map/ppermute | solution.py:18
  15.3 3.4 copy-start.2
  15.9 3.7 %copy-start.5 = (bf16[16,4096]{1,0:T(8,128)(2,1)}, bf16[16,4096]{1,0:T(8,128)(2,1)S(1)}, u32[]{:S(2)}) copy-start(bf16[16,4096]{1,0:T(8,128)(2,1)S(1)} %get-tuple-element.24) | copy-start | bytes 393220
  15.9 3.7 %copy-start.1 = (bf16[4096,256]{1,0:T(8,128)(2,1)S(1)}, bf16[4096,256]{1,0:T(8,128)(2,1)}, u32[]{:S(2)}) copy-start(bf16[4096,256]{1,0:T(8,128)(2,1)} %param.22) | copy-start | bytes 6291460
  22.4 2.8 copy-start.3
  26.2 0.9 copy-start.14
  40.9 3.2 copy-start.20
  42.5 13.4 %collective-permute-start.3 = (bf16[2,16,33,256]{3,1,2,0:T(8,128)(2,1)S(1)}, bf16[2,16,33,256]{3,1,2,0:T(8,128)(2,1)S(1)}, u32[]{:S(2)}, u32[]{:S(2)}) collective-permute-start(bf16[2,16,33,256]{3,1,2,0:T(8,128)(2,1)S(1)} %pad_maximum_fusion.1), channel_id=1, source_target_pairs={{64,0},{72,8},{80,16},{88,24},{96,32},{104,40},{112,48},{120,56},{... | collective-permute-start | bytes 1622024 | tf_op jit(solution)/shard_map/ppermute | solution.py:18
  42.6 14.5 %collective-permute-start.4 = (bf16[2,16,33,256]{3,1,2,0:T(8,128)(2,1)S(1)}, bf16[2,16,33,256]{3,1,2,0:T(8,128)(2,1)S(1)}, u32[]{:S(2)}, u32[]{:S(2)}) collective-permute-start(bf16[2,16,33,256]{3,1,2,0:T(8,128)(2,1)S(1)} %pad_maximum_fusion.1), channel_id=1, source_target_pairs={{128,0},{136,8},{144,16},{152,24},{160,32},{168,40},{176,48},{184,... | collective-permute-start | bytes 1622024 | tf_op jit(solution)/shard_map/ppermute | solution.py:18
  43.0 26.9 %collective-permute-start.5 = (bf16[2,16,33,256]{3,1,2,0:T(8,128)(2,1)S(1)}, bf16[2,16,33,256]{3,1,2,0:T(8,128)(2,1)S(1)}, u32[]{:S(2)}, u32[]{:S(2)}) collective-permute-start(bf16[2,16,33,256]{3,1,2,0:T(8,128)(2,1)S(1)} %pad_maximum_fusion.1), channel_id=1, source_target_pairs={{192,0},{200,8},{208,16},{216,24},{224,32},{232,40},{240,48},{248,... | collective-permute-start | bytes 1622024 | tf_op jit(solution)/shard_map/ppermute | solution.py:18
  70.2 13.8 %collective-permute-start.6 = (bf16[2,16,34,256]{3,1,2,0:T(8,128)(2,1)S(1)}, bf16[2,16,34,256]{3,1,2,0:T(8,128)(2,1)S(1)}, u32[]{:S(2)}, u32[]{:S(2)}) collective-permute-start(bf16[2,16,34,256]{3,1,2,0:T(8,128)(2,1)S(1)} %pad_maximum_fusion), channel_id=1, source_target_pairs={{64,0},{72,8},{80,16},{88,24},{96,32},{104,40},{112,48},{120,56},{... | collective-permute-start | bytes 1671176 | tf_op jit(solution)/shard_map/ppermute | solution.py:18
  70.2 14.4 %collective-permute-start.7 = (bf16[2,16,34,256]{3,1,2,0:T(8,128)(2,1)S(1)}, bf16[2,16,34,256]{3,1,2,0:T(8,128)(2,1)S(1)}, u32[]{:S(2)}, u32[]{:S(2)}) collective-permute-start(bf16[2,16,34,256]{3,1,2,0:T(8,128)(2,1)S(1)} %pad_maximum_fusion), channel_id=1, source_target_pairs={{128,0},{136,8},{144,16},{152,24},{160,32},{168,40},{176,48},{184,... | collective-permute-start | bytes 1671176 | tf_op jit(solution)/shard_map/ppermute | solution.py:18
  70.7 27.6 %collective-permute-start.8 = (bf16[2,16,34,256]{3,1,2,0:T(8,128)(2,1)S(1)}, bf16[2,16,34,256]{3,1,2,0:T(8,128)(2,1)S(1)}, u32[]{:S(2)}, u32[]{:S(2)}) collective-permute-start(bf16[2,16,34,256]{3,1,2,0:T(8,128)(2,1)S(1)} %pad_maximum_fusion), channel_id=1, source_target_pairs={{192,0},{200,8},{208,16},{216,24},{224,32},{232,40},{240,48},{248,... | collective-permute-start | bytes 1671176 | tf_op jit(solution)/shard_map/ppermute | solution.py:18
  73.6 25.0 %copy-start.19 = (bf16[16,256,1]{1,0,2:T(8,128)(2,1)S(1)}, bf16[16,256,1]{1,0,2:T(8,128)(2,1)}, u32[]{:S(2)}) copy-start(bf16[16,256,1]{1,0,2:T(8,128)(2,1)} %fusion.9) | copy-start | bytes 24580
  98.6 0.9 copy-start.9
  99.5 78.1 %copy-start.10 = (f32[4096]{0:T(1024)S(1)}, f32[4096]{0:T(1024)}, u32[]{:S(2)}) copy-start(f32[4096]{0:T(1024)} %param.24) | copy-start | bytes 49156
  100.6 170.0 %all-gather.8.cloned.1.call-start = ((), (), s32[]{:S(2)}) async-start(), calls=%async_computation.1 | async-start | bytes 4325376 | tf_op jit(solution)/shard_map/all_gather | solution.py:112
  101.2 169.5 %all-gather.6.cloned.1.call-start = ((), (), s32[]{:S(2)}) async-start(), calls=%async_computation | async-start | bytes 7077888 | tf_op jit(solution)/shard_map/all_gather | solution.py:114
  175.8 43.1 %copy-start.8 = (bf16[16,4096]{1,0:T(8,128)(2,1)S(1)}, bf16[16,4096]{1,0:T(8,128)(2,1)}, u32[]{:S(2)}) copy-start(bf16[16,4096]{1,0:T(8,128)(2,1)} %get-tuple-element.11) | copy-start | bytes 393220
  179.7 66.1 %copy-start.7 = (bf16[16,4096]{1,0:T(8,128)(2,1)S(1)}, bf16[16,4096]{1,0:T(8,128)(2,1)}, u32[]{:S(2)}) copy-start(bf16[16,4096]{1,0:T(8,128)(2,1)} %get-tuple-element.10) | copy-start | bytes 393220
  217.7 28.1 %copy-start.23 = (f32[16]{0:T(128)S(1)}, f32[16]{0:T(128)}, u32[]{:S(2)}) copy-start(f32[16]{0:T(128)} %get-tuple-element.3) | copy-start | bytes 196
  270.6 7.6 %copy-start.12 = (bf16[16,256]{1,0:T(8,128)(2,1)S(1)}, bf16[16,256]{1,0:T(8,128)(2,1)}, u32[]{:S(2)}) copy-start(bf16[16,256]{1,0:T(8,128)(2,1)} %reshape.403) | copy-start | bytes 24580
  270.6 7.6 %copy-start.18 = (pred[768]{0:T(1024)(128)(4,1)S(1)}, pred[768]{0:T(1024)(128)(4,1)}, u32[]{:S(2)}) copy-start(pred[768]{0:T(1024)(128)(4,1)} %iota_compare_fusion.2) | copy-start | bytes 2308
  270.6 32.9 %copy-start.11 = (bf16[16,256]{1,0:T(8,128)(2,1)S(1)}, bf16[16,256]{1,0:T(8,128)(2,1)}, u32[]{:S(2)}) copy-start(bf16[16,256]{1,0:T(8,128)(2,1)} %reshape.398) | copy-start | bytes 24580
  (5 other events, 3.9 us)
Sparse Core Ops, SparseCore 0:
  100.7 74.9 all-reduce.2
Sparse Core Ops, SparseCore 1:
  103.7 52.1 all-gather.7
  157.5 73.3 all-gather.5
where the time goes:
time: 360 us
  blocking collectives  156 us (43%)
  waiting for transfers between devices  136 us (38%)
  matrix products  30.7 us (9%)
  between operations  16.7 us (5%)
  other arithmetic  8.37 us (2%)
  starting transfers between devices  7.79 us (2%)
  local copies, waits for them, and re-layouts  4.05 us (1%)
    all_gather x3, blocking collectives, shards(): every_query = lax.all_gather(cross_query, 'hyp', axis=0, tiled=True)  84.7 us
    psum x1, waiting for transfers between devices, shards(): lax.psum(partial_out.astype(jnp.bfloat16), 'head').astype(jnp.float32)  72.8 us
    all_gather x3, blocking collectives, shards(): every_answer = lax.all_gather(answer, 'hyp', axis=0, tiled=True)  71.4 us
    ppermute x9, waiting for transfers between devices, shifted(): return lax.ppermute(block, axis, route)  62.5 us
    ppermute x9, starting transfers between devices, shifted(): return lax.ppermute(block, axis, route)  7.67 us
    dot_general x1, matrix products, shards(): jnp.dot(lax.all_gather(encoder_rows, 'head', axis=1, tiled=True), full_we...  7.47 us
  transfers between devices with their start and end apart: 12, of which 9 were waited for; matrix products, arithmetic and copies ran while one was open for 7% of the time, Pallas kernels for 0%

commit v1 on v0

v1 whole, which is shorter than its diff:
```python
import jax
import jax.numpy as jnp
from jax import lax
from jax.sharding import PartitionSpec as P

HEAD = 256
BEAMS = 4
TARGETS = 4
STEPS = 3


EPSILON = 1e-06


def rms_scaled(values_in, gain):
    mean_square = jnp.mean(values_in * values_in, axis=-1, keepdims=True)
    return values_in * lax.rsqrt(mean_square + EPSILON) * gain


def pick_rows(candidates, selector, row_axis):
    shape_list = [1] * candidates[0].ndim
    shape_list[row_axis] = selector.shape[0]
    chosen = candidates[0]
    for position in range(1, len(candidates)):
        chosen = jnp.where((selector == position).reshape(shape_list), candidates[position], chosen)
    return chosen


def beam_copies(block, hyp_count, group_size):
    copies = [block]
    for hop in range(1, BEAMS):
        distance = hop * group_size
        route = [((i - distance) % hyp_count, i) for i in range(hyp_count)]
        copies.append(lax.ppermute(block, "hyp", route))
    return copies


def cross_attend(queries, cross_keys, cross_values, doc_length, scaling):
    scores = (
        jnp.einsum("qd,jd->qj", queries, cross_keys, preferred_element_type=jnp.float32) * scaling
    )
    live_mask = lax.broadcasted_iota(jnp.int32, (1, cross_keys.shape[0]), 1) < doc_length
    scores = jnp.where(live_mask, scores, -jnp.inf)
    highest = jnp.max(scores, axis=1, keepdims=True)
    raw_weights = jnp.exp(scores - highest)
    totals = jnp.sum(raw_weights, axis=1, keepdims=True)
    weights = (raw_weights / totals).astype(jnp.bfloat16)
    output = jnp.einsum("qj,jd->qd", weights, cross_values, preferred_element_type=jnp.float32)
    return output.astype(jnp.bfloat16)


def shards(
    step_embeds,
    lang_table,
    lang_ids,
    self_gain,
    self_wq,
    self_wk,
    self_wv,
    self_wo,
    cross_gain,
    cross_wq,
    cross_wkv,
    encoder_rows,
    doc_lengths,
    past_keys,
    past_values,
    parents,
):
    hyp_count = lax.axis_size("hyp")
    group_size = hyp_count // BEAMS
    my_index = lax.axis_index("hyp")
    my_beam = my_index // group_size
    my_slot = my_index % group_size
    steps = step_embeds.shape[0]
    row_count = step_embeds.shape[1]
    docs_here = row_count // TARGETS
    head_width = self_wq.shape[1]
    doc_count = lang_ids.shape[0]
    past_len = past_keys.shape[1]
    scaling = HEAD ** (-0.5)

    full_weights = lax.all_gather(cross_wkv, "hyp", axis=0, tiled=True)
    full_rows = lax.all_gather(encoder_rows, "head", axis=1, tiled=True)
    cross_kv = jnp.dot(full_rows, full_weights, preferred_element_type=jnp.float32).astype(
        jnp.bfloat16
    )
    cross_kv = cross_kv.reshape(encoder_rows.shape[0], 2, HEAD)
    cross_keys = cross_kv[:, 0, :]
    cross_values = cross_kv[:, 1, :]
    doc_length = doc_lengths[0]

    past_stack = jnp.stack([past_keys, past_values])
    past_all = beam_copies(past_stack, hyp_count, group_size)

    my_langs = lax.dynamic_slice_in_dim(lang_ids, my_slot * docs_here, docs_here, 0).reshape(row_count)
    one_hot = (
        my_langs[:, None] == lax.broadcasted_iota(jnp.int32, (1, lang_table.shape[0]), 1)
    ).astype(jnp.bfloat16)
    lang_rows = jnp.dot(one_hot, lang_table, preferred_element_type=jnp.float32)

    hidden_in = step_embeds.astype(jnp.float32) + lang_rows[None]
    normed = rms_scaled(hidden_in, self_gain).astype(jnp.bfloat16).reshape(steps * row_count, -1)
    new_query = jnp.dot(normed, self_wq, preferred_element_type=jnp.float32).astype(jnp.bfloat16)
    new_key = jnp.dot(normed, self_wk, preferred_element_type=jnp.float32).astype(jnp.bfloat16)
    new_value = jnp.dot(normed, self_wv, preferred_element_type=jnp.float32).astype(jnp.bfloat16)
    new_query = new_query.reshape(steps, row_count, head_width)
    fresh = jnp.stack([new_key, new_value]).reshape(2, steps, row_count, head_width)
    fresh_all = beam_copies(fresh, hyp_count, group_size)

    parent_view = parents.reshape(steps, BEAMS, doc_count * TARGETS)
    parent_of = lax.dynamic_slice_in_dim(parent_view, my_slot * row_count, row_count, 2)
    own_beam = jnp.full((row_count,), my_beam, jnp.int32)

    def hop_of(beam):
        return (my_beam - beam) % BEAMS

    def climb(step_idx, beam):
        return jnp.take_along_axis(parent_of[step_idx], beam[None, :], axis=0)[0]

    def cache_at(step_idx):
        ancestor = own_beam
        new_parts = [None] * (step_idx + 1)
        new_parts[step_idx] = fresh[:, step_idx]
        for back in range(step_idx, 0, -1):
            ancestor = climb(back, ancestor)
            new_parts[back - 1] = pick_rows(
                [f[:, back - 1] for f in fresh_all], hop_of(ancestor), 1
            )
        ancestor = climb(0, ancestor)
        past_part = pick_rows(past_all, hop_of(ancestor), 1)
        return jnp.concatenate([past_part] + [n[:, :, None, :] for n in new_parts], axis=2)

    contexts = []
    final_cache = None
    for step_idx in range(steps):
        cache = cache_at(step_idx)
        if step_idx == steps - 1:
            final_cache = cache
        query = new_query[step_idx]
        scores = (
            jnp.einsum("rd,rpd->rp", query, cache[0], preferred_element_type=jnp.float32) * scaling
        )
        highest = jnp.max(scores, axis=1, keepdims=True)
        raw_weights = jnp.exp(scores - highest)
        totals = jnp.sum(raw_weights, axis=1, keepdims=True)
        summed = jnp.einsum(
            "rp,rpd->rd", raw_weights, cache[1].astype(jnp.float32), preferred_element_type=jnp.float32
        )
        contexts.append((summed / totals).astype(jnp.bfloat16))
    self_context = jnp.stack(contexts).reshape(steps * row_count, head_width)
    partial_out = jnp.dot(self_context, self_wo, preferred_element_type=jnp.float32)
    summed_out = lax.psum(partial_out.astype(jnp.bfloat16), "head").astype(jnp.float32)
    residual = hidden_in + summed_out.reshape(hidden_in.shape)
    normed_cross = rms_scaled(residual, cross_gain).astype(jnp.bfloat16)
    cross_query = jnp.dot(
        normed_cross.reshape(steps * row_count, -1), cross_wq, preferred_element_type=jnp.float32
    ).astype(jnp.bfloat16)
    by_doc = cross_query.reshape(steps, docs_here, TARGETS, head_width)

    sent = []
    for shift in range(BEAMS):
        route = [
            (beam * group_size + slot, slot * docs_here + (beam + shift) % BEAMS)
            for beam in range(BEAMS)
            for slot in range(group_size)
        ]
        piece = lax.dynamic_index_in_dim(by_doc, (my_beam + shift) % BEAMS, 1, keepdims=False)
        sent.append(lax.ppermute(piece, "hyp", route))
    doc_queries = jnp.stack(sent).reshape(BEAMS * steps * TARGETS, head_width)
    answer = cross_attend(doc_queries, cross_keys, cross_values, doc_length, scaling)
    answer = answer.reshape(BEAMS, steps, TARGETS, head_width)

    back = []
    for shift in range(BEAMS):
        route = [
            (slot * docs_here + (beam + shift) % BEAMS, beam * group_size + slot)
            for beam in range(BEAMS)
            for slot in range(group_size)
        ]
        back.append(lax.ppermute(answer[shift], "hyp", route))
    back = jnp.stack(back)
    order = (jnp.arange(docs_here, dtype=jnp.int32) - my_beam) % BEAMS
    by_k = jnp.take(back, order, axis=0)
    contexts_out = by_k.transpose(1, 0, 2, 3).reshape(steps, row_count, head_width)
    return (contexts_out, final_cache[0], final_cache[1])


def solution(mesh):
    return jax.shard_map(
        shards,
        mesh=mesh,
        in_specs=(
            P(None, "hyp", None),
            P(),
            P(),
            P(),
            P(None, "head"),
            P(None, "head"),
            P(None, "head"),
            P("head", None),
            P(),
            P(None, "head"),
            P("hyp", "head"),
            P("hyp", "head"),
            P("hyp"),
            P("hyp", None, "head"),
            P("hyp", None, "head"),
            P(),
        ),
        out_specs=(P(None, "hyp", "head"), P("hyp", None, "head"), P("hyp", None, "head")),
        check_vma=False,
    )
```

time: 360 us -> 225 us (0.62)
  blocking collectives: 156 us -> 0 us
  starting transfers between devices: 7.79 us -> 50.4 us
  waiting for transfers between devices: 136 us -> 116 us
  matrix products: 30.7 us -> 16.7 us
  other arithmetic: 8.37 us -> 13.6 us
  local copies, waits for them, and re-layouts: 4.05 us -> 8.23 us
    all_gather x6 -> x0, blocking collectives: 156 us -> none  [the longest x3 84.7 us: shards(): every_query = lax.all_gather(cross_query, 'hyp', axis=0, tiled=True)]
    ppermute x9 -> x14, waiting for transfers between devices: 62.5 us -> 16.1 us  [the longest x6 12.6 us: beam_copies(): copies.append(lax.ppermute(block, 'hyp', route))]
    ppermute x9 -> x14, starting transfers between devices: 7.67 us -> 50.3 us  [the longest x4 27.4 us: shards(): sent.append(lax.ppermute(piece, 'hyp', route))]
    all_gather x1, waiting for transfers between devices: 0.02 us -> 23.4 us  [shards(): full_rows = lax.all_gather(encoder_rows, 'head', axis=1, tiled=True)]
    dot_general x16 -> x10, matrix products: 16.4 us -> 9.77 us  [the longest x1 7.47 us: shards(): jnp.dot(full_rows, full_weights, preferred_element_type=jnp.float32)]
    gather x0 -> x8, local copies, waits for them, and re-layouts: none -> 5.28 us  [the longest x7 4.69 us: climb(): return jnp.take_along_axis(parent_of[step_idx], beam[None, :], axis=0)[0]]
  transfers between devices with their start and end apart: 12 -> 17, of which waited for: 9 -> 6; matrix products, arithmetic and copies ran while one was open for 7% -> 7% of each run, Pallas kernels for 0% -> 0%
where the time goes in v1:
time: 225 us; the launch traced here: 222 us
  waiting for transfers between devices  116 us (52%)
  starting transfers between devices  50.4 us (22%)
  between operations  16.9 us (8%)
  matrix products  16.7 us (7%)
  other arithmetic  13.6 us (6%)
  local copies, waits for them, and re-layouts  8.23 us (4%)
    psum x1, waiting for transfers between devices, shards(): lax.psum(partial_out.astype(jnp.bfloat16), 'head').astype(jnp.float32)  75.1 us
    ppermute x4, starting transfers between devices, shards(): sent.append(lax.ppermute(piece, 'hyp', route))  27.4 us
    all_gather x1, waiting for transfers between devices, shards(): full_rows = lax.all_gather(encoder_rows, 'head', axis=1, tiled=True)  23.4 us
    ppermute x4, starting transfers between devices, shards(): back.append(lax.ppermute(answer[shift], 'hyp', route))  14.8 us
    ppermute x6, waiting for transfers between devices, beam_copies(): copies.append(lax.ppermute(block, 'hyp', route))  12.6 us
    ppermute x6, starting transfers between devices, beam_copies(): copies.append(lax.ppermute(block, 'hyp', route))  8.15 us
    dot_general x1, matrix products, shards(): jnp.dot(full_rows, full_weights, preferred_element_type=jnp.float32)  7.47 us
    gather x7, local copies, waits for them, and re-layouts, climb(): return jnp.take_along_axis(parent_of[step_idx], beam[None, :], axis=0)[0]  4.69 us
  transfers between devices with their start and end apart: 17, of which 6 were waited for; matrix products, arithmetic and copies ran while one was open for 7% of the time, Pallas kernels for 0%

profile of v1, /device:TPU:1, one launch (start us, length us, event | category | flops | bytes accessed | tf_op | source)
XLA Modules:
  0.0 221.6 jit_solution(5241141596806689058)
XLA Ops:
  8.1 0.9 constant_dynamic-slice_fusion
  9.2 1.1 fusion.42
  10.2 1.3 multiply_reduce_fusion.1
  11.6 1.2 multiply_convert_fusion.1
  12.8 2.1 convolution_convert_fusion.4
  15.4 3.6 %collective-permute-start.3 = (bf16[2,3,16,256]{3,2,0,1:T(8,128)(2,1)S(1)}, bf16[2,3,16,256]{3,2,0,1:T(8,128)(2,1)S(1)}, u32[]{:S(2)}, u32[]{:S(2)}) collective-permute-start(bf16[2,3,16,256]{3,2,0,1:T(8,128)(2,1)S(1)} %pad_maximum_fusion.4), channel_id=1, source_target_pairs={{64,0},{72,8},{80,16},{88,24},{96,32},{104,40},{112,48},{120,56},{... | collective-permute-start | bytes 147464 | tf_op jit(solution)/shard_map/ppermute | solution.py:34
  19.4 0.7 collective-permute-start.5
  20.4 0.8 pad_maximum_fusion.2
  21.2 2.0 collective-permute-start
  23.2 1.4 collective-permute-start.1
  27.3 1.2 gather_fusion.5
  30.6 1.2 broadcast_compare_fusion.16
  32.3 1.1 broadcast_compare_fusion.6
  34.2 2.1 convolution_convert_fusion.6
  36.7 12.5 %collective-permute-done.2 = bf16[2,16,32,256]{3,1,2,0:T(8,128)(2,1)S(1)} collective-permute-done((bf16[2,16,32,256]{3,1,2,0:T(8,128)(2,1)}, bf16[2,16,32,256]{3,1,2,0:T(8,128)(2,1)S(1)}, u32[]{:S(2)}, u32[]{:S(2)}) %collective-permute-start.2) | collective-permute-done | bytes 524320 | tf_op jit(solution)/shard_map/ppermute | solution.py:34
  49.2 1.5 select_select_fusion.2
  53.6 1.2 convolution_convert_fusion
  56.8 75.1 %all-reduce.2.cloned.1.call-done = bf16[3,16,4096]{2,1,0:T(8,128)(2,1)} async-done(((bf16[3,16,4096]{2,1,0:T(8,128)(2,1)}), bf16[3,16,4096]{2,1,0:T(8,128)(2,1)}) %all-reduce.2.cloned.1.call-update) | async-done | bytes 393232 | tf_op jit(solution)/shard_map/psum | solution.py:153
  131.9 1.4 multiply_reduce_fusion
  133.3 1.2 multiply_convert_fusion
  135.0 5.0 %collective-permute-start.9 = (bf16[3,4,256]{2,1,0:T(4,128)(2,1)S(1)}, bf16[3,4,256]{2,1,0:T(4,128)(2,1)S(1)}, u32[]{:S(2)}, u32[]{:S(2)}) collective-permute-start(bf16[3,4,256]{2,1,0:T(4,128)(2,1)S(1)} %get-tuple-element.43), channel_id=1, source_target_pairs={{0,24},{8,56},{16,88},{24,120},{32,152},{40,184},{48,216},{56,248}... | collective-permute-start | bytes 18440 | tf_op jit(solution)/shard_map/ppermute | solution.py:169
  140.0 12.5 %collective-permute-start.8 = (bf16[3,4,256]{2,1,0:T(4,128)(2,1)S(1)}, bf16[3,4,256]{2,1,0:T(4,128)(2,1)S(1)}, u32[]{:S(2)}, u32[]{:S(2)}) collective-permute-start(bf16[3,4,256]{2,1,0:T(4,128)(2,1)S(1)} %get-tuple-element.44), channel_id=1, source_target_pairs={{0,16},{8,48},{16,80},{24,112},{32,144},{40,176},{48,208},{56,240}... | collective-permute-start | bytes 18440 | tf_op jit(solution)/shard_map/ppermute | solution.py:169
  152.5 5.5 %collective-permute-start.7 = (bf16[3,4,256]{2,1,0:T(4,128)(2,1)S(1)}, bf16[3,4,256]{2,1,0:T(4,128)(2,1)S(1)}, u32[]{:S(2)}, u32[]{:S(2)}) collective-permute-start(bf16[3,4,256]{2,1,0:T(4,128)(2,1)S(1)} %get-tuple-element.45), channel_id=1, source_target_pairs={{0,8},{8,40},{16,72},{24,104},{32,136},{40,168},{48,200},{56,232},... | collective-permute-start | bytes 18440 | tf_op jit(solution)/shard_map/ppermute | solution.py:169
  158.1 4.4 %collective-permute-start.6 = (bf16[3,4,256]{2,1,0:T(4,128)(2,1)S(1)}, bf16[3,4,256]{2,1,0:T(4,128)(2,1)S(1)}, u32[]{:S(2)}, u32[]{:S(2)}) collective-permute-start(bf16[3,4,256]{2,1,0:T(4,128)(2,1)S(1)} %get-tuple-element.42), channel_id=1, source_target_pairs={{0,0},{8,32},{16,64},{24,96},{32,128},{40,160},{48,192},{56,224},{... | collective-permute-start | bytes 18440 | tf_op jit(solution)/shard_map/ppermute | solution.py:169
  162.5 0.9 collective-permute-done.6
  163.5 23.4 %all-gather.3.cloned.1.call-done = bf16[768,4096]{1,0:T(8,128)(2,1)} async-done(((bf16[768,512]{1,0:T(8,128)(2,1)}), bf16[768,4096]{1,0:T(8,128)(2,1)}) %all-gather.3.cloned.1.call-update) | async-done | bytes 6291472 | tf_op jit(solution)/shard_map/all_gather | solution.py:84
  186.9 7.5 %convolution_convert_fusion.1 = bf16[768,512]{0,1:T(8,128)(2,1)S(1)} fusion(bf16[768,4096]{1,0:T(8,128)(2,1)} %all-gather.3.cloned.1.call-done, bf16[4096,512]{1,0:T(8,128)(2,1)} %all-gather.5.cloned.1.call-done), kind=kOutput, calls=%fused_computation.8 | convolution fusion | flops 3221618688 | bytes 11272192 | tf_op jit(solution)/shard_map/dot_general | solution.py:85
  195.3 5.7 %collective-permute-start.13 = (bf16[3,4,256]{2,1,0:T(4,128)(2,1)S(1)}, bf16[3,4,256]{2,1,0:T(4,128)(2,1)S(1)}, u32[]{:S(2)}, u32[]{:S(2)}) collective-permute-start(bf16[3,4,256]{2,1,0:T(4,128)(2,1)S(1)} %squeeze.124), channel_id=1, source_target_pairs={{24,0},{56,8},{88,16},{120,24},{152,32},{184,40},{216,48},{248,56}... | collective-permute-start | bytes 18440 | tf_op jit(solution)/shard_map/ppermute | solution.py:181
  201.0 3.4 %collective-permute-start.12 = (bf16[3,4,256]{2,1,0:T(4,128)(2,1)S(1)}, bf16[3,4,256]{2,1,0:T(4,128)(2,1)S(1)}, u32[]{:S(2)}, u32[]{:S(2)}) collective-permute-start(bf16[3,4,256]{2,1,0:T(4,128)(2,1)S(1)} %squeeze.123), channel_id=1, source_target_pairs={{16,0},{48,8},{80,16},{112,24},{144,32},{176,40},{208,48},{240,56}... | collective-permute-start | bytes 18440 | tf_op jit(solution)/shard_map/ppermute | solution.py:181
  204.3 2.0 collective-permute-start.11
  206.3 3.7 %collective-permute-start.10 = (bf16[3,4,256]{2,1,0:T(4,128)(2,1)S(1)}, bf16[3,4,256]{2,1,0:T(4,128)(2,1)S(1)}, u32[]{:S(2)}, u32[]{:S(2)}) collective-permute-start(bf16[3,4,256]{2,1,0:T(4,128)(2,1)S(1)} %squeeze.121), channel_id=1, source_target_pairs={{0,0},{32,8},{64,16},{96,24},{128,32},{160,40},{192,48},{224,56},{... | collective-permute-start | bytes 18440 | tf_op jit(solution)/shard_map/ppermute | solution.py:181
  210.2 2.6 %collective-permute-done.10 = bf16[3,4,256]{2,1,0:T(4,128)(2,1)S(1)} collective-permute-done((bf16[3,4,256]{2,1,0:T(4,128)(2,1)S(1)}, bf16[3,4,256]{2,1,0:T(4,128)(2,1)S(1)}, u32[]{:S(2)}, u32[]{:S(2)}) %collective-permute-start.10) | collective-permute-done | bytes 6176 | tf_op jit(solution)/shard_map/ppermute | solution.py:181
  (132 shorter events, 14.5 us)
Async XLA Ops:
  8.0 45.6 %copy-start = (bf16[256,4096]{1,0:T(8,128)(2,1)S(1)}, bf16[256,4096]{1,0:T(8,128)(2,1)}, u32[]{:S(2)}) copy-start(bf16[256,4096]{1,0:T(8,128)(2,1)} %param.25) | copy-start | bytes 6291460
  8.0 123.9 %all-reduce.2.cloned.1.call-start = ((), (), s32[]{:S(2)}) async-start(), calls=%async_computation | async-start | bytes 786432 | tf_op jit(solution)/shard_map/psum | solution.py:153
  10.2 4.7 %copy-start.2 = (bf16[4096,256]{1,0:T(8,128)(2,1)S(1)}, bf16[4096,256]{1,0:T(8,128)(2,1)}, u32[]{:S(2)}) copy-start(bf16[4096,256]{1,0:T(8,128)(2,1)} %param.23) | copy-start | bytes 6291460
  12.7 7.3 %copy-start.6 = (bf16[16,32,256]{2,1,0:T(8,128)(2,1)S(1)}, bf16[16,32,256]{2,1,0:T(8,128)(2,1)}, u32[]{:S(2)}) copy-start(bf16[16,32,256]{2,1,0:T(8,128)(2,1)} %param.32) | copy-start | bytes 786436
  12.7 7.3 %copy-start.7 = (bf16[16,32,256]{2,1,0:T(8,128)(2,1)S(1)}, bf16[16,32,256]{2,1,0:T(8,128)(2,1)}, u32[]{:S(2)}) copy-start(bf16[16,32,256]{2,1,0:T(8,128)(2,1)} %param.31) | copy-start | bytes 786436
  14.9 9.7 %copy-start.9 = (s32[3,512]{1,0:T(4,128)S(1)}, s32[3,512]{1,0:T(4,128)}, u32[]{:S(2)}) copy-start(s32[3,512]{1,0:T(4,128)} %param.33) | copy-start | bytes 18436
  15.4 20.9 %collective-permute-start.3 = (bf16[2,3,16,256]{3,2,0,1:T(8,128)(2,1)S(1)}, bf16[2,3,16,256]{3,2,0,1:T(8,128)(2,1)S(1)}, u32[]{:S(2)}, u32[]{:S(2)}) collective-permute-start(bf16[2,3,16,256]{3,2,0,1:T(8,128)(2,1)S(1)} %pad_maximum_fusion.4), channel_id=1, source_target_pairs={{64,0},{72,8},{80,16},{88,24},{96,32},{104,40},{112,48},{120,56},{... | collective-permute-start | bytes 147464 | tf_op jit(solution)/shard_map/ppermute | solution.py:34
  19.0 17.4 %collective-permute-start.4 = (bf16[2,3,16,256]{3,2,0,1:T(8,128)(2,1)S(1)}, bf16[2,3,16,256]{3,2,0,1:T(8,128)(2,1)S(1)}, u32[]{:S(2)}, u32[]{:S(2)}) collective-permute-start(bf16[2,3,16,256]{3,2,0,1:T(8,128)(2,1)S(1)} %pad_maximum_fusion.4), channel_id=1, source_target_pairs={{128,0},{136,8},{144,16},{152,24},{160,32},{168,40},{176,48},{184,... | collective-permute-start | bytes 147464 | tf_op jit(solution)/shard_map/ppermute | solution.py:34
  19.4 17.1 %collective-permute-start.5 = (bf16[2,3,16,256]{3,2,0,1:T(8,128)(2,1)S(1)}, bf16[2,3,16,256]{3,2,0,1:T(8,128)(2,1)S(1)}, u32[]{:S(2)}, u32[]{:S(2)}) collective-permute-start(bf16[2,3,16,256]{3,2,0,1:T(8,128)(2,1)S(1)} %pad_maximum_fusion.4), channel_id=1, source_target_pairs={{192,0},{200,8},{208,16},{216,24},{224,32},{232,40},{240,48},{248,... | collective-permute-start | bytes 147464 | tf_op jit(solution)/shard_map/ppermute | solution.py:34
  21.2 15.5 %collective-permute-start = (bf16[2,16,32,256]{3,1,2,0:T(8,128)(2,1)}, bf16[2,16,32,256]{3,1,2,0:T(8,128)(2,1)}, u32[]{:S(2)}, u32[]{:S(2)}) collective-permute-start(bf16[2,16,32,256]{3,1,2,0:T(8,128)(2,1)} %pad_maximum_fusion.2), channel_id=1, source_target_pairs={{64,0},{72,8},{80,16},{88,24},{96,32},{104,40},{112,48},{120,56},{... | collective-permute-start | bytes 1572872 | tf_op jit(solution)/shard_map/ppermute | solution.py:34
  23.2 13.5 %collective-permute-start.1 = (bf16[2,16,32,256]{3,1,2,0:T(8,128)(2,1)}, bf16[2,16,32,256]{3,1,2,0:T(8,128)(2,1)}, u32[]{:S(2)}, u32[]{:S(2)}) collective-permute-start(bf16[2,16,32,256]{3,1,2,0:T(8,128)(2,1)} %pad_maximum_fusion.2), channel_id=1, source_target_pairs={{128,0},{136,8},{144,16},{152,24},{160,32},{168,40},{176,48},{184,... | collective-permute-start | bytes 1572872 | tf_op jit(solution)/shard_map/ppermute | solution.py:34
  34.1 2.2 copy-start.15
  34.1 2.4 %copy-start.11 = (pred[16]{0:T(512)(128)(4,1)S(1)}, pred[16]{0:T(512)(128)(4,1)}, u32[]{:S(2)}) copy-start(pred[16]{0:T(512)(128)(4,1)} %get-tuple-element.66) | copy-start | bytes 52
  34.1 2.4 %copy-start.12 = (pred[16]{0:T(512)(128)(4,1)S(1)}, pred[16]{0:T(512)(128)(4,1)}, u32[]{:S(2)}) copy-start(pred[16]{0:T(512)(128)(4,1)} %get-tuple-element.67) | copy-start | bytes 52
  34.1 2.4 %copy-start.13 = (pred[16]{0:T(512)(128)(4,1)S(1)}, pred[16]{0:T(512)(128)(4,1)}, u32[]{:S(2)}) copy-start(pred[16]{0:T(512)(128)(4,1)} %get-tuple-element.68) | copy-start | bytes 52
  34.1 2.4 %copy-start.14 = (pred[16]{0:T(512)(128)(4,1)S(1)}, pred[16]{0:T(512)(128)(4,1)}, u32[]{:S(2)}) copy-start(pred[16]{0:T(512)(128)(4,1)} %get-tuple-element.69) | copy-start | bytes 52
  36.3 12.9 %collective-permute-start.2 = (bf16[2,16,32,256]{3,1,2,0:T(8,128)(2,1)}, bf16[2,16,32,256]{3,1,2,0:T(8,128)(2,1)S(1)}, u32[]{:S(2)}, u32[]{:S(2)}) collective-permute-start(bf16[2,16,32,256]{3,1,2,0:T(8,128)(2,1)} %pad_maximum_fusion.2), channel_id=1, source_target_pairs={{192,0},{200,8},{208,16},{216,24},{224,32},{232,40},{240,48},{248,... | collective-permute-start | bytes 1572872 | tf_op jit(solution)/shard_map/ppermute | solution.py:34
  50.9 1.2 copy-start.5
  50.9 1.8 copy-start.4
  53.5 78.4 %copy-start.1 = (bf16[3,16,4096]{2,1,0:T(8,128)(2,1)S(1)}, bf16[3,16,4096]{2,1,0:T(8,128)(2,1)}, u32[]{:S(2)}) copy-start(bf16[3,16,4096]{2,1,0:T(8,128)(2,1)} %param.18) | copy-start | bytes 1179652
  53.6 79.7 %copy-start.8 = (f32[4096]{0:T(1024)S(1)}, f32[4096]{0:T(1024)}, u32[]{:S(2)}) copy-start(f32[4096]{0:T(1024)} %param.26) | copy-start | bytes 49156
  54.9 108.6 %all-gather.5.cloned.1.call-start = ((), (), s32[]{:S(2)}) async-start(), calls=%async_computation.2 | async-start | bytes 4325376 | tf_op jit(solution)/shard_map/all_gather | solution.py:83
  55.5 131.5 %all-gather.3.cloned.1.call-start = ((), (), s32[]{:S(2)}) async-start(), calls=%async_computation.1 | async-start | bytes 7077888 | tf_op jit(solution)/shard_map/all_gather | solution.py:84
  131.9 2.6 %copy-start.3 = (bf16[4096,256]{1,0:T(8,128)(2,1)S(1)}, bf16[4096,256]{1,0:T(8,128)(2,1)}, u32[]{:S(2)}) copy-start(bf16[4096,256]{1,0:T(8,128)(2,1)} %param.27) | copy-start | bytes 6291460
  135.0 27.5 %collective-permute-start.9 = (bf16[3,4,256]{2,1,0:T(4,128)(2,1)S(1)}, bf16[3,4,256]{2,1,0:T(4,128)(2,1)S(1)}, u32[]{:S(2)}, u32[]{:S(2)}) collective-permute-start(bf16[3,4,256]{2,1,0:T(4,128)(2,1)S(1)} %get-tuple-element.43), channel_id=1, source_target_pairs={{0,24},{8,56},{16,88},{24,120},{32,152},{40,184},{48,216},{56,248}... | collective-permute-start | bytes 18440 | tf_op jit(solution)/shard_map/ppermute | solution.py:169
  140.0 22.5 %collective-permute-start.8 = (bf16[3,4,256]{2,1,0:T(4,128)(2,1)S(1)}, bf16[3,4,256]{2,1,0:T(4,128)(2,1)S(1)}, u32[]{:S(2)}, u32[]{:S(2)}) collective-permute-start(bf16[3,4,256]{2,1,0:T(4,128)(2,1)S(1)} %get-tuple-element.44), channel_id=1, source_target_pairs={{0,16},{8,48},{16,80},{24,112},{32,144},{40,176},{48,208},{56,240}... | collective-permute-start | bytes 18440 | tf_op jit(solution)/shard_map/ppermute | solution.py:169
  152.5 10.0 %collective-permute-start.7 = (bf16[3,4,256]{2,1,0:T(4,128)(2,1)S(1)}, bf16[3,4,256]{2,1,0:T(4,128)(2,1)S(1)}, u32[]{:S(2)}, u32[]{:S(2)}) collective-permute-start(bf16[3,4,256]{2,1,0:T(4,128)(2,1)S(1)} %get-tuple-element.45), channel_id=1, source_target_pairs={{0,8},{8,40},{16,72},{24,104},{32,136},{40,168},{48,200},{56,232},... | collective-permute-start | bytes 18440 | tf_op jit(solution)/shard_map/ppermute | solution.py:169
  158.1 5.3 %collective-permute-start.6 = (bf16[3,4,256]{2,1,0:T(4,128)(2,1)S(1)}, bf16[3,4,256]{2,1,0:T(4,128)(2,1)S(1)}, u32[]{:S(2)}, u32[]{:S(2)}) collective-permute-start(bf16[3,4,256]{2,1,0:T(4,128)(2,1)S(1)} %get-tuple-element.42), channel_id=1, source_target_pairs={{0,0},{8,32},{16,64},{24,96},{32,128},{40,160},{48,192},{56,224},{... | collective-permute-start | bytes 18440 | tf_op jit(solution)/shard_map/ppermute | solution.py:169
  195.3 14.8 %collective-permute-start.13 = (bf16[3,4,256]{2,1,0:T(4,128)(2,1)S(1)}, bf16[3,4,256]{2,1,0:T(4,128)(2,1)S(1)}, u32[]{:S(2)}, u32[]{:S(2)}) collective-permute-start(bf16[3,4,256]{2,1,0:T(4,128)(2,1)S(1)} %squeeze.124), channel_id=1, source_target_pairs={{24,0},{56,8},{88,16},{120,24},{152,32},{184,40},{216,48},{248,56}... | collective-permute-start | bytes 18440 | tf_op jit(solution)/shard_map/ppermute | solution.py:181
  201.0 9.1 %collective-permute-start.12 = (bf16[3,4,256]{2,1,0:T(4,128)(2,1)S(1)}, bf16[3,4,256]{2,1,0:T(4,128)(2,1)S(1)}, u32[]{:S(2)}, u32[]{:S(2)}) collective-permute-start(bf16[3,4,256]{2,1,0:T(4,128)(2,1)S(1)} %squeeze.123), channel_id=1, source_target_pairs={{16,0},{48,8},{80,16},{112,24},{144,32},{176,40},{208,48},{240,56}... | collective-permute-start | bytes 18440 | tf_op jit(solution)/shard_map/ppermute | solution.py:181
  204.3 5.9 %collective-permute-start.11 = (bf16[3,4,256]{2,1,0:T(4,128)(2,1)S(1)}, bf16[3,4,256]{2,1,0:T(4,128)(2,1)S(1)}, u32[]{:S(2)}, u32[]{:S(2)}) collective-permute-start(bf16[3,4,256]{2,1,0:T(4,128)(2,1)S(1)} %squeeze.122), channel_id=1, source_target_pairs={{8,0},{40,8},{72,16},{104,24},{136,32},{168,40},{200,48},{232,56},... | collective-permute-start | bytes 18440 | tf_op jit(solution)/shard_map/ppermute | solution.py:181
  206.3 6.5 %collective-permute-start.10 = (bf16[3,4,256]{2,1,0:T(4,128)(2,1)S(1)}, bf16[3,4,256]{2,1,0:T(4,128)(2,1)S(1)}, u32[]{:S(2)}, u32[]{:S(2)}) collective-permute-start(bf16[3,4,256]{2,1,0:T(4,128)(2,1)S(1)} %squeeze.121), channel_id=1, source_target_pairs={{0,0},{32,8},{64,16},{96,24},{128,32},{160,40},{192,48},{224,56},{... | collective-permute-start | bytes 18440 | tf_op jit(solution)/shard_map/ppermute | solution.py:181
  (1 other events, 0.5 us)
Sparse Core Ops, SparseCore 0:
  55.0 76.8 all-reduce.1
Sparse Core Ops, SparseCore 1:
  57.9 54.1 all-gather.4
  113.7 73.2 all-gather.2

commit v2 on v1

--- a/solution.py
+++ b/solution.py
@@ -3,10 +3,10 @@
 from jax import lax
 from jax.sharding import PartitionSpec as P
 
+
 HEAD = 256
 BEAMS = 4
 TARGETS = 4
-STEPS = 3
 
 
 EPSILON = 1e-06
@@ -33,6 +33,31 @@
         route = [((i - distance) % hyp_count, i) for i in range(hyp_count)]
         copies.append(lax.ppermute(block, "hyp", route))
     return copies
+
+
+def ring_gather(block, axis):
+    count = lax.axis_size(axis)
+    me = lax.axis_index(axis)
+    right = [(i, (i + 1) % count) for i in range(count)]
+    left = [(i, (i - 1) % count) for i in range(count)]
+    pieces = {0: block}
+    from_left = block
+    from_right = block
+    for hop in range(1, count // 2):
+        from_left = lax.ppermute(from_left, axis, right)
+        from_right = lax.ppermute(from_right, axis, left)
+        pieces[-hop] = from_left
+        pieces[hop] = from_right
+    if count % 2 == 0 and count > 1:
+        half = block.shape[0] // 2
+        top = lax.ppermute(from_left[:half], axis, right)
+        bottom = lax.ppermute(from_right[half:], axis, left)
+        pieces[count // 2] = jnp.concatenate([top, bottom], axis=0)
+    ordered = jnp.stack([pieces[d] if d in pieces else pieces[d - count] for d in range(count // 2 - count + 1, count // 2 + 1)])
+    first = (me + count // 2 - count + 1) % count
+    order = (jnp.arange(count, dtype=jnp.int32) - first) % count
+    by_device = jnp.take(ordered, order, axis=0)
+    return by_device.transpose(1, 0, 2).reshape(block.shape[0], count * block.shape[1])
 
 
 def cross_attend(queries, cross_keys, cross_values, doc_length, scaling):
@@ -77,11 +102,10 @@
     docs_here = row_count // TARGETS
     head_width = self_wq.shape[1]
     doc_count = lang_ids.shape[0]
-    past_len = past_keys.shape[1]
     scaling = HEAD ** (-0.5)
 
     full_weights = lax.all_gather(cross_wkv, "hyp", axis=0, tiled=True)
-    full_rows = lax.all_gather(encoder_rows, "head", axis=1, tiled=True)
+    full_rows = ring_gather(encoder_rows, "head")
     cross_kv = jnp.dot(full_rows, full_weights, preferred_element_type=jnp.float32).astype(
         jnp.bfloat16
     )

time: 225 us -> 237 us (1.053)
  waiting for transfers between devices: 116 us -> 77.1 us
  local copies, waits for them, and re-layouts: 8.23 us -> 37 us
  other arithmetic: 13.6 us -> 25.9 us
  starting transfers between devices: 50.4 us -> 58.4 us
  matrix products: 16.7 us -> 19.9 us
    psum x1, waiting for transfers between devices: 75.1 us -> 45.9 us  [shards(): lax.psum(partial_out.astype(jnp.bfloat16), 'head').astype(jnp.float32)]
    all_gather x1 -> x0, waiting for transfers between devices: 23.4 us -> none  [shards(): full_rows = lax.all_gather(encoder_rows, 'head', axis=1, tiled=True)]
    ppermute x0 -> x8, waiting for transfers between devices: none -> 15.4 us  [the longest x3 15.4 us: ring_gather(): from_left = lax.ppermute(from_left, axis, right)]
    ppermute x0 -> x8, starting transfers between devices: none -> 12.8 us  [the longest x3 8.74 us: ring_gather(): from_right = lax.ppermute(from_right, axis, left)]
    unnamed x32 -> x29, local copies, waits for them, and re-layouts: 0.61 us -> 12.6 us
    select_n x0 -> x1, local copies, waits for them, and re-layouts: none -> 8.64 us  [ring_gather(): by_device = jnp.take(ordered, order, axis=0)]
    ppermute x4, starting transfers between devices: 27.4 us -> 19.8 us  [shards(): sent.append(lax.ppermute(piece, 'hyp', route))]
    gather x0 -> x1, local copies, waits for them, and re-layouts: none -> 6.48 us  [ring_gather(): by_device = jnp.take(ordered, order, axis=0)]
  transfers between devices with their start and end apart: 17 -> 24, of which waited for: 6 -> 5; matrix products, arithmetic and copies ran while one was open for 7% -> 25% of each run, Pallas kernels for 0% -> 0%
where the time goes in v2:
time: 237 us; the launch traced here: 235 us
  waiting for transfers between devices  77.1 us (33%)
  starting transfers between devices  58.4 us (25%)
  local copies, waits for them, and re-layouts  37 us (16%)
  other arithmetic  25.9 us (11%)
  matrix products  19.9 us (8%)
  between operations  16.7 us (7%)
    psum x1, waiting for transfers between devices, shards(): lax.psum(partial_out.astype(jnp.bfloat16), 'head').astype(jnp.float32)  45.9 us
    ppermute x4, starting transfers between devices, shards(): sent.append(lax.ppermute(piece, 'hyp', route))  19.8 us
    ppermute x4, starting transfers between devices, shards(): back.append(lax.ppermute(answer[shift], 'hyp', route))  17.7 us
    ppermute x3, waiting for transfers between devices, ring_gather(): from_left = lax.ppermute(from_left, axis, right)  15.4 us
    unnamed x29, local copies, waits for them, and re-layouts  12.6 us
    ppermute x6, waiting for transfers between devices, beam_copies(): copies.append(lax.ppermute(block, 'hyp', route))  12 us
    ppermute x3, starting transfers between devices, ring_gather(): from_right = lax.ppermute(from_right, axis, left)  8.74 us
    select_n x1, local copies, waits for them, and re-layouts, ring_gather(): by_device = jnp.take(ordered, order, axis=0)  8.64 us
  transfers between devices with their start and end apart: 24, of which 5 were waited for; matrix products, arithmetic and copies ran while one was open for 25% of the time, Pallas kernels for 0%

profile of v2, /device:TPU:1, one launch (start us, length us, event | category | flops | bytes accessed | tf_op | source)
XLA Modules:
  0.0 235.1 jit_solution(6972785757054806505)
XLA Ops:
  12.6 2.1 convolution_convert_fusion.4
  14.7 2.1 convolution_convert_fusion.5
  16.8 3.6 %collective-permute-start.3 = (bf16[2,3,16,256]{3,2,0,1:T(8,128)(2,1)S(1)}, bf16[2,3,16,256]{3,2,0,1:T(8,128)(2,1)S(1)}, u32[]{:S(2)}, u32[]{:S(2)}) collective-permute-start(bf16[2,3,16,256]{3,2,0,1:T(8,128)(2,1)S(1)} %pad_maximum_fusion.4), channel_id=1, source_target_pairs={{64,0},{72,8},{80,16},{88,24},{96,32},{104,40},{112,48},{120,56},{... | collective-permute-start | bytes 147464 | tf_op jit(solution)/shard_map/ppermute | solution.py:34
  22.6 2.0 collective-permute-start
  38.7 2.1 convolution_convert_fusion.6
  42.4 11.9 %collective-permute-done.2 = bf16[2,16,32,256]{3,1,2,0:T(8,128)(2,1)S(1)} collective-permute-done((bf16[2,16,32,256]{3,1,2,0:T(8,128)(2,1)}, bf16[2,16,32,256]{3,1,2,0:T(8,128)(2,1)S(1)}, u32[]{:S(2)}, u32[]{:S(2)}) %collective-permute-start.2) | collective-permute-done | bytes 524320 | tf_op jit(solution)/shard_map/ppermute | solution.py:34
  54.3 1.5 select_select_fusion.2
  60.8 1.7 collective-permute-start.10
  62.5 4.0 %collective-permute-start.13 = (bf16[768,512]{1,0:T(8,128)(2,1)S(1)}, bf16[768,512]{1,0:T(8,128)(2,1)}, u32[]{:S(2)}, u32[]{:S(2)}) collective-permute-start(bf16[768,512]{1,0:T(8,128)(2,1)S(1)} %copy-done.3), channel_id=1, source_target_pairs={{0,7},{1,0},{2,1},{3,2},{4,3},{5,4},{6,5},{7,6},{8,15},{9,8},{10,9... | collective-permute-start | bytes 2359304 | tf_op jit(solution)/shard_map/ppermute | solution.py:48
  67.2 15.4 %collective-permute-done.10 = bf16[768,512]{1,0:T(8,128)(2,1)} collective-permute-done((bf16[768,512]{1,0:T(8,128)(2,1)S(1)}, bf16[768,512]{1,0:T(8,128)(2,1)}, u32[]{:S(2)}, u32[]{:S(2)}) %collective-permute-start.10) | collective-permute-done | bytes 786464 | tf_op jit(solution)/shard_map/ppermute | solution.py:47
  82.5 2.7 %collective-permute-start.14 = (bf16[768,512]{1,0:T(8,128)(2,1)}, bf16[768,512]{1,0:T(8,128)(2,1)}, u32[]{:S(2)}, u32[]{:S(2)}) collective-permute-start(bf16[768,512]{1,0:T(8,128)(2,1)} %collective-permute-done.13), channel_id=1, source_target_pairs={{0,7},{1,0},{2,1},{3,2},{4,3},{5,4},{6,5},{7,6},{8,15},{9,8},{10,9... | collective-permute-start | bytes 2359304 | tf_op jit(solution)/shard_map/ppermute | solution.py:48
  86.5 45.9 %all-reduce.2.cloned.1.call-done = bf16[3,16,4096]{2,1,0:T(8,128)(2,1)} async-done(((bf16[3,16,4096]{2,1,0:T(8,128)(2,1)}), bf16[3,16,4096]{2,1,0:T(8,128)(2,1)}) %all-reduce.2.cloned.1.call-update) | async-done | bytes 393232 | tf_op jit(solution)/shard_map/psum | solution.py:177
  134.3 2.0 collective-permute-start.15
  137.5 2.1 convolution_convert_fusion.3
  139.7 4.3 %collective-permute-start.9 = (bf16[3,4,256]{2,1,0:T(4,128)(2,1)S(1)}, bf16[3,4,256]{2,1,0:T(4,128)(2,1)S(1)}, u32[]{:S(2)}, u32[]{:S(2)}) collective-permute-start(bf16[3,4,256]{2,1,0:T(4,128)(2,1)S(1)} %get-tuple-element.43), channel_id=1, source_target_pairs={{0,24},{8,56},{16,88},{24,120},{32,152},{40,184},{48,216},{56,248}... | collective-permute-start | bytes 18440 | tf_op jit(solution)/shard_map/ppermute | solution.py:193
  143.9 5.8 %collective-permute-start.8 = (bf16[3,4,256]{2,1,0:T(4,128)(2,1)S(1)}, bf16[3,4,256]{2,1,0:T(4,128)(2,1)S(1)}, u32[]{:S(2)}, u32[]{:S(2)}) collective-permute-start(bf16[3,4,256]{2,1,0:T(4,128)(2,1)S(1)} %get-tuple-element.44), channel_id=1, source_target_pairs={{0,16},{8,48},{16,80},{24,112},{32,144},{40,176},{48,208},{56,240}... | collective-permute-start | bytes 18440 | tf_op jit(solution)/shard_map/ppermute | solution.py:193
  149.7 5.6 %collective-permute-start.7 = (bf16[3,4,256]{2,1,0:T(4,128)(2,1)S(1)}, bf16[3,4,256]{2,1,0:T(4,128)(2,1)S(1)}, u32[]{:S(2)}, u32[]{:S(2)}) collective-permute-start(bf16[3,4,256]{2,1,0:T(4,128)(2,1)S(1)} %get-tuple-element.45), channel_id=1, source_target_pairs={{0,8},{8,40},{16,72},{24,104},{32,136},{40,168},{48,200},{56,232},... | collective-permute-start | bytes 18440 | tf_op jit(solution)/shard_map/ppermute | solution.py:193
  155.3 4.2 %collective-permute-start.6 = (bf16[3,4,256]{2,1,0:T(4,128)(2,1)S(1)}, bf16[3,4,256]{2,1,0:T(4,128)(2,1)S(1)}, u32[]{:S(2)}, u32[]{:S(2)}) collective-permute-start(bf16[3,4,256]{2,1,0:T(4,128)(2,1)S(1)} %get-tuple-element.42), channel_id=1, source_target_pairs={{0,0},{8,32},{16,64},{24,96},{32,128},{40,160},{48,192},{56,224},{... | collective-permute-start | bytes 18440 | tf_op jit(solution)/shard_map/ppermute | solution.py:193
  163.3 2.1 bitcast_dynamic-update-slice_fusion.6
  165.4 2.1 bitcast_dynamic-update-slice_fusion.5
  167.5 2.1 bitcast_dynamic-update-slice_fusion.4
  170.6 2.1 bitcast_dynamic-update-slice_fusion.2
  172.6 2.1 bitcast_dynamic-update-slice_fusion.1
  176.6 6.5 %gather_fusion = bf16[8,768,512]{2,1,0:T(8,128)(2,1)} fusion(bf16[8,768,512]{2,1,0:T(8,128)(2,1)} %fusion.1, s32[1024]{0:T(1024)} %pad_clamp_fusion.1), kind=kCustom, calls=%fused_computation.6 | custom fusion | bytes 12582944 | tf_op jit(solution)/shard_map/jit(_take)/gather | solution.py:59
  183.1 6.1 %select_bitcast_fusion = bf16[768,8,512]{2,0,1:T(8,128)(2,1)} fusion(bf16[8,768,512]{2,1,0:T(8,128)(2,1)} %gather_fusion, pred[8]{0:T(512)(128)(4,1)S(1)} %compare_and_fusion), kind=kLoop, calls=%fused_computation.8 | loop fusion | flops 3145728 | bytes 12582920 | tf_op jit(solution)/shard_map/jit(_take)/select_n | solution.py:59
  189.2 8.6 %copy.63 = bf16[768,8,512]{0,2,1:T(8,128)(2,1)} copy(bf16[768,8,512]{2,0,1:T(8,128)(2,1)} %select_bitcast_fusion) | data formatting | bytes 12582912 | tf_op jit(solution)/shard_map/jit(_take)/select_n | solution.py:59
  197.8 7.5 %convolution_convert_fusion.1 = bf16[768,512]{0,1:T(8,128)(2,1)S(1)} fusion(bf16[768,4096]{0,1:T(8,128)(2,1)} %bitcast.304, bf16[4096,512]{1,0:T(8,128)(2,1)} %all-gather.2.cloned.1.call-done), kind=kOutput, calls=%fused_computation.10 | convolution fusion | flops 3221618688 | bytes 11272192 | tf_op jit(solution)/shard_map/dot_general | solution.py:109
  206.1 9.5 %collective-permute-start.21 = (bf16[3,4,256]{2,1,0:T(4,128)(2,1)S(1)}, bf16[3,4,256]{2,1,0:T(4,128)(2,1)S(1)}, u32[]{:S(2)}, u32[]{:S(2)}) collective-permute-start(bf16[3,4,256]{2,1,0:T(4,128)(2,1)S(1)} %squeeze.124), channel_id=1, source_target_pairs={{24,0},{56,8},{88,16},{120,24},{152,32},{184,40},{216,48},{248,56}... | collective-permute-start | bytes 18440 | tf_op jit(solution)/shard_map/ppermute | solution.py:205
  215.7 2.1 collective-permute-start.20
  217.8 1.9 collective-permute-start.19
  219.7 4.1 %collective-permute-start.18 = (bf16[3,4,256]{2,1,0:T(4,128)(2,1)S(1)}, bf16[3,4,256]{2,1,0:T(4,128)(2,1)S(1)}, u32[]{:S(2)}, u32[]{:S(2)}) collective-permute-start(bf16[3,4,256]{2,1,0:T(4,128)(2,1)S(1)} %squeeze.121), channel_id=1, source_target_pairs={{0,0},{32,8},{64,16},{96,24},{128,32},{160,40},{192,48},{224,56},{... | collective-permute-start | bytes 18440 | tf_op jit(solution)/shard_map/ppermute | solution.py:205
  223.9 2.3 collective-permute-done.18
  (151 shorter events, 40.5 us)
Async XLA Ops:
  8.0 50.9 %copy-start = (bf16[256,4096]{1,0:T(8,128)(2,1)S(1)}, bf16[256,4096]{1,0:T(8,128)(2,1)}, u32[]{:S(2)}) copy-start(bf16[256,4096]{1,0:T(8,128)(2,1)} %param.25) | copy-start | bytes 6291460
  8.0 18.0 %copy-start.9 = (s32[3,512]{1,0:T(4,128)S(1)}, s32[3,512]{1,0:T(4,128)}, u32[]{:S(2)}) copy-start(s32[3,512]{1,0:T(4,128)} %param.33) | copy-start | bytes 18436
  8.0 124.3 %all-reduce.2.cloned.1.call-start = ((), (), s32[]{:S(2)}) async-start(), calls=%async_computation | async-start | bytes 786432 | tf_op jit(solution)/shard_map/psum | solution.py:177
  9.2 12.3 %copy-start.6 = (bf16[16,32,256]{2,1,0:T(8,128)(2,1)S(1)}, bf16[16,32,256]{2,1,0:T(8,128)(2,1)}, u32[]{:S(2)}) copy-start(bf16[16,32,256]{2,1,0:T(8,128)(2,1)} %param.32) | copy-start | bytes 786436
  9.2 12.3 %copy-start.7 = (bf16[16,32,256]{2,1,0:T(8,128)(2,1)S(1)}, bf16[16,32,256]{2,1,0:T(8,128)(2,1)}, u32[]{:S(2)}) copy-start(bf16[16,32,256]{2,1,0:T(8,128)(2,1)} %param.31) | copy-start | bytes 786436
  16.8 24.7 %collective-permute-start.3 = (bf16[2,3,16,256]{3,2,0,1:T(8,128)(2,1)S(1)}, bf16[2,3,16,256]{3,2,0,1:T(8,128)(2,1)S(1)}, u32[]{:S(2)}, u32[]{:S(2)}) collective-permute-start(bf16[2,3,16,256]{3,2,0,1:T(8,128)(2,1)S(1)} %pad_maximum_fusion.4), channel_id=1, source_target_pairs={{64,0},{72,8},{80,16},{88,24},{96,32},{104,40},{112,48},{120,56},{... | collective-permute-start | bytes 147464 | tf_op jit(solution)/shard_map/ppermute | solution.py:34
  20.4 21.1 %collective-permute-start.4 = (bf16[2,3,16,256]{3,2,0,1:T(8,128)(2,1)S(1)}, bf16[2,3,16,256]{3,2,0,1:T(8,128)(2,1)S(1)}, u32[]{:S(2)}, u32[]{:S(2)}) collective-permute-start(bf16[2,3,16,256]{3,2,0,1:T(8,128)(2,1)S(1)} %pad_maximum_fusion.4), channel_id=1, source_target_pairs={{128,0},{136,8},{144,16},{152,24},{160,32},{168,40},{176,48},{184,... | collective-permute-start | bytes 147464 | tf_op jit(solution)/shard_map/ppermute | solution.py:34
  20.8 20.7 %collective-permute-start.5 = (bf16[2,3,16,256]{3,2,0,1:T(8,128)(2,1)S(1)}, bf16[2,3,16,256]{3,2,0,1:T(8,128)(2,1)S(1)}, u32[]{:S(2)}, u32[]{:S(2)}) collective-permute-start(bf16[2,3,16,256]{3,2,0,1:T(8,128)(2,1)S(1)} %pad_maximum_fusion.4), channel_id=1, source_target_pairs={{192,0},{200,8},{208,16},{216,24},{224,32},{232,40},{240,48},{248,... | collective-permute-start | bytes 147464 | tf_op jit(solution)/shard_map/ppermute | solution.py:34
  22.6 19.8 %collective-permute-start = (bf16[2,16,32,256]{3,1,2,0:T(8,128)(2,1)}, bf16[2,16,32,256]{3,1,2,0:T(8,128)(2,1)}, u32[]{:S(2)}, u32[]{:S(2)}) collective-permute-start(bf16[2,16,32,256]{3,1,2,0:T(8,128)(2,1)} %pad_maximum_fusion.2), channel_id=1, source_target_pairs={{64,0},{72,8},{80,16},{88,24},{96,32},{104,40},{112,48},{120,56},{... | collective-permute-start | bytes 1572872 | tf_op jit(solution)/shard_map/ppermute | solution.py:34
  24.6 17.8 %collective-permute-start.1 = (bf16[2,16,32,256]{3,1,2,0:T(8,128)(2,1)}, bf16[2,16,32,256]{3,1,2,0:T(8,128)(2,1)}, u32[]{:S(2)}, u32[]{:S(2)}) collective-permute-start(bf16[2,16,32,256]{3,1,2,0:T(8,128)(2,1)} %pad_maximum_fusion.2), channel_id=1, source_target_pairs={{128,0},{136,8},{144,16},{152,24},{160,32},{168,40},{176,48},{184,... | collective-permute-start | bytes 1572872 | tf_op jit(solution)/shard_map/ppermute | solution.py:34
  41.5 12.8 %collective-permute-start.2 = (bf16[2,16,32,256]{3,1,2,0:T(8,128)(2,1)}, bf16[2,16,32,256]{3,1,2,0:T(8,128)(2,1)S(1)}, u32[]{:S(2)}, u32[]{:S(2)}) collective-permute-start(bf16[2,16,32,256]{3,1,2,0:T(8,128)(2,1)} %pad_maximum_fusion.2), channel_id=1, source_target_pairs={{192,0},{200,8},{208,16},{216,24},{224,32},{232,40},{240,48},{248,... | collective-permute-start | bytes 1572872 | tf_op jit(solution)/shard_map/ppermute | solution.py:34
  55.8 4.9 %copy-start.3 = (bf16[768,512]{1,0:T(8,128)(2,1)S(1)}, bf16[768,512]{1,0:T(8,128)(2,1)}, u32[]{:S(2)}) copy-start(bf16[768,512]{1,0:T(8,128)(2,1)} %param.29) | copy-start | bytes 2359300
  55.8 76.5 %copy-start.1 = (bf16[3,16,4096]{2,1,0:T(8,128)(2,1)S(1)}, bf16[3,16,4096]{2,1,0:T(8,128)(2,1)}, u32[]{:S(2)}) copy-start(bf16[3,16,4096]{2,1,0:T(8,128)(2,1)} %param.18) | copy-start | bytes 1179652
  55.8 80.5 %copy-start.8 = (f32[4096]{0:T(1024)S(1)}, f32[4096]{0:T(1024)}, u32[]{:S(2)}) copy-start(f32[4096]{0:T(1024)} %param.26) | copy-start | bytes 49156
  60.2 137.7 %all-gather.2.cloned.1.call-start = ((), (), s32[]{:S(2)}) async-start(), calls=%async_computation.1 | async-start | bytes 4325376 | tf_op jit(solution)/shard_map/all_gather | solution.py:107
  60.8 21.8 %collective-permute-start.10 = (bf16[768,512]{1,0:T(8,128)(2,1)S(1)}, bf16[768,512]{1,0:T(8,128)(2,1)}, u32[]{:S(2)}, u32[]{:S(2)}) collective-permute-start(bf16[768,512]{1,0:T(8,128)(2,1)S(1)} %copy-done.3), channel_id=1, source_target_pairs={{0,1},{1,2},{2,3},{3,4},{4,5},{5,6},{6,7},{7,0},{8,9},{9,10},{10,1... | collective-permute-start | bytes 2359304 | tf_op jit(solution)/shard_map/ppermute | solution.py:47
  62.5 20.1 %collective-permute-start.13 = (bf16[768,512]{1,0:T(8,128)(2,1)S(1)}, bf16[768,512]{1,0:T(8,128)(2,1)}, u32[]{:S(2)}, u32[]{:S(2)}) collective-permute-start(bf16[768,512]{1,0:T(8,128)(2,1)S(1)} %copy-done.3), channel_id=1, source_target_pairs={{0,7},{1,0},{2,1},{3,2},{4,3},{5,4},{6,5},{7,6},{8,15},{9,8},{10,9... | collective-permute-start | bytes 2359304 | tf_op jit(solution)/shard_map/ppermute | solution.py:48
  82.5 51.1 %collective-permute-start.11 = (bf16[768,512]{1,0:T(8,128)(2,1)}, bf16[768,512]{1,0:T(8,128)(2,1)}, u32[]{:S(2)}, u32[]{:S(2)}) collective-permute-start(bf16[768,512]{1,0:T(8,128)(2,1)} %collective-permute-done.10), channel_id=1, source_target_pairs={{0,1},{1,2},{2,3},{3,4},{4,5},{5,6},{6,7},{7,0},{8,9},{9,10},{10,1... | collective-permute-start | bytes 2359304 | tf_op jit(solution)/shard_map/ppermute | solution.py:47
  82.5 51.8 %collective-permute-start.14 = (bf16[768,512]{1,0:T(8,128)(2,1)}, bf16[768,512]{1,0:T(8,128)(2,1)}, u32[]{:S(2)}, u32[]{:S(2)}) collective-permute-start(bf16[768,512]{1,0:T(8,128)(2,1)} %collective-permute-done.13), channel_id=1, source_target_pairs={{0,7},{1,0},{2,1},{3,2},{4,3},{5,4},{6,5},{7,6},{8,15},{9,8},{10,9... | collective-permute-start | bytes 2359304 | tf_op jit(solution)/shard_map/ppermute | solution.py:48
  133.6 27.5 %collective-permute-start.12 = (bf16[768,512]{1,0:T(8,128)(2,1)}, bf16[768,512]{1,0:T(8,128)(2,1)}, u32[]{:S(2)}, u32[]{:S(2)}) collective-permute-start(bf16[768,512]{1,0:T(8,128)(2,1)} %collective-permute-done.11), channel_id=1, source_target_pairs={{0,1},{1,2},{2,3},{3,4},{4,5},{5,6},{6,7},{7,0},{8,9},{9,10},{10,1... | collective-permute-start | bytes 2359304 | tf_op jit(solution)/shard_map/ppermute | solution.py:47
  134.3 26.3 %collective-permute-start.15 = (bf16[768,512]{1,0:T(8,128)(2,1)}, bf16[768,512]{1,0:T(8,128)(2,1)S(1)}, u32[]{:S(2)}, u32[]{:S(2)}) collective-permute-start(bf16[768,512]{1,0:T(8,128)(2,1)} %collective-permute-done.14), channel_id=1, source_target_pairs={{0,7},{1,0},{2,1},{3,2},{4,3},{5,4},{6,5},{7,6},{8,15},{9,8},{10,9... | collective-permute-start | bytes 2359304 | tf_op jit(solution)/shard_map/ppermute | solution.py:48
  139.7 15.7 %collective-permute-start.9 = (bf16[3,4,256]{2,1,0:T(4,128)(2,1)S(1)}, bf16[3,4,256]{2,1,0:T(4,128)(2,1)S(1)}, u32[]{:S(2)}, u32[]{:S(2)}) collective-permute-start(bf16[3,4,256]{2,1,0:T(4,128)(2,1)S(1)} %get-tuple-element.43), channel_id=1, source_target_pairs={{0,24},{8,56},{16,88},{24,120},{32,152},{40,184},{48,216},{56,248}... | collective-permute-start | bytes 18440 | tf_op jit(solution)/shard_map/ppermute | solution.py:193
  143.9 15.6 %collective-permute-start.8 = (bf16[3,4,256]{2,1,0:T(4,128)(2,1)S(1)}, bf16[3,4,256]{2,1,0:T(4,128)(2,1)S(1)}, u32[]{:S(2)}, u32[]{:S(2)}) collective-permute-start(bf16[3,4,256]{2,1,0:T(4,128)(2,1)S(1)} %get-tuple-element.44), channel_id=1, source_target_pairs={{0,16},{8,48},{16,80},{24,112},{32,144},{40,176},{48,208},{56,240}... | collective-permute-start | bytes 18440 | tf_op jit(solution)/shard_map/ppermute | solution.py:193
  149.7 9.8 %collective-permute-start.7 = (bf16[3,4,256]{2,1,0:T(4,128)(2,1)S(1)}, bf16[3,4,256]{2,1,0:T(4,128)(2,1)S(1)}, u32[]{:S(2)}, u32[]{:S(2)}) collective-permute-start(bf16[3,4,256]{2,1,0:T(4,128)(2,1)S(1)} %get-tuple-element.45), channel_id=1, source_target_pairs={{0,8},{8,40},{16,72},{24,104},{32,136},{40,168},{48,200},{56,232},... | collective-permute-start | bytes 18440 | tf_op jit(solution)/shard_map/ppermute | solution.py:193
  155.3 5.2 %collective-permute-start.6 = (bf16[3,4,256]{2,1,0:T(4,128)(2,1)S(1)}, bf16[3,4,256]{2,1,0:T(4,128)(2,1)S(1)}, u32[]{:S(2)}, u32[]{:S(2)}) collective-permute-start(bf16[3,4,256]{2,1,0:T(4,128)(2,1)S(1)} %get-tuple-element.42), channel_id=1, source_target_pairs={{0,0},{8,32},{16,64},{24,96},{32,128},{40,160},{48,192},{56,224},{... | collective-permute-start | bytes 18440 | tf_op jit(solution)/shard_map/ppermute | solution.py:193
  160.6 9.0 %copy-start.4 = (bf16[768,512]{1,0:T(8,128)(2,1)S(1)}, bf16[768,512]{1,0:T(8,128)(2,1)}, u32[]{:S(2)}) copy-start(bf16[768,512]{1,0:T(8,128)(2,1)} %param.29) | copy-start | bytes 2359300
  160.7 15.0 %collective-permute-start.17 = (bf16[384,512]{1,0:T(8,128)(2,1)S(1)}, bf16[384,512]{1,0:T(8,128)(2,1)S(1)}, u32[]{:S(2)}, u32[]{:S(2)}) collective-permute-start(bf16[384,512]{1,0:T(8,128)(2,1)S(1)} %slice.184), channel_id=1, source_target_pairs={{0,7},{1,0},{2,1},{3,2},{4,3},{5,4},{6,5},{7,6},{8,15},{9,8},{10,9... | collective-permute-start | bytes 1179656 | tf_op jit(solution)/shard_map/ppermute | solution.py:54
  162.1 13.6 %collective-permute-start.16 = (bf16[384,512]{1,0:T(8,128)(2,1)S(1)}, bf16[384,512]{1,0:T(8,128)(2,1)S(1)}, u32[]{:S(2)}, u32[]{:S(2)}) collective-permute-start(bf16[384,512]{1,0:T(8,128)(2,1)S(1)} %slice.183), channel_id=1, source_target_pairs={{0,1},{1,2},{2,3},{3,4},{4,5},{5,6},{6,7},{7,0},{8,9},{9,10},{10,1... | collective-permute-start | bytes 1179656 | tf_op jit(solution)/shard_map/ppermute | solution.py:53
  206.1 17.8 %collective-permute-start.21 = (bf16[3,4,256]{2,1,0:T(4,128)(2,1)S(1)}, bf16[3,4,256]{2,1,0:T(4,128)(2,1)S(1)}, u32[]{:S(2)}, u32[]{:S(2)}) collective-permute-start(bf16[3,4,256]{2,1,0:T(4,128)(2,1)S(1)} %squeeze.124), channel_id=1, source_target_pairs={{24,0},{56,8},{88,16},{120,24},{152,32},{184,40},{216,48},{248,56}... | collective-permute-start | bytes 18440 | tf_op jit(solution)/shard_map/ppermute | solution.py:205
  215.7 8.2 %collective-permute-start.20 = (bf16[3,4,256]{2,1,0:T(4,128)(2,1)S(1)}, bf16[3,4,256]{2,1,0:T(4,128)(2,1)S(1)}, u32[]{:S(2)}, u32[]{:S(2)}) collective-permute-start(bf16[3,4,256]{2,1,0:T(4,128)(2,1)S(1)} %squeeze.123), channel_id=1, source_target_pairs={{16,0},{48,8},{80,16},{112,24},{144,32},{176,40},{208,48},{240,56}... | collective-permute-start | bytes 18440 | tf_op jit(solution)/shard_map/ppermute | solution.py:205
  217.8 6.1 %collective-permute-start.19 = (bf16[3,4,256]{2,1,0:T(4,128)(2,1)S(1)}, bf16[3,4,256]{2,1,0:T(4,128)(2,1)S(1)}, u32[]{:S(2)}, u32[]{:S(2)}) collective-permute-start(bf16[3,4,256]{2,1,0:T(4,128)(2,1)S(1)} %squeeze.122), channel_id=1, source_target_pairs={{8,0},{40,8},{72,16},{104,24},{136,32},{168,40},{200,48},{232,56},... | collective-permute-start | bytes 18440 | tf_op jit(solution)/shard_map/ppermute | solution.py:205
  219.7 6.5 %collective-permute-start.18 = (bf16[3,4,256]{2,1,0:T(4,128)(2,1)S(1)}, bf16[3,4,256]{2,1,0:T(4,128)(2,1)S(1)}, u32[]{:S(2)}, u32[]{:S(2)}) collective-permute-start(bf16[3,4,256]{2,1,0:T(4,128)(2,1)S(1)} %squeeze.121), channel_id=1, source_target_pairs={{0,0},{32,8},{64,16},{96,24},{128,32},{160,40},{192,48},{224,56},{... | collective-permute-start | bytes 18440 | tf_op jit(solution)/shard_map/ppermute | solution.py:205
  (3 other events, 4.2 us)
Sparse Core Ops, SparseCore 0:
  60.3 72.0 all-reduce.1
Sparse Core Ops, SparseCore 1:
  63.2 54.1 all-gather.1

commit v3 on v2

--- a/solution.py
+++ b/solution.py
@@ -35,29 +35,32 @@
     return copies
 
 
-def ring_gather(block, axis):
+def ring_project(block, weights, axis):
     count = lax.axis_size(axis)
     me = lax.axis_index(axis)
+    width = block.shape[1]
     right = [(i, (i + 1) % count) for i in range(count)]
     left = [(i, (i - 1) % count) for i in range(count)]
-    pieces = {0: block}
+
+    def partial(piece, offset):
+        source = (me + offset) % count
+        w = lax.dynamic_slice_in_dim(weights, source * width, width, 0)
+        return jnp.dot(piece, w, preferred_element_type=jnp.float32)
+
+    total = partial(block, 0)
     from_left = block
     from_right = block
     for hop in range(1, count // 2):
         from_left = lax.ppermute(from_left, axis, right)
         from_right = lax.ppermute(from_right, axis, left)
-        pieces[-hop] = from_left
-        pieces[hop] = from_right
+        total = total + partial(from_left, -hop) + partial(from_right, hop)
     if count % 2 == 0 and count > 1:
         half = block.shape[0] // 2
         top = lax.ppermute(from_left[:half], axis, right)
         bottom = lax.ppermute(from_right[half:], axis, left)
-        pieces[count // 2] = jnp.concatenate([top, bottom], axis=0)
-    ordered = jnp.stack([pieces[d] if d in pieces else pieces[d - count] for d in range(count // 2 - count + 1, count // 2 + 1)])
-    first = (me + count // 2 - count + 1) % count
-    order = (jnp.arange(count, dtype=jnp.int32) - first) % count
-    by_device = jnp.take(ordered, order, axis=0)
-    return by_device.transpose(1, 0, 2).reshape(block.shape[0], count * block.shape[1])
+        last = jnp.concatenate([top, bottom], axis=0)
+        total = total + partial(last, count // 2)
+    return total
 
 
 def cross_attend(queries, cross_keys, cross_values, doc_length, scaling):
@@ -105,10 +108,7 @@
     scaling = HEAD ** (-0.5)
 
     full_weights = lax.all_gather(cross_wkv, "hyp", axis=0, tiled=True)
-    full_rows = ring_gather(encoder_rows, "head")
-    cross_kv = jnp.dot(full_rows, full_weights, preferred_element_type=jnp.float32).astype(
-        jnp.bfloat16
-    )
+    cross_kv = ring_project(encoder_rows, full_weights, "head").astype(jnp.bfloat16)
     cross_kv = cross_kv.reshape(encoder_rows.shape[0], 2, HEAD)
     cross_keys = cross_kv[:, 0, :]
     cross_values = cross_kv[:, 1, :]
@@ -163,18 +163,23 @@
             final_cache = cache
         query = new_query[step_idx]
         scores = (
-            jnp.einsum("rd,rpd->rp", query, cache[0], preferred_element_type=jnp.float32) * scaling
+            jnp.einsum("rd,rpd->rp", query, cache[0], preferred_element_type=jnp.float32)
+            * scaling
         )
         highest = jnp.max(scores, axis=1, keepdims=True)
         raw_weights = jnp.exp(scores - highest)
         totals = jnp.sum(raw_weights, axis=1, keepdims=True)
         summed = jnp.einsum(
-            "rp,rpd->rd", raw_weights, cache[1].astype(jnp.float32), preferred_element_type=jnp.float32
+            "rp,rpd->rd",
+            raw_weights,
+            cache[1].astype(jnp.float32),
+            preferred_element_type=jnp.float32,
         )
         contexts.append((summed / totals).astype(jnp.bfloat16))
     self_context = jnp.stack(contexts).reshape(steps * row_count, head_width)
     partial_out = jnp.dot(self_context, self_wo, preferred_element_type=jnp.float32)
-    summed_out = lax.psum(partial_out.astype(jnp.bfloat16), "head").astype(jnp.float32)
+    every_part = lax.all_gather(partial_out.astype(jnp.bfloat16), "head", axis=0, tiled=False)
+    summed_out = jnp.sum(every_part.astype(jnp.float32), axis=0)
     residual = hidden_in + summed_out.reshape(hidden_in.shape)
     normed_cross = rms_scaled(residual, cross_gain).astype(jnp.bfloat16)
     cross_query = jnp.dot(

time: 237 us -> 220 us (0.928)
  local copies, waits for them, and re-layouts: 37 us -> 12.1 us
  waiting for transfers between devices: 77.1 us -> 96.6 us
  other arithmetic: 25.9 us -> 14 us
    psum x1 -> x0, waiting for transfers between devices: 45.9 us -> none  [shards(): lax.psum(partial_out.astype(jnp.bfloat16), 'head').astype(jnp.float32)]
    ppermute x8, waiting for transfers between devices: 15.4 us -> 52.3 us  [the longest x3 52.3 us: ring_project(): from_right = lax.ppermute(from_right, axis, left)]
    all_gather x1, waiting for transfers between devices: 0.01 us -> 24.3 us  [shards(): full_weights = lax.all_gather(cross_wkv, 'hyp', axis=0, tiled=True)]
    unnamed x29 -> x38, local copies, waits for them, and re-layouts: 12.6 us -> 1.93 us
    select_n x1 -> x0, local copies, waits for them, and re-layouts: 8.64 us -> none  [ring_gather(): by_device = jnp.take(ordered, order, axis=0)]
    gather x1 -> x0, local copies, waits for them, and re-layouts: 6.48 us -> none  [ring_gather(): by_device = jnp.take(ordered, order, axis=0)]
    select_n x2 -> x0, other arithmetic: 6.08 us -> none  [ring_gather(): by_device = jnp.take(ordered, order, axis=0)]
    all_gather x0 -> x1, waiting for transfers between devices: none -> 6.04 us  [shards(): lax.all_gather(partial_out.astype(jnp.bfloat16), 'head', axis=0, tiled=Fa...]
  transfers between devices with their start and end apart: 24 -> 24, of which waited for: 5 -> 6; matrix products, arithmetic and copies ran while one was open for 25% -> 13% of each run, Pallas kernels for 0% -> 0%
where the time goes in v3:
time: 220 us; the launch traced here: 216 us
  waiting for transfers between devices  96.6 us (44%)
  starting transfers between devices  56.5 us (26%)
  matrix products  21.6 us (10%)
  between operations  15.6 us (7%)
  other arithmetic  14 us (6%)
  local copies, waits for them, and re-layouts  12.1 us (6%)
    ppermute x3, waiting for transfers between devices, ring_project(): from_right = lax.ppermute(from_right, axis, left)  52.3 us
    all_gather x1, waiting for transfers between devices, shards(): full_weights = lax.all_gather(cross_wkv, 'hyp', axis=0, tiled=True)  24.3 us
    ppermute x4, starting transfers between devices, shards(): sent.append(lax.ppermute(piece, 'hyp', route))  18.3 us
    ppermute x4, starting transfers between devices, shards(): back.append(lax.ppermute(answer[shift], 'hyp', route))  14.4 us
    ppermute x3, starting transfers between devices, ring_project(): from_right = lax.ppermute(from_right, axis, left)  12.6 us
    ppermute x6, waiting for transfers between devices, beam_copies(): copies.append(lax.ppermute(block, 'hyp', route))  12.6 us
    dot_general x8, matrix products, partial(): return jnp.dot(piece, w, preferred_element_type=jnp.float32)  12.4 us
    ppermute x6, starting transfers between devices, beam_copies(): copies.append(lax.ppermute(block, 'hyp', route))  8.15 us
  transfers between devices with their start and end apart: 24, of which 6 were waited for; matrix products, arithmetic and copies ran while one was open for 13% of the time, Pallas kernels for 0%

profile of v3, /device:TPU:1, one launch (start us, length us, event | category | flops | bytes accessed | tf_op | source)
XLA Modules:
  0.0 216.5 jit_solution(8226138228956062717)
XLA Ops:
  9.4 1.3 multiply_reduce_fusion.1
  11.9 2.1 convolution_convert_fusion.3
  14.6 3.6 %collective-permute-start.3 = (bf16[2,3,16,256]{3,2,0,1:T(8,128)(2,1)S(1)}, bf16[2,3,16,256]{3,2,0,1:T(8,128)(2,1)S(1)}, u32[]{:S(2)}, u32[]{:S(2)}) collective-permute-start(bf16[2,3,16,256]{3,2,0,1:T(8,128)(2,1)S(1)} %pad_maximum_fusion.4), channel_id=1, source_target_pairs={{64,0},{72,8},{80,16},{88,24},{96,32},{104,40},{112,48},{120,56},{... | collective-permute-start | bytes 147464 | tf_op jit(solution)/shard_map/ppermute | solution.py:34
  20.4 2.0 collective-permute-start
  22.3 1.4 collective-permute-start.1
  33.6 2.1 convolution_convert_fusion.5
  36.0 12.5 %collective-permute-done.2 = bf16[2,16,32,256]{3,1,2,0:T(8,128)(2,1)S(1)} collective-permute-done((bf16[2,16,32,256]{3,1,2,0:T(8,128)(2,1)}, bf16[2,16,32,256]{3,1,2,0:T(8,128)(2,1)S(1)}, u32[]{:S(2)}, u32[]{:S(2)}) %collective-permute-start.2) | collective-permute-done | bytes 524320 | tf_op jit(solution)/shard_map/ppermute | solution.py:34
  48.6 1.5 select_select_fusion.2
  55.2 5.7 %collective-permute-start.11 = (bf16[768,512]{1,0:T(8,128)(2,1)S(1)}, bf16[768,512]{1,0:T(8,128)(2,1)}, u32[]{:S(2)}, u32[]{:S(2)}) collective-permute-start(bf16[768,512]{1,0:T(8,128)(2,1)S(1)} %copy-done.6), channel_id=1, source_target_pairs={{0,7},{1,0},{2,1},{3,2},{4,3},{5,4},{6,5},{7,6},{8,15},{9,8},{10,9... | collective-permute-start | bytes 2359304 | tf_op jit(solution)/shard_map/ppermute | solution.py:55
  60.8 20.1 %collective-permute-done.11 = bf16[768,512]{1,0:T(8,128)(2,1)} collective-permute-done((bf16[768,512]{1,0:T(8,128)(2,1)S(1)}, bf16[768,512]{1,0:T(8,128)(2,1)}, u32[]{:S(2)}, u32[]{:S(2)}) %collective-permute-start.11) | collective-permute-done | bytes 786464 | tf_op jit(solution)/shard_map/ppermute | solution.py:55
  81.0 3.5 %collective-permute-start.13 = (bf16[768,512]{1,0:T(8,128)(2,1)}, bf16[768,512]{1,0:T(8,128)(2,1)}, u32[]{:S(2)}, u32[]{:S(2)}) collective-permute-start(bf16[768,512]{1,0:T(8,128)(2,1)} %collective-permute-done.11), channel_id=1, source_target_pairs={{0,7},{1,0},{2,1},{3,2},{4,3},{5,4},{6,5},{7,6},{8,15},{9,8},{10,9... | collective-permute-start | bytes 2359304 | tf_op jit(solution)/shard_map/ppermute | solution.py:55
  85.2 32.1 %collective-permute-done.13 = bf16[768,512]{1,0:T(8,128)(2,1)} collective-permute-done((bf16[768,512]{1,0:T(8,128)(2,1)}, bf16[768,512]{1,0:T(8,128)(2,1)}, u32[]{:S(2)}, u32[]{:S(2)}) %collective-permute-start.13) | collective-permute-done | bytes 786464 | tf_op jit(solution)/shard_map/ppermute | solution.py:55
  117.3 3.4 %collective-permute-start.15 = (bf16[768,512]{1,0:T(8,128)(2,1)}, bf16[768,512]{1,0:T(8,128)(2,1)S(1)}, u32[]{:S(2)}, u32[]{:S(2)}) collective-permute-start(bf16[768,512]{1,0:T(8,128)(2,1)} %collective-permute-done.13), channel_id=1, source_target_pairs={{0,7},{1,0},{2,1},{3,2},{4,3},{5,4},{6,5},{7,6},{8,15},{9,8},{10,9... | collective-permute-start | bytes 2359304 | tf_op jit(solution)/shard_map/ppermute | solution.py:55
  120.7 6.0 %all-gather.6.cloned.1.call-done = bf16[384,4096]{1,0:T(8,128)(2,1)} async-done(((bf16[48,4096]{1,0:T(8,128)(2,1)}), bf16[384,4096]{1,0:T(8,128)(2,1)}) %all-gather.6.cloned.1.call-update) | async-done | bytes 3145744 | tf_op jit(solution)/shard_map/all_gather | solution.py:181
  126.8 2.4 %convert_reduce_fusion = f32[48,4096]{1,0:T(8,128)S(1)} fusion(bf16[8,48,4096]{2,1,0:T(8,128)(2,1)} %bitcast.294), kind=kLoop, calls=%fused_computation.7 | loop fusion | flops 2949120 | bytes 3932160 | tf_op jit(solution)/shard_map/reduce_sum | solution.py:182
  131.3 4.3 %collective-permute-start.9 = (bf16[3,4,256]{2,1,0:T(4,128)(2,1)S(1)}, bf16[3,4,256]{2,1,0:T(4,128)(2,1)S(1)}, u32[]{:S(2)}, u32[]{:S(2)}) collective-permute-start(bf16[3,4,256]{2,1,0:T(4,128)(2,1)S(1)} %get-tuple-element.43), channel_id=1, source_target_pairs={{0,24},{8,56},{16,88},{24,120},{32,152},{40,184},{48,216},{56,248}... | collective-permute-start | bytes 18440 | tf_op jit(solution)/shard_map/ppermute | solution.py:198
  135.7 4.3 %collective-permute-start.8 = (bf16[3,4,256]{2,1,0:T(4,128)(2,1)S(1)}, bf16[3,4,256]{2,1,0:T(4,128)(2,1)S(1)}, u32[]{:S(2)}, u32[]{:S(2)}) collective-permute-start(bf16[3,4,256]{2,1,0:T(4,128)(2,1)S(1)} %get-tuple-element.44), channel_id=1, source_target_pairs={{0,16},{8,48},{16,80},{24,112},{32,144},{40,176},{48,208},{56,240}... | collective-permute-start | bytes 18440 | tf_op jit(solution)/shard_map/ppermute | solution.py:198
  140.0 3.2 %collective-permute-start.7 = (bf16[3,4,256]{2,1,0:T(4,128)(2,1)S(1)}, bf16[3,4,256]{2,1,0:T(4,128)(2,1)S(1)}, u32[]{:S(2)}, u32[]{:S(2)}) collective-permute-start(bf16[3,4,256]{2,1,0:T(4,128)(2,1)S(1)} %get-tuple-element.45), channel_id=1, source_target_pairs={{0,8},{8,40},{16,72},{24,104},{32,136},{40,168},{48,200},{56,232},... | collective-permute-start | bytes 18440 | tf_op jit(solution)/shard_map/ppermute | solution.py:198
  143.2 6.5 %collective-permute-start.6 = (bf16[3,4,256]{2,1,0:T(4,128)(2,1)S(1)}, bf16[3,4,256]{2,1,0:T(4,128)(2,1)S(1)}, u32[]{:S(2)}, u32[]{:S(2)}) collective-permute-start(bf16[3,4,256]{2,1,0:T(4,128)(2,1)S(1)} %get-tuple-element.42), channel_id=1, source_target_pairs={{0,0},{8,32},{16,64},{24,96},{32,128},{40,160},{48,192},{56,224},{... | collective-permute-start | bytes 18440 | tf_op jit(solution)/shard_map/ppermute | solution.py:198
  150.6 2.9 %collective-permute-start.17 = (bf16[384,512]{1,0:T(8,128)(2,1)}, bf16[384,512]{1,0:T(8,128)(2,1)S(1)}, u32[]{:S(2)}, u32[]{:S(2)}) collective-permute-start(bf16[384,512]{1,0:T(8,128)(2,1)} %slice.182), channel_id=1, source_target_pairs={{0,7},{1,0},{2,1},{3,2},{4,3},{5,4},{6,5},{7,6},{8,15},{9,8},{10,9... | collective-permute-start | bytes 1179656 | tf_op jit(solution)/shard_map/ppermute | solution.py:60
  153.6 1.8 slice.181
  155.4 24.3 %all-gather.4.cloned.1.call-done = bf16[4096,512]{1,0:T(8,128)(2,1)} async-done(((bf16[128,512]{1,0:T(8,128)(2,1)}), bf16[4096,512]{1,0:T(8,128)(2,1)}) %all-gather.4.cloned.1.call-update) | async-done | bytes 4194320 | tf_op jit(solution)/shard_map/all_gather | solution.py:110
  179.8 2.1 fusion.12
  181.8 1.9 fusion.14
  183.8 1.8 fusion.16
  185.5 1.8 fusion.18
  188.0 1.8 fusion.20
  189.8 1.6 fusion.2
  193.1 3.8 %collective-permute-start.21 = (bf16[3,4,256]{2,1,0:T(4,128)(2,1)S(1)}, bf16[3,4,256]{2,1,0:T(4,128)(2,1)S(1)}, u32[]{:S(2)}, u32[]{:S(2)}) collective-permute-start(bf16[3,4,256]{2,1,0:T(4,128)(2,1)S(1)} %squeeze.124), channel_id=1, source_target_pairs={{24,0},{56,8},{88,16},{120,24},{152,32},{184,40},{216,48},{248,56}... | collective-permute-start | bytes 18440 | tf_op jit(solution)/shard_map/ppermute | solution.py:210
  196.9 2.5 %collective-permute-start.20 = (bf16[3,4,256]{2,1,0:T(4,128)(2,1)S(1)}, bf16[3,4,256]{2,1,0:T(4,128)(2,1)S(1)}, u32[]{:S(2)}, u32[]{:S(2)}) collective-permute-start(bf16[3,4,256]{2,1,0:T(4,128)(2,1)S(1)} %squeeze.123), channel_id=1, source_target_pairs={{16,0},{48,8},{80,16},{112,24},{144,32},{176,40},{208,48},{240,56}... | collective-permute-start | bytes 18440 | tf_op jit(solution)/shard_map/ppermute | solution.py:210
  199.4 2.0 collective-permute-start.19
  201.5 6.1 %collective-permute-start.18 = (bf16[3,4,256]{2,1,0:T(4,128)(2,1)S(1)}, bf16[3,4,256]{2,1,0:T(4,128)(2,1)S(1)}, u32[]{:S(2)}, u32[]{:S(2)}) collective-permute-start(bf16[3,4,256]{2,1,0:T(4,128)(2,1)S(1)} %squeeze.121), channel_id=1, source_target_pairs={{0,0},{32,8},{64,16},{96,24},{128,32},{160,40},{192,48},{224,56},{... | collective-permute-start | bytes 18440 | tf_op jit(solution)/shard_map/ppermute | solution.py:210
  (161 shorter events, 28.3 us)
Async XLA Ops:
  7.2 46.0 %copy-start = (bf16[256,4096]{1,0:T(8,128)(2,1)S(1)}, bf16[256,4096]{1,0:T(8,128)(2,1)}, u32[]{:S(2)}) copy-start(bf16[256,4096]{1,0:T(8,128)(2,1)} %param.25) | copy-start | bytes 6291460
  7.2 119.6 %all-gather.6.cloned.1.call-start = ((), (), s32[]{:S(2)}) async-start(), calls=%async_computation.1 | async-start | bytes 3538944 | tf_op jit(solution)/shard_map/all_gather | solution.py:181
  9.4 4.7 %copy-start.3 = (bf16[4096,256]{1,0:T(8,128)(2,1)S(1)}, bf16[4096,256]{1,0:T(8,128)(2,1)}, u32[]{:S(2)}) copy-start(bf16[4096,256]{1,0:T(8,128)(2,1)} %param.23) | copy-start | bytes 6291460
  11.9 7.3 %copy-start.9 = (bf16[16,32,256]{2,1,0:T(8,128)(2,1)S(1)}, bf16[16,32,256]{2,1,0:T(8,128)(2,1)}, u32[]{:S(2)}) copy-start(bf16[16,32,256]{2,1,0:T(8,128)(2,1)} %param.32) | copy-start | bytes 786436
  11.9 7.3 %copy-start.10 = (bf16[16,32,256]{2,1,0:T(8,128)(2,1)S(1)}, bf16[16,32,256]{2,1,0:T(8,128)(2,1)}, u32[]{:S(2)}) copy-start(bf16[16,32,256]{2,1,0:T(8,128)(2,1)} %param.31) | copy-start | bytes 786436
  14.1 9.7 %copy-start.12 = (s32[3,512]{1,0:T(4,128)S(1)}, s32[3,512]{1,0:T(4,128)}, u32[]{:S(2)}) copy-start(s32[3,512]{1,0:T(4,128)} %param.33) | copy-start | bytes 18436
  14.6 21.1 %collective-permute-start.3 = (bf16[2,3,16,256]{3,2,0,1:T(8,128)(2,1)S(1)}, bf16[2,3,16,256]{3,2,0,1:T(8,128)(2,1)S(1)}, u32[]{:S(2)}, u32[]{:S(2)}) collective-permute-start(bf16[2,3,16,256]{3,2,0,1:T(8,128)(2,1)S(1)} %pad_maximum_fusion.4), channel_id=1, source_target_pairs={{64,0},{72,8},{80,16},{88,24},{96,32},{104,40},{112,48},{120,56},{... | collective-permute-start | bytes 147464 | tf_op jit(solution)/shard_map/ppermute | solution.py:34
  18.2 17.6 %collective-permute-start.4 = (bf16[2,3,16,256]{3,2,0,1:T(8,128)(2,1)S(1)}, bf16[2,3,16,256]{3,2,0,1:T(8,128)(2,1)S(1)}, u32[]{:S(2)}, u32[]{:S(2)}) collective-permute-start(bf16[2,3,16,256]{3,2,0,1:T(8,128)(2,1)S(1)} %pad_maximum_fusion.4), channel_id=1, source_target_pairs={{128,0},{136,8},{144,16},{152,24},{160,32},{168,40},{176,48},{184,... | collective-permute-start | bytes 147464 | tf_op jit(solution)/shard_map/ppermute | solution.py:34
  18.5 17.3 %collective-permute-start.5 = (bf16[2,3,16,256]{3,2,0,1:T(8,128)(2,1)S(1)}, bf16[2,3,16,256]{3,2,0,1:T(8,128)(2,1)S(1)}, u32[]{:S(2)}, u32[]{:S(2)}) collective-permute-start(bf16[2,3,16,256]{3,2,0,1:T(8,128)(2,1)S(1)} %pad_maximum_fusion.4), channel_id=1, source_target_pairs={{192,0},{200,8},{208,16},{216,24},{224,32},{232,40},{240,48},{248,... | collective-permute-start | bytes 147464 | tf_op jit(solution)/shard_map/ppermute | solution.py:34
  20.4 15.7 %collective-permute-start = (bf16[2,16,32,256]{3,1,2,0:T(8,128)(2,1)}, bf16[2,16,32,256]{3,1,2,0:T(8,128)(2,1)}, u32[]{:S(2)}, u32[]{:S(2)}) collective-permute-start(bf16[2,16,32,256]{3,1,2,0:T(8,128)(2,1)} %pad_maximum_fusion.2), channel_id=1, source_target_pairs={{64,0},{72,8},{80,16},{88,24},{96,32},{104,40},{112,48},{120,56},{... | collective-permute-start | bytes 1572872 | tf_op jit(solution)/shard_map/ppermute | solution.py:34
  22.3 13.7 %collective-permute-start.1 = (bf16[2,16,32,256]{3,1,2,0:T(8,128)(2,1)}, bf16[2,16,32,256]{3,1,2,0:T(8,128)(2,1)}, u32[]{:S(2)}, u32[]{:S(2)}) collective-permute-start(bf16[2,16,32,256]{3,1,2,0:T(8,128)(2,1)} %pad_maximum_fusion.2), channel_id=1, source_target_pairs={{128,0},{136,8},{144,16},{152,24},{160,32},{168,40},{176,48},{184,... | collective-permute-start | bytes 1572872 | tf_op jit(solution)/shard_map/ppermute | solution.py:34
  35.7 12.9 %collective-permute-start.2 = (bf16[2,16,32,256]{3,1,2,0:T(8,128)(2,1)}, bf16[2,16,32,256]{3,1,2,0:T(8,128)(2,1)S(1)}, u32[]{:S(2)}, u32[]{:S(2)}) collective-permute-start(bf16[2,16,32,256]{3,1,2,0:T(8,128)(2,1)} %pad_maximum_fusion.2), channel_id=1, source_target_pairs={{192,0},{200,8},{208,16},{216,24},{224,32},{232,40},{240,48},{248,... | collective-permute-start | bytes 1572872 | tf_op jit(solution)/shard_map/ppermute | solution.py:34
  52.2 3.0 %copy-start.6 = (bf16[768,512]{1,0:T(8,128)(2,1)S(1)}, bf16[768,512]{1,0:T(8,128)(2,1)}, u32[]{:S(2)}) copy-start(bf16[768,512]{1,0:T(8,128)(2,1)} %param.29) | copy-start | bytes 2359300
  54.4 74.8 %copy-start.1 = (bf16[3,16,4096]{2,1,0:T(8,128)(2,1)S(1)}, bf16[3,16,4096]{2,1,0:T(8,128)(2,1)}, u32[]{:S(2)}) copy-start(bf16[3,16,4096]{2,1,0:T(8,128)(2,1)} %param.18) | copy-start | bytes 1179652
  54.4 125.4 %all-gather.4.cloned.1.call-start = ((), (), s32[]{:S(2)}) async-start(), calls=%async_computation | async-start | bytes 4325376 | tf_op jit(solution)/shard_map/all_gather | solution.py:110
  55.2 25.8 %collective-permute-start.11 = (bf16[768,512]{1,0:T(8,128)(2,1)S(1)}, bf16[768,512]{1,0:T(8,128)(2,1)}, u32[]{:S(2)}, u32[]{:S(2)}) collective-permute-start(bf16[768,512]{1,0:T(8,128)(2,1)S(1)} %copy-done.6), channel_id=1, source_target_pairs={{0,7},{1,0},{2,1},{3,2},{4,3},{5,4},{6,5},{7,6},{8,15},{9,8},{10,9... | collective-permute-start | bytes 2359304 | tf_op jit(solution)/shard_map/ppermute | solution.py:55
  60.8 23.7 %collective-permute-start.10 = (bf16[768,512]{1,0:T(8,128)(2,1)S(1)}, bf16[768,512]{1,0:T(8,128)(2,1)}, u32[]{:S(2)}, u32[]{:S(2)}) collective-permute-start(bf16[768,512]{1,0:T(8,128)(2,1)S(1)} %copy-done.6), channel_id=1, source_target_pairs={{0,1},{1,2},{2,3},{3,4},{4,5},{5,6},{6,7},{7,0},{8,9},{9,10},{10,1... | collective-permute-start | bytes 2359304 | tf_op jit(solution)/shard_map/ppermute | solution.py:54
  81.0 36.4 %collective-permute-start.13 = (bf16[768,512]{1,0:T(8,128)(2,1)}, bf16[768,512]{1,0:T(8,128)(2,1)}, u32[]{:S(2)}, u32[]{:S(2)}) collective-permute-start(bf16[768,512]{1,0:T(8,128)(2,1)} %collective-permute-done.11), channel_id=1, source_target_pairs={{0,7},{1,0},{2,1},{3,2},{4,3},{5,4},{6,5},{7,6},{8,15},{9,8},{10,9... | collective-permute-start | bytes 2359304 | tf_op jit(solution)/shard_map/ppermute | solution.py:55
  84.5 36.3 %collective-permute-start.12 = (bf16[768,512]{1,0:T(8,128)(2,1)}, bf16[768,512]{1,0:T(8,128)(2,1)}, u32[]{:S(2)}, u32[]{:S(2)}) collective-permute-start(bf16[768,512]{1,0:T(8,128)(2,1)} %collective-permute-done.10), channel_id=1, source_target_pairs={{0,1},{1,2},{2,3},{3,4},{4,5},{5,6},{6,7},{7,0},{8,9},{9,10},{10,1... | collective-permute-start | bytes 2359304 | tf_op jit(solution)/shard_map/ppermute | solution.py:54
  117.3 25.9 %collective-permute-start.15 = (bf16[768,512]{1,0:T(8,128)(2,1)}, bf16[768,512]{1,0:T(8,128)(2,1)S(1)}, u32[]{:S(2)}, u32[]{:S(2)}) collective-permute-start(bf16[768,512]{1,0:T(8,128)(2,1)} %collective-permute-done.13), channel_id=1, source_target_pairs={{0,7},{1,0},{2,1},{3,2},{4,3},{5,4},{6,5},{7,6},{8,15},{9,8},{10,9... | collective-permute-start | bytes 2359304 | tf_op jit(solution)/shard_map/ppermute | solution.py:55
  120.7 29.9 %collective-permute-start.14 = (bf16[768,512]{1,0:T(8,128)(2,1)}, bf16[768,512]{1,0:T(8,128)(2,1)}, u32[]{:S(2)}, u32[]{:S(2)}) collective-permute-start(bf16[768,512]{1,0:T(8,128)(2,1)} %collective-permute-done.12), channel_id=1, source_target_pairs={{0,1},{1,2},{2,3},{3,4},{4,5},{5,6},{6,7},{7,0},{8,9},{9,10},{10,1... | collective-permute-start | bytes 2359304 | tf_op jit(solution)/shard_map/ppermute | solution.py:54
  131.3 24.0 %collective-permute-start.9 = (bf16[3,4,256]{2,1,0:T(4,128)(2,1)S(1)}, bf16[3,4,256]{2,1,0:T(4,128)(2,1)S(1)}, u32[]{:S(2)}, u32[]{:S(2)}) collective-permute-start(bf16[3,4,256]{2,1,0:T(4,128)(2,1)S(1)} %get-tuple-element.43), channel_id=1, source_target_pairs={{0,24},{8,56},{16,88},{24,120},{32,152},{40,184},{48,216},{56,248}... | collective-permute-start | bytes 18440 | tf_op jit(solution)/shard_map/ppermute | solution.py:198
  135.7 19.7 %collective-permute-start.8 = (bf16[3,4,256]{2,1,0:T(4,128)(2,1)S(1)}, bf16[3,4,256]{2,1,0:T(4,128)(2,1)S(1)}, u32[]{:S(2)}, u32[]{:S(2)}) collective-permute-start(bf16[3,4,256]{2,1,0:T(4,128)(2,1)S(1)} %get-tuple-element.44), channel_id=1, source_target_pairs={{0,16},{8,48},{16,80},{24,112},{32,144},{40,176},{48,208},{56,240}... | collective-permute-start | bytes 18440 | tf_op jit(solution)/shard_map/ppermute | solution.py:198
  140.0 15.4 %collective-permute-start.7 = (bf16[3,4,256]{2,1,0:T(4,128)(2,1)S(1)}, bf16[3,4,256]{2,1,0:T(4,128)(2,1)S(1)}, u32[]{:S(2)}, u32[]{:S(2)}) collective-permute-start(bf16[3,4,256]{2,1,0:T(4,128)(2,1)S(1)} %get-tuple-element.45), channel_id=1, source_target_pairs={{0,8},{8,40},{16,72},{24,104},{32,136},{40,168},{48,200},{56,232},... | collective-permute-start | bytes 18440 | tf_op jit(solution)/shard_map/ppermute | solution.py:198
  143.2 12.2 %collective-permute-start.6 = (bf16[3,4,256]{2,1,0:T(4,128)(2,1)S(1)}, bf16[3,4,256]{2,1,0:T(4,128)(2,1)S(1)}, u32[]{:S(2)}, u32[]{:S(2)}) collective-permute-start(bf16[3,4,256]{2,1,0:T(4,128)(2,1)S(1)} %get-tuple-element.42), channel_id=1, source_target_pairs={{0,0},{8,32},{16,64},{24,96},{32,128},{40,160},{48,192},{56,224},{... | collective-permute-start | bytes 18440 | tf_op jit(solution)/shard_map/ppermute | solution.py:198
  150.6 39.1 %collective-permute-start.17 = (bf16[384,512]{1,0:T(8,128)(2,1)}, bf16[384,512]{1,0:T(8,128)(2,1)S(1)}, u32[]{:S(2)}, u32[]{:S(2)}) collective-permute-start(bf16[384,512]{1,0:T(8,128)(2,1)} %slice.182), channel_id=1, source_target_pairs={{0,7},{1,0},{2,1},{3,2},{4,3},{5,4},{6,5},{7,6},{8,15},{9,8},{10,9... | collective-permute-start | bytes 1179656 | tf_op jit(solution)/shard_map/ppermute | solution.py:60
  155.4 34.4 %collective-permute-start.16 = (bf16[384,512]{1,0:T(8,128)(2,1)}, bf16[384,512]{1,0:T(8,128)(2,1)}, u32[]{:S(2)}, u32[]{:S(2)}) collective-permute-start(bf16[384,512]{1,0:T(8,128)(2,1)} %slice.181), channel_id=1, source_target_pairs={{0,1},{1,2},{2,3},{3,4},{4,5},{5,6},{6,7},{7,0},{8,9},{9,10},{10,1... | collective-permute-start | bytes 1179656 | tf_op jit(solution)/shard_map/ppermute | solution.py:59
  179.8 4.0 %copy-start.2 = (bf16[4096,512]{1,0:T(8,128)(2,1)S(1)}, bf16[4096,512]{1,0:T(8,128)(2,1)}, u32[]{:S(2)}) copy-start(bf16[4096,512]{1,0:T(8,128)(2,1)} %all-gather.4.cloned.1.call-done) | copy-start | bytes 12582916
  193.1 14.5 %collective-permute-start.21 = (bf16[3,4,256]{2,1,0:T(4,128)(2,1)S(1)}, bf16[3,4,256]{2,1,0:T(4,128)(2,1)S(1)}, u32[]{:S(2)}, u32[]{:S(2)}) collective-permute-start(bf16[3,4,256]{2,1,0:T(4,128)(2,1)S(1)} %squeeze.124), channel_id=1, source_target_pairs={{24,0},{56,8},{88,16},{120,24},{152,32},{184,40},{216,48},{248,56}... | collective-permute-start | bytes 18440 | tf_op jit(solution)/shard_map/ppermute | solution.py:210
  196.9 10.7 %collective-permute-start.20 = (bf16[3,4,256]{2,1,0:T(4,128)(2,1)S(1)}, bf16[3,4,256]{2,1,0:T(4,128)(2,1)S(1)}, u32[]{:S(2)}, u32[]{:S(2)}) collective-permute-start(bf16[3,4,256]{2,1,0:T(4,128)(2,1)S(1)} %squeeze.123), channel_id=1, source_target_pairs={{16,0},{48,8},{80,16},{112,24},{144,32},{176,40},{208,48},{240,56}... | collective-permute-start | bytes 18440 | tf_op jit(solution)/shard_map/ppermute | solution.py:210
  199.4 8.2 %collective-permute-start.19 = (bf16[3,4,256]{2,1,0:T(4,128)(2,1)S(1)}, bf16[3,4,256]{2,1,0:T(4,128)(2,1)S(1)}, u32[]{:S(2)}, u32[]{:S(2)}) collective-permute-start(bf16[3,4,256]{2,1,0:T(4,128)(2,1)S(1)} %squeeze.122), channel_id=1, source_target_pairs={{8,0},{40,8},{72,16},{104,24},{136,32},{168,40},{200,48},{232,56},... | collective-permute-start | bytes 18440 | tf_op jit(solution)/shard_map/ppermute | solution.py:210
  201.5 6.9 %collective-permute-start.18 = (bf16[3,4,256]{2,1,0:T(4,128)(2,1)S(1)}, bf16[3,4,256]{2,1,0:T(4,128)(2,1)S(1)}, u32[]{:S(2)}, u32[]{:S(2)}) collective-permute-start(bf16[3,4,256]{2,1,0:T(4,128)(2,1)S(1)} %squeeze.121), channel_id=1, source_target_pairs={{0,0},{32,8},{64,16},{96,24},{128,32},{160,40},{192,48},{224,56},{... | collective-permute-start | bytes 18440 | tf_op jit(solution)/shard_map/ppermute | solution.py:210
  (11 other events, 21.0 us)
Sparse Core Ops, SparseCore 0:
  54.5 72.2 all-gather.5
  129.3 50.4 all-gather.3

commit v4 on v3

--- a/solution.py
+++ b/solution.py
@@ -178,8 +178,10 @@
         contexts.append((summed / totals).astype(jnp.bfloat16))
     self_context = jnp.stack(contexts).reshape(steps * row_count, head_width)
     partial_out = jnp.dot(self_context, self_wo, preferred_element_type=jnp.float32)
-    every_part = lax.all_gather(partial_out.astype(jnp.bfloat16), "head", axis=0, tiled=False)
-    summed_out = jnp.sum(every_part.astype(jnp.float32), axis=0)
+    block_sum = lax.psum_scatter(
+        partial_out.astype(jnp.bfloat16), "head", scatter_dimension=1, tiled=True
+    )
+    summed_out = lax.all_gather(block_sum, "head", axis=1, tiled=True).astype(jnp.float32)
     residual = hidden_in + summed_out.reshape(hidden_in.shape)
     normed_cross = rms_scaled(residual, cross_gain).astype(jnp.bfloat16)
     cross_query = jnp.dot(

time: 220 us -> 191 us (0.87); the launches traced: 216 us -> 190 us
  waiting for transfers between devices: 96.6 us -> 41.6 us
  blocking collectives: 0 us -> 22.3 us
  starting transfers between devices: 56.5 us -> 63.2 us
    ppermute x3, waiting for transfers between devices: 52.3 us -> 14.4 us  [ring_project(): from_right = lax.ppermute(from_right, axis, left)]
    all_gather x1, waiting for transfers between devices: 24.3 us -> 0.01 us  [shards(): full_weights = lax.all_gather(cross_wkv, 'hyp', axis=0, tiled=True)]
    all_gather x0 -> x1, blocking collectives: none -> 22.3 us  [shards(): lax.all_gather(block_sum, 'head', axis=1, tiled=True).astype(jnp.float32)]
    reduce_scatter x0 -> x1, waiting for transfers between devices: none -> 11.8 us  [shards(): lax.psum_scatter(partial_out.astype(jnp.bfloat16), 'head', scatter_dimens...]
    all_gather x1 -> x0, waiting for transfers between devices: 6.04 us -> none  [shards(): lax.all_gather(partial_out.astype(jnp.bfloat16), 'head', axis=0, tiled=Fa...]
    ppermute x4, starting transfers between devices: 18.3 us -> 23.6 us  [shards(): sent.append(lax.ppermute(piece, 'hyp', route))]
    ppermute x4, starting transfers between devices: 14.4 us -> 19.2 us  [shards(): back.append(lax.ppermute(answer[shift], 'hyp', route))]
    ppermute x3, starting transfers between devices: 12.6 us -> 9.58 us  [ring_project(): from_right = lax.ppermute(from_right, axis, left)]
  transfers between devices with their start and end apart: 24 -> 24, of which waited for: 6 -> 5; matrix products, arithmetic and copies ran while one was open for 13% -> 15% of each run, Pallas kernels for 0% -> 0%
where the time goes in v4:
time: 191 us; the launch traced here: 190 us
  starting transfers between devices  63.2 us (33%)
  waiting for transfers between devices  41.6 us (22%)
  blocking collectives  22.3 us (12%)
  matrix products  21.6 us (11%)
  between operations  17 us (9%)
  other arithmetic  13.3 us (7%)
  local copies, waits for them, and re-layouts  11.1 us (6%)
    ppermute x4, starting transfers between devices, shards(): sent.append(lax.ppermute(piece, 'hyp', route))  23.6 us
    all_gather x1, blocking collectives, shards(): lax.all_gather(block_sum, 'head', axis=1, tiled=True).astype(jnp.float32)  22.3 us
    ppermute x4, starting transfers between devices, shards(): back.append(lax.ppermute(answer[shift], 'hyp', route))  19.2 us
    ppermute x3, waiting for transfers between devices, ring_project(): from_right = lax.ppermute(from_right, axis, left)  14.4 us
    ppermute x6, waiting for transfers between devices, beam_copies(): copies.append(lax.ppermute(block, 'hyp', route))  12.6 us
    dot_general x8, matrix products, partial(): return jnp.dot(piece, w, preferred_element_type=jnp.float32)  12.4 us
    reduce_scatter x1, waiting for transfers between devices, shards(): lax.psum_scatter(partial_out.astype(jnp.bfloat16), 'head', scatter_dimens...  11.8 us
    ppermute x3, starting transfers between devices, ring_project(): from_right = lax.ppermute(from_right, axis, left)  9.58 us
  transfers between devices with their start and end apart: 24, of which 5 were waited for; matrix products, arithmetic and copies ran while one was open for 15% of the time, Pallas kernels for 0%

profile of v4, /device:TPU:1, one launch (start us, length us, event | category | flops | bytes accessed | tf_op | source)
XLA Modules:
  0.0 190.2 jit_solution(11853109962258523196)
XLA Ops:
  10.2 1.3 multiply_reduce_fusion.1
  12.8 2.1 %convolution_convert_fusion.3 = bf16[48,256]{1,0:T(8,128)(2,1)S(1)} fusion(bf16[48,4096]{1,0:T(8,128)(2,1)S(1)} %bitcast.288, bf16[4096,256]{1,0:T(8,128)(2,1)} %param.24), kind=kOutput, calls=%fused_computation.14 | convolution fusion | flops 100675584 | bytes 2514944 | tf_op jit(solution)/shard_map/dot_general | solution.py:130
  15.4 3.6 %collective-permute-start.3 = (bf16[2,3,16,256]{3,2,0,1:T(8,128)(2,1)S(1)}, bf16[2,3,16,256]{3,2,0,1:T(8,128)(2,1)S(1)}, u32[]{:S(2)}, u32[]{:S(2)}) collective-permute-start(bf16[2,3,16,256]{3,2,0,1:T(8,128)(2,1)S(1)} %pad_maximum_fusion.4), channel_id=1, source_target_pairs={{64,0},{72,8},{80,16},{88,24},{96,32},{104,40},{112,48},{120,56},{... | collective-permute-start | bytes 147464 | tf_op jit(solution)/shard_map/ppermute | solution.py:34
  21.2 2.0 %collective-permute-start = (bf16[2,16,32,256]{3,1,2,0:T(8,128)(2,1)}, bf16[2,16,32,256]{3,1,2,0:T(8,128)(2,1)}, u32[]{:S(2)}, u32[]{:S(2)}) collective-permute-start(bf16[2,16,32,256]{3,1,2,0:T(8,128)(2,1)} %pad_maximum_fusion.2), channel_id=1, source_target_pairs={{64,0},{72,8},{80,16},{88,24},{96,32},{104,40},{112,48},{120,56},{... | collective-permute-start | bytes 1572872 | tf_op jit(solution)/shard_map/ppermute | solution.py:34
  23.2 1.4 collective-permute-start.1
  27.4 1.2 gather_fusion.5
  32.8 1.2 broadcast_compare_fusion.6
  35.5 2.1 %convolution_convert_fusion.5 = bf16[48,256]{1,0:T(8,128)(2,1)S(1)} fusion(bf16[48,4096]{1,0:T(8,128)(2,1)S(1)} %bitcast.290, bf16[4096,256]{1,0:T(8,128)(2,1)} %param.22), kind=kOutput, calls=%fused_computation.16 | convolution fusion | flops 100675584 | bytes 2514944 | tf_op jit(solution)/shard_map/dot_general | solution.py:128
  38.0 12.6 %collective-permute-done.2 = bf16[2,16,32,256]{3,1,2,0:T(8,128)(2,1)S(1)} collective-permute-done((bf16[2,16,32,256]{3,1,2,0:T(8,128)(2,1)}, bf16[2,16,32,256]{3,1,2,0:T(8,128)(2,1)S(1)}, u32[]{:S(2)}, u32[]{:S(2)}) %collective-permute-start.2) | collective-permute-done | bytes 524320 | tf_op jit(solution)/shard_map/ppermute | solution.py:34
  50.6 1.5 select_select_fusion.2
  55.1 1.2 convolution_convert_fusion
  57.0 5.7 %collective-permute-start.11 = (bf16[768,512]{1,0:T(8,128)(2,1)S(1)}, bf16[768,512]{1,0:T(8,128)(2,1)}, u32[]{:S(2)}, u32[]{:S(2)}) collective-permute-start(bf16[768,512]{1,0:T(8,128)(2,1)S(1)} %copy-done.6), channel_id=1, source_target_pairs={{0,7},{1,0},{2,1},{3,2},{4,3},{5,4},{6,5},{7,6},{8,15},{9,8},{10,9... | collective-permute-start | bytes 2359304 | tf_op jit(solution)/shard_map/ppermute | solution.py:55
  63.3 14.4 %collective-permute-done.11 = bf16[768,512]{1,0:T(8,128)(2,1)} collective-permute-done((bf16[768,512]{1,0:T(8,128)(2,1)S(1)}, bf16[768,512]{1,0:T(8,128)(2,1)}, u32[]{:S(2)}, u32[]{:S(2)}) %collective-permute-start.11) | collective-permute-done | bytes 786464 | tf_op jit(solution)/shard_map/ppermute | solution.py:55
  77.7 3.5 %collective-permute-start.13 = (bf16[768,512]{1,0:T(8,128)(2,1)}, bf16[768,512]{1,0:T(8,128)(2,1)}, u32[]{:S(2)}, u32[]{:S(2)}) collective-permute-start(bf16[768,512]{1,0:T(8,128)(2,1)} %collective-permute-done.11), channel_id=1, source_target_pairs={{0,7},{1,0},{2,1},{3,2},{4,3},{5,4},{6,5},{7,6},{8,15},{9,8},{10,9... | collective-permute-start | bytes 2359304 | tf_op jit(solution)/shard_map/ppermute | solution.py:55
  81.8 11.8 %reduce-scatter.2.cloned.1.call-done = bf16[48,512]{1,0:T(8,128)(2,1)} async-done(((bf16[48,4096]{1,0:T(8,128)(2,1)}), bf16[48,512]{1,0:T(8,128)(2,1)}) %reduce-scatter.2.cloned.1.call-update) | async-done | bytes 49168 | tf_op jit(solution)/shard_map/reduce_scatter | solution.py:181
  93.7 22.3 %all_gather.6 = bf16[48,4096]{1,0:T(8,128)(2,1)S(1)} all-gather(bf16[48,512]{1,0:T(8,128)(2,1)} %reduce-scatter.2.cloned.1.call-done), channel_id=1, replica_groups=mesh['hyp'=32,'head'=8] {'head'}, dimensions={1}, use_global_device_ids=true | all-gather | bytes 442368 | tf_op jit(solution)/shard_map/all_gather | solution.py:184
  118.5 4.6 %collective-permute-start.9 = (bf16[3,4,256]{2,1,0:T(4,128)(2,1)S(1)}, bf16[3,4,256]{2,1,0:T(4,128)(2,1)S(1)}, u32[]{:S(2)}, u32[]{:S(2)}) collective-permute-start(bf16[3,4,256]{2,1,0:T(4,128)(2,1)S(1)} %get-tuple-element.43), channel_id=1, source_target_pairs={{0,24},{8,56},{16,88},{24,120},{32,152},{40,184},{48,216},{56,248}... | collective-permute-start | bytes 18440 | tf_op jit(solution)/shard_map/ppermute | solution.py:200
  123.1 9.3 %collective-permute-start.8 = (bf16[3,4,256]{2,1,0:T(4,128)(2,1)S(1)}, bf16[3,4,256]{2,1,0:T(4,128)(2,1)S(1)}, u32[]{:S(2)}, u32[]{:S(2)}) collective-permute-start(bf16[3,4,256]{2,1,0:T(4,128)(2,1)S(1)} %get-tuple-element.44), channel_id=1, source_target_pairs={{0,16},{8,48},{16,80},{24,112},{32,144},{40,176},{48,208},{56,240}... | collective-permute-start | bytes 18440 | tf_op jit(solution)/shard_map/ppermute | solution.py:200
  132.4 4.2 %collective-permute-start.7 = (bf16[3,4,256]{2,1,0:T(4,128)(2,1)S(1)}, bf16[3,4,256]{2,1,0:T(4,128)(2,1)S(1)}, u32[]{:S(2)}, u32[]{:S(2)}) collective-permute-start(bf16[3,4,256]{2,1,0:T(4,128)(2,1)S(1)} %get-tuple-element.45), channel_id=1, source_target_pairs={{0,8},{8,40},{16,72},{24,104},{32,136},{40,168},{48,200},{56,232},... | collective-permute-start | bytes 18440 | tf_op jit(solution)/shard_map/ppermute | solution.py:200
  136.6 5.5 %collective-permute-start.6 = (bf16[3,4,256]{2,1,0:T(4,128)(2,1)S(1)}, bf16[3,4,256]{2,1,0:T(4,128)(2,1)S(1)}, u32[]{:S(2)}, u32[]{:S(2)}) collective-permute-start(bf16[3,4,256]{2,1,0:T(4,128)(2,1)S(1)} %get-tuple-element.42), channel_id=1, source_target_pairs={{0,0},{8,32},{16,64},{24,96},{32,128},{40,160},{48,192},{56,224},{... | collective-permute-start | bytes 18440 | tf_op jit(solution)/shard_map/ppermute | solution.py:200
  144.9 1.8 slice.181
  147.0 2.1 %fusion.11 = f32[512,768]{1,0:T(8,128)S(1)} fusion(bf16[768,512]{1,0:T(8,128)(2,1)} %collective-permute-done.14, bf16[4096,512]{1,0:T(8,128)(2,1)} %all-gather.2.cloned.1.call-done, s32[]{:T(128)S(6)} %select_n.409), kind=kOutput, calls=%fused_computation.35 | convolution fusion | flops 402653184 | bytes 2883588 | tf_op jit(solution)/shard_map/dot_general | solution.py:48
  149.1 1.9 %fusion.13 = f32[512,768]{1,0:T(8,128)S(1)} fusion(bf16[768,512]{1,0:T(8,128)(2,1)} %collective-permute-done.13, bf16[4096,512]{1,0:T(8,128)(2,1)} %all-gather.2.cloned.1.call-done, s32[]{:T(128)S(6)} %select_n.407), kind=kOutput, calls=%fused_computation.37 | convolution fusion | flops 402653184 | bytes 2883588 | tf_op jit(solution)/shard_map/dot_general | solution.py:48
  151.0 1.8 fusion.15
  152.8 1.8 fusion.17
  155.3 1.8 fusion.19
  157.1 1.6 fusion.2
  160.3 9.5 %collective-permute-start.21 = (bf16[3,4,256]{2,1,0:T(4,128)(2,1)S(1)}, bf16[3,4,256]{2,1,0:T(4,128)(2,1)S(1)}, u32[]{:S(2)}, u32[]{:S(2)}) collective-permute-start(bf16[3,4,256]{2,1,0:T(4,128)(2,1)S(1)} %squeeze.124), channel_id=1, source_target_pairs={{24,0},{56,8},{88,16},{120,24},{152,32},{184,40},{216,48},{248,56}... | collective-permute-start | bytes 18440 | tf_op jit(solution)/shard_map/ppermute | solution.py:212
  169.9 3.0 %collective-permute-start.20 = (bf16[3,4,256]{2,1,0:T(4,128)(2,1)S(1)}, bf16[3,4,256]{2,1,0:T(4,128)(2,1)S(1)}, u32[]{:S(2)}, u32[]{:S(2)}) collective-permute-start(bf16[3,4,256]{2,1,0:T(4,128)(2,1)S(1)} %squeeze.123), channel_id=1, source_target_pairs={{16,0},{48,8},{80,16},{112,24},{144,32},{176,40},{208,48},{240,56}... | collective-permute-start | bytes 18440 | tf_op jit(solution)/shard_map/ppermute | solution.py:212
  172.9 1.9 %collective-permute-start.19 = (bf16[3,4,256]{2,1,0:T(4,128)(2,1)S(1)}, bf16[3,4,256]{2,1,0:T(4,128)(2,1)S(1)}, u32[]{:S(2)}, u32[]{:S(2)}) collective-permute-start(bf16[3,4,256]{2,1,0:T(4,128)(2,1)S(1)} %squeeze.122), channel_id=1, source_target_pairs={{8,0},{40,8},{72,16},{104,24},{136,32},{168,40},{200,48},{232,56},... | collective-permute-start | bytes 18440 | tf_op jit(solution)/shard_map/ppermute | solution.py:212
  174.8 4.7 %collective-permute-start.18 = (bf16[3,4,256]{2,1,0:T(4,128)(2,1)S(1)}, bf16[3,4,256]{2,1,0:T(4,128)(2,1)S(1)}, u32[]{:S(2)}, u32[]{:S(2)}) collective-permute-start(bf16[3,4,256]{2,1,0:T(4,128)(2,1)S(1)} %squeeze.121), channel_id=1, source_target_pairs={{0,0},{32,8},{64,16},{96,24},{128,32},{160,40},{192,48},{224,56},{... | collective-permute-start | bytes 18440 | tf_op jit(solution)/shard_map/ppermute | solution.py:212
  179.7 1.6 collective-permute-done.18
  (159 shorter events, 28.1 us)
Async XLA Ops:
  8.0 47.1 %copy-start = (bf16[256,4096]{1,0:T(8,128)(2,1)S(1)}, bf16[256,4096]{1,0:T(8,128)(2,1)}, u32[]{:S(2)}) copy-start(bf16[256,4096]{1,0:T(8,128)(2,1)} %param.25) | copy-start | bytes 6291460
  8.0 85.6 %reduce-scatter.2.cloned.1.call-start = ((), (), s32[]{:S(2)}) async-start(), calls=%async_computation.1 | async-start | bytes 442368 | tf_op jit(solution)/shard_map/reduce_scatter | solution.py:181
  10.2 4.7 %copy-start.3 = (bf16[4096,256]{1,0:T(8,128)(2,1)S(1)}, bf16[4096,256]{1,0:T(8,128)(2,1)}, u32[]{:S(2)}) copy-start(bf16[4096,256]{1,0:T(8,128)(2,1)} %param.23) | copy-start | bytes 6291460
  12.7 7.3 %copy-start.9 = (bf16[16,32,256]{2,1,0:T(8,128)(2,1)S(1)}, bf16[16,32,256]{2,1,0:T(8,128)(2,1)}, u32[]{:S(2)}) copy-start(bf16[16,32,256]{2,1,0:T(8,128)(2,1)} %param.32) | copy-start | bytes 786436
  12.7 7.3 %copy-start.10 = (bf16[16,32,256]{2,1,0:T(8,128)(2,1)S(1)}, bf16[16,32,256]{2,1,0:T(8,128)(2,1)}, u32[]{:S(2)}) copy-start(bf16[16,32,256]{2,1,0:T(8,128)(2,1)} %param.31) | copy-start | bytes 786436
  14.9 9.7 %copy-start.12 = (s32[3,512]{1,0:T(4,128)S(1)}, s32[3,512]{1,0:T(4,128)}, u32[]{:S(2)}) copy-start(s32[3,512]{1,0:T(4,128)} %param.33) | copy-start | bytes 18436
  15.4 22.3 %collective-permute-start.3 = (bf16[2,3,16,256]{3,2,0,1:T(8,128)(2,1)S(1)}, bf16[2,3,16,256]{3,2,0,1:T(8,128)(2,1)S(1)}, u32[]{:S(2)}, u32[]{:S(2)}) collective-permute-start(bf16[2,3,16,256]{3,2,0,1:T(8,128)(2,1)S(1)} %pad_maximum_fusion.4), channel_id=1, source_target_pairs={{64,0},{72,8},{80,16},{88,24},{96,32},{104,40},{112,48},{120,56},{... | collective-permute-start | bytes 147464 | tf_op jit(solution)/shard_map/ppermute | solution.py:34
  19.0 18.7 %collective-permute-start.4 = (bf16[2,3,16,256]{3,2,0,1:T(8,128)(2,1)S(1)}, bf16[2,3,16,256]{3,2,0,1:T(8,128)(2,1)S(1)}, u32[]{:S(2)}, u32[]{:S(2)}) collective-permute-start(bf16[2,3,16,256]{3,2,0,1:T(8,128)(2,1)S(1)} %pad_maximum_fusion.4), channel_id=1, source_target_pairs={{128,0},{136,8},{144,16},{152,24},{160,32},{168,40},{176,48},{184,... | collective-permute-start | bytes 147464 | tf_op jit(solution)/shard_map/ppermute | solution.py:34
  19.4 18.4 %collective-permute-start.5 = (bf16[2,3,16,256]{3,2,0,1:T(8,128)(2,1)S(1)}, bf16[2,3,16,256]{3,2,0,1:T(8,128)(2,1)S(1)}, u32[]{:S(2)}, u32[]{:S(2)}) collective-permute-start(bf16[2,3,16,256]{3,2,0,1:T(8,128)(2,1)S(1)} %pad_maximum_fusion.4), channel_id=1, source_target_pairs={{192,0},{200,8},{208,16},{216,24},{224,32},{232,40},{240,48},{248,... | collective-permute-start | bytes 147464 | tf_op jit(solution)/shard_map/ppermute | solution.py:34
  21.2 16.8 %collective-permute-start = (bf16[2,16,32,256]{3,1,2,0:T(8,128)(2,1)}, bf16[2,16,32,256]{3,1,2,0:T(8,128)(2,1)}, u32[]{:S(2)}, u32[]{:S(2)}) collective-permute-start(bf16[2,16,32,256]{3,1,2,0:T(8,128)(2,1)} %pad_maximum_fusion.2), channel_id=1, source_target_pairs={{64,0},{72,8},{80,16},{88,24},{96,32},{104,40},{112,48},{120,56},{... | collective-permute-start | bytes 1572872 | tf_op jit(solution)/shard_map/ppermute | solution.py:34
  23.2 14.8 %collective-permute-start.1 = (bf16[2,16,32,256]{3,1,2,0:T(8,128)(2,1)}, bf16[2,16,32,256]{3,1,2,0:T(8,128)(2,1)}, u32[]{:S(2)}, u32[]{:S(2)}) collective-permute-start(bf16[2,16,32,256]{3,1,2,0:T(8,128)(2,1)} %pad_maximum_fusion.2), channel_id=1, source_target_pairs={{128,0},{136,8},{144,16},{152,24},{160,32},{168,40},{176,48},{184,... | collective-permute-start | bytes 1572872 | tf_op jit(solution)/shard_map/ppermute | solution.py:34
  37.7 12.9 %collective-permute-start.2 = (bf16[2,16,32,256]{3,1,2,0:T(8,128)(2,1)}, bf16[2,16,32,256]{3,1,2,0:T(8,128)(2,1)S(1)}, u32[]{:S(2)}, u32[]{:S(2)}) collective-permute-start(bf16[2,16,32,256]{3,1,2,0:T(8,128)(2,1)} %pad_maximum_fusion.2), channel_id=1, source_target_pairs={{192,0},{200,8},{208,16},{216,24},{224,32},{232,40},{240,48},{248,... | collective-permute-start | bytes 1572872 | tf_op jit(solution)/shard_map/ppermute | solution.py:34
  54.7 61.3 %copy-start.1 = (bf16[3,16,4096]{2,1,0:T(8,128)(2,1)S(1)}, bf16[3,16,4096]{2,1,0:T(8,128)(2,1)}, u32[]{:S(2)}) copy-start(bf16[3,16,4096]{2,1,0:T(8,128)(2,1)} %param.18) | copy-start | bytes 1179652
  55.1 62.7 %copy-start.11 = (f32[4096]{0:T(1024)S(1)}, f32[4096]{0:T(1024)}, u32[]{:S(2)}) copy-start(f32[4096]{0:T(1024)} %param.26) | copy-start | bytes 49156
  56.4 90.6 %all-gather.2.cloned.1.call-start = ((), (), s32[]{:S(2)}) async-start(), calls=%async_computation.2 | async-start | bytes 4325376 | tf_op jit(solution)/shard_map/all_gather | solution.py:110
  57.0 20.7 %collective-permute-start.11 = (bf16[768,512]{1,0:T(8,128)(2,1)S(1)}, bf16[768,512]{1,0:T(8,128)(2,1)}, u32[]{:S(2)}, u32[]{:S(2)}) collective-permute-start(bf16[768,512]{1,0:T(8,128)(2,1)S(1)} %copy-done.6), channel_id=1, source_target_pairs={{0,7},{1,0},{2,1},{3,2},{4,3},{5,4},{6,5},{7,6},{8,15},{9,8},{10,9... | collective-permute-start | bytes 2359304 | tf_op jit(solution)/shard_map/ppermute | solution.py:55
  62.6 18.5 %collective-permute-start.10 = (bf16[768,512]{1,0:T(8,128)(2,1)S(1)}, bf16[768,512]{1,0:T(8,128)(2,1)}, u32[]{:S(2)}, u32[]{:S(2)}) collective-permute-start(bf16[768,512]{1,0:T(8,128)(2,1)S(1)} %copy-done.6), channel_id=1, source_target_pairs={{0,1},{1,2},{2,3},{3,4},{4,5},{5,6},{6,7},{7,0},{8,9},{9,10},{10,1... | collective-permute-start | bytes 2359304 | tf_op jit(solution)/shard_map/ppermute | solution.py:54
  77.7 38.6 %collective-permute-start.13 = (bf16[768,512]{1,0:T(8,128)(2,1)}, bf16[768,512]{1,0:T(8,128)(2,1)}, u32[]{:S(2)}, u32[]{:S(2)}) collective-permute-start(bf16[768,512]{1,0:T(8,128)(2,1)} %collective-permute-done.11), channel_id=1, source_target_pairs={{0,7},{1,0},{2,1},{3,2},{4,3},{5,4},{6,5},{7,6},{8,15},{9,8},{10,9... | collective-permute-start | bytes 2359304 | tf_op jit(solution)/shard_map/ppermute | solution.py:55
  81.2 35.5 %collective-permute-start.12 = (bf16[768,512]{1,0:T(8,128)(2,1)}, bf16[768,512]{1,0:T(8,128)(2,1)}, u32[]{:S(2)}, u32[]{:S(2)}) collective-permute-start(bf16[768,512]{1,0:T(8,128)(2,1)} %collective-permute-done.10), channel_id=1, source_target_pairs={{0,1},{1,2},{2,3},{3,4},{4,5},{5,6},{6,7},{7,0},{8,9},{9,10},{10,1... | collective-permute-start | bytes 2359304 | tf_op jit(solution)/shard_map/ppermute | solution.py:54
  93.7 24.3 %copy-start.4 = (bf16[4096,256]{1,0:T(8,128)(2,1)S(1)}, bf16[4096,256]{1,0:T(8,128)(2,1)}, u32[]{:S(2)}) copy-start(bf16[4096,256]{1,0:T(8,128)(2,1)} %param.27) | copy-start | bytes 6291460
  116.2 26.7 %collective-permute-start.15 = (bf16[768,512]{1,0:T(8,128)(2,1)}, bf16[768,512]{1,0:T(8,128)(2,1)S(1)}, u32[]{:S(2)}, u32[]{:S(2)}) collective-permute-start(bf16[768,512]{1,0:T(8,128)(2,1)} %collective-permute-done.13), channel_id=1, source_target_pairs={{0,7},{1,0},{2,1},{3,2},{4,3},{5,4},{6,5},{7,6},{8,15},{9,8},{10,9... | collective-permute-start | bytes 2359304 | tf_op jit(solution)/shard_map/ppermute | solution.py:55
  116.6 28.3 %collective-permute-start.14 = (bf16[768,512]{1,0:T(8,128)(2,1)}, bf16[768,512]{1,0:T(8,128)(2,1)}, u32[]{:S(2)}, u32[]{:S(2)}) collective-permute-start(bf16[768,512]{1,0:T(8,128)(2,1)} %collective-permute-done.12), channel_id=1, source_target_pairs={{0,1},{1,2},{2,3},{3,4},{4,5},{5,6},{6,7},{7,0},{8,9},{9,10},{10,1... | collective-permute-start | bytes 2359304 | tf_op jit(solution)/shard_map/ppermute | solution.py:54
  118.5 18.1 %collective-permute-start.9 = (bf16[3,4,256]{2,1,0:T(4,128)(2,1)S(1)}, bf16[3,4,256]{2,1,0:T(4,128)(2,1)S(1)}, u32[]{:S(2)}, u32[]{:S(2)}) collective-permute-start(bf16[3,4,256]{2,1,0:T(4,128)(2,1)S(1)} %get-tuple-element.43), channel_id=1, source_target_pairs={{0,24},{8,56},{16,88},{24,120},{32,152},{40,184},{48,216},{56,248}... | collective-permute-start | bytes 18440 | tf_op jit(solution)/shard_map/ppermute | solution.py:200
  123.1 19.2 %collective-permute-start.8 = (bf16[3,4,256]{2,1,0:T(4,128)(2,1)S(1)}, bf16[3,4,256]{2,1,0:T(4,128)(2,1)S(1)}, u32[]{:S(2)}, u32[]{:S(2)}) collective-permute-start(bf16[3,4,256]{2,1,0:T(4,128)(2,1)S(1)} %get-tuple-element.44), channel_id=1, source_target_pairs={{0,16},{8,48},{16,80},{24,112},{32,144},{40,176},{48,208},{56,240}... | collective-permute-start | bytes 18440 | tf_op jit(solution)/shard_map/ppermute | solution.py:200
  132.4 9.9 %collective-permute-start.7 = (bf16[3,4,256]{2,1,0:T(4,128)(2,1)S(1)}, bf16[3,4,256]{2,1,0:T(4,128)(2,1)S(1)}, u32[]{:S(2)}, u32[]{:S(2)}) collective-permute-start(bf16[3,4,256]{2,1,0:T(4,128)(2,1)S(1)} %get-tuple-element.45), channel_id=1, source_target_pairs={{0,8},{8,40},{16,72},{24,104},{32,136},{40,168},{48,200},{56,232},... | collective-permute-start | bytes 18440 | tf_op jit(solution)/shard_map/ppermute | solution.py:200
  136.6 6.3 %collective-permute-start.6 = (bf16[3,4,256]{2,1,0:T(4,128)(2,1)S(1)}, bf16[3,4,256]{2,1,0:T(4,128)(2,1)S(1)}, u32[]{:S(2)}, u32[]{:S(2)}) collective-permute-start(bf16[3,4,256]{2,1,0:T(4,128)(2,1)S(1)} %get-tuple-element.42), channel_id=1, source_target_pairs={{0,0},{8,32},{16,64},{24,96},{32,128},{40,160},{48,192},{56,224},{... | collective-permute-start | bytes 18440 | tf_op jit(solution)/shard_map/ppermute | solution.py:200
  143.8 13.3 %collective-permute-start.17 = (bf16[384,512]{1,0:T(8,128)(2,1)}, bf16[384,512]{1,0:T(8,128)(2,1)S(1)}, u32[]{:S(2)}, u32[]{:S(2)}) collective-permute-start(bf16[384,512]{1,0:T(8,128)(2,1)} %slice.182), channel_id=1, source_target_pairs={{0,7},{1,0},{2,1},{3,2},{4,3},{5,4},{6,5},{7,6},{8,15},{9,8},{10,9... | collective-permute-start | bytes 1179656 | tf_op jit(solution)/shard_map/ppermute | solution.py:60
  146.7 10.4 %collective-permute-start.16 = (bf16[384,512]{1,0:T(8,128)(2,1)}, bf16[384,512]{1,0:T(8,128)(2,1)}, u32[]{:S(2)}, u32[]{:S(2)}) collective-permute-start(bf16[384,512]{1,0:T(8,128)(2,1)} %slice.181), channel_id=1, source_target_pairs={{0,1},{1,2},{2,3},{3,4},{4,5},{5,6},{6,7},{7,0},{8,9},{9,10},{10,1... | collective-permute-start | bytes 1179656 | tf_op jit(solution)/shard_map/ppermute | solution.py:59
  160.3 19.3 %collective-permute-start.21 = (bf16[3,4,256]{2,1,0:T(4,128)(2,1)S(1)}, bf16[3,4,256]{2,1,0:T(4,128)(2,1)S(1)}, u32[]{:S(2)}, u32[]{:S(2)}) collective-permute-start(bf16[3,4,256]{2,1,0:T(4,128)(2,1)S(1)} %squeeze.124), channel_id=1, source_target_pairs={{24,0},{56,8},{88,16},{120,24},{152,32},{184,40},{216,48},{248,56}... | collective-permute-start | bytes 18440 | tf_op jit(solution)/shard_map/ppermute | solution.py:212
  169.9 9.7 %collective-permute-start.20 = (bf16[3,4,256]{2,1,0:T(4,128)(2,1)S(1)}, bf16[3,4,256]{2,1,0:T(4,128)(2,1)S(1)}, u32[]{:S(2)}, u32[]{:S(2)}) collective-permute-start(bf16[3,4,256]{2,1,0:T(4,128)(2,1)S(1)} %squeeze.123), channel_id=1, source_target_pairs={{16,0},{48,8},{80,16},{112,24},{144,32},{176,40},{208,48},{240,56}... | collective-permute-start | bytes 18440 | tf_op jit(solution)/shard_map/ppermute | solution.py:212
  172.9 6.7 %collective-permute-start.19 = (bf16[3,4,256]{2,1,0:T(4,128)(2,1)S(1)}, bf16[3,4,256]{2,1,0:T(4,128)(2,1)S(1)}, u32[]{:S(2)}, u32[]{:S(2)}) collective-permute-start(bf16[3,4,256]{2,1,0:T(4,128)(2,1)S(1)} %squeeze.122), channel_id=1, source_target_pairs={{8,0},{40,8},{72,16},{104,24},{136,32},{168,40},{200,48},{232,56},... | collective-permute-start | bytes 18440 | tf_op jit(solution)/shard_map/ppermute | solution.py:212
  174.8 6.5 %collective-permute-start.18 = (bf16[3,4,256]{2,1,0:T(4,128)(2,1)S(1)}, bf16[3,4,256]{2,1,0:T(4,128)(2,1)S(1)}, u32[]{:S(2)}, u32[]{:S(2)}) collective-permute-start(bf16[3,4,256]{2,1,0:T(4,128)(2,1)S(1)} %squeeze.121), channel_id=1, source_target_pairs={{0,0},{32,8},{64,16},{96,24},{128,32},{160,40},{192,48},{224,56},{... | collective-permute-start | bytes 18440 | tf_op jit(solution)/shard_map/ppermute | solution.py:212
  (10 other events, 23.8 us)
Sparse Core Ops, SparseCore 0:
  56.5 37.0 reduce-scatter.1
Sparse Core Ops, SparseCore 1:
  59.4 54.1 all-gather.1

commit v5 on v3

--- a/solution.py
+++ b/solution.py
@@ -124,10 +124,14 @@
     lang_rows = jnp.dot(one_hot, lang_table, preferred_element_type=jnp.float32)
 
     hidden_in = step_embeds.astype(jnp.float32) + lang_rows[None]
-    normed = rms_scaled(hidden_in, self_gain).astype(jnp.bfloat16).reshape(steps * row_count, -1)
-    new_query = jnp.dot(normed, self_wq, preferred_element_type=jnp.float32).astype(jnp.bfloat16)
-    new_key = jnp.dot(normed, self_wk, preferred_element_type=jnp.float32).astype(jnp.bfloat16)
-    new_value = jnp.dot(normed, self_wv, preferred_element_type=jnp.float32).astype(jnp.bfloat16)
+    normed = rms_scaled(hidden_in, self_gain).astype(jnp.bfloat16)
+    normed = normed.reshape(steps * row_count, -1)
+    new_query = jnp.dot(normed, self_wq, preferred_element_type=jnp.float32)
+    new_key = jnp.dot(normed, self_wk, preferred_element_type=jnp.float32)
+    new_value = jnp.dot(normed, self_wv, preferred_element_type=jnp.float32)
+    new_query = new_query.astype(jnp.bfloat16)
+    new_key = new_key.astype(jnp.bfloat16)
+    new_value = new_value.astype(jnp.bfloat16)
     new_query = new_query.reshape(steps, row_count, head_width)
     fresh = jnp.stack([new_key, new_value]).reshape(2, steps, row_count, head_width)
     fresh_all = beam_copies(fresh, hyp_count, group_size)

time: 220 us -> 220 us (level)
  no operation moved by 1% of the time
where the time goes in v5:
time: 220 us; the launch traced here: 216 us
  waiting for transfers between devices  96.6 us (44%)
  starting transfers between devices  56.5 us (26%)
  matrix products  21.6 us (10%)
  between operations  15.6 us (7%)
  other arithmetic  14 us (6%)
  local copies, waits for them, and re-layouts  12.1 us (6%)
    ppermute x3, waiting for transfers between devices, ring_project(): from_right = lax.ppermute(from_right, axis, left)  52.3 us
    all_gather x1, waiting for transfers between devices, shards(): full_weights = lax.all_gather(cross_wkv, 'hyp', axis=0, tiled=True)  24.3 us
    ppermute x4, starting transfers between devices, shards(): sent.append(lax.ppermute(piece, 'hyp', route))  18.3 us
    ppermute x4, starting transfers between devices, shards(): back.append(lax.ppermute(answer[shift], 'hyp', route))  14.4 us
    ppermute x3, starting transfers between devices, ring_project(): from_right = lax.ppermute(from_right, axis, left)  12.6 us
    ppermute x6, waiting for transfers between devices, beam_copies(): copies.append(lax.ppermute(block, 'hyp', route))  12.6 us
    dot_general x8, matrix products, partial(): return jnp.dot(piece, w, preferred_element_type=jnp.float32)  12.4 us
    ppermute x6, starting transfers between devices, beam_copies(): copies.append(lax.ppermute(block, 'hyp', route))  8.15 us
  transfers between devices with their start and end apart: 24, of which 6 were waited for; matrix products, arithmetic and copies ran while one was open for 13% of the time, Pallas kernels for 0%

profile of v5, /device:TPU:1, one launch (start us, length us, event | category | flops | bytes accessed | tf_op | source)
XLA Modules:
  0.0 216.5 jit_solution(8226138228956062717)
XLA Ops:
  9.4 1.3 multiply_reduce_fusion.1
  11.9 2.1 convolution_convert_fusion.3
  14.6 3.6 %collective-permute-start.3 = (bf16[2,3,16,256]{3,2,0,1:T(8,128)(2,1)S(1)}, bf16[2,3,16,256]{3,2,0,1:T(8,128)(2,1)S(1)}, u32[]{:S(2)}, u32[]{:S(2)}) collective-permute-start(bf16[2,3,16,256]{3,2,0,1:T(8,128)(2,1)S(1)} %pad_maximum_fusion.4), channel_id=1, source_target_pairs={{64,0},{72,8},{80,16},{88,24},{96,32},{104,40},{112,48},{120,56},{... | collective-permute-start | bytes 147464 | tf_op jit(solution)/shard_map/ppermute | solution.py:34
  20.4 2.0 collective-permute-start
  22.3 1.4 collective-permute-start.1
  33.6 2.1 convolution_convert_fusion.5
  36.0 12.5 %collective-permute-done.2 = bf16[2,16,32,256]{3,1,2,0:T(8,128)(2,1)S(1)} collective-permute-done((bf16[2,16,32,256]{3,1,2,0:T(8,128)(2,1)}, bf16[2,16,32,256]{3,1,2,0:T(8,128)(2,1)S(1)}, u32[]{:S(2)}, u32[]{:S(2)}) %collective-permute-start.2) | collective-permute-done | bytes 524320 | tf_op jit(solution)/shard_map/ppermute | solution.py:34
  48.6 1.5 select_select_fusion.2
  55.2 5.7 %collective-permute-start.11 = (bf16[768,512]{1,0:T(8,128)(2,1)S(1)}, bf16[768,512]{1,0:T(8,128)(2,1)}, u32[]{:S(2)}, u32[]{:S(2)}) collective-permute-start(bf16[768,512]{1,0:T(8,128)(2,1)S(1)} %copy-done.6), channel_id=1, source_target_pairs={{0,7},{1,0},{2,1},{3,2},{4,3},{5,4},{6,5},{7,6},{8,15},{9,8},{10,9... | collective-permute-start | bytes 2359304 | tf_op jit(solution)/shard_map/ppermute | solution.py:55
  60.8 20.1 %collective-permute-done.11 = bf16[768,512]{1,0:T(8,128)(2,1)} collective-permute-done((bf16[768,512]{1,0:T(8,128)(2,1)S(1)}, bf16[768,512]{1,0:T(8,128)(2,1)}, u32[]{:S(2)}, u32[]{:S(2)}) %collective-permute-start.11) | collective-permute-done | bytes 786464 | tf_op jit(solution)/shard_map/ppermute | solution.py:55
  81.0 3.5 %collective-permute-start.13 = (bf16[768,512]{1,0:T(8,128)(2,1)}, bf16[768,512]{1,0:T(8,128)(2,1)}, u32[]{:S(2)}, u32[]{:S(2)}) collective-permute-start(bf16[768,512]{1,0:T(8,128)(2,1)} %collective-permute-done.11), channel_id=1, source_target_pairs={{0,7},{1,0},{2,1},{3,2},{4,3},{5,4},{6,5},{7,6},{8,15},{9,8},{10,9... | collective-permute-start | bytes 2359304 | tf_op jit(solution)/shard_map/ppermute | solution.py:55
  85.2 32.1 %collective-permute-done.13 = bf16[768,512]{1,0:T(8,128)(2,1)} collective-permute-done((bf16[768,512]{1,0:T(8,128)(2,1)}, bf16[768,512]{1,0:T(8,128)(2,1)}, u32[]{:S(2)}, u32[]{:S(2)}) %collective-permute-start.13) | collective-permute-done | bytes 786464 | tf_op jit(solution)/shard_map/ppermute | solution.py:55
  117.3 3.4 %collective-permute-start.15 = (bf16[768,512]{1,0:T(8,128)(2,1)}, bf16[768,512]{1,0:T(8,128)(2,1)S(1)}, u32[]{:S(2)}, u32[]{:S(2)}) collective-permute-start(bf16[768,512]{1,0:T(8,128)(2,1)} %collective-permute-done.13), channel_id=1, source_target_pairs={{0,7},{1,0},{2,1},{3,2},{4,3},{5,4},{6,5},{7,6},{8,15},{9,8},{10,9... | collective-permute-start | bytes 2359304 | tf_op jit(solution)/shard_map/ppermute | solution.py:55
  120.7 6.0 %all-gather.6.cloned.1.call-done = bf16[384,4096]{1,0:T(8,128)(2,1)} async-done(((bf16[48,4096]{1,0:T(8,128)(2,1)}), bf16[384,4096]{1,0:T(8,128)(2,1)}) %all-gather.6.cloned.1.call-update) | async-done | bytes 3145744 | tf_op jit(solution)/shard_map/all_gather | solution.py:185
  126.8 2.4 %convert_reduce_fusion = f32[48,4096]{1,0:T(8,128)S(1)} fusion(bf16[8,48,4096]{2,1,0:T(8,128)(2,1)} %bitcast.294), kind=kLoop, calls=%fused_computation.7 | loop fusion | flops 2949120 | bytes 3932160 | tf_op jit(solution)/shard_map/reduce_sum | solution.py:186
  131.3 4.3 %collective-permute-start.9 = (bf16[3,4,256]{2,1,0:T(4,128)(2,1)S(1)}, bf16[3,4,256]{2,1,0:T(4,128)(2,1)S(1)}, u32[]{:S(2)}, u32[]{:S(2)}) collective-permute-start(bf16[3,4,256]{2,1,0:T(4,128)(2,1)S(1)} %get-tuple-element.43), channel_id=1, source_target_pairs={{0,24},{8,56},{16,88},{24,120},{32,152},{40,184},{48,216},{56,248}... | collective-permute-start | bytes 18440 | tf_op jit(solution)/shard_map/ppermute | solution.py:202
  135.7 4.3 %collective-permute-start.8 = (bf16[3,4,256]{2,1,0:T(4,128)(2,1)S(1)}, bf16[3,4,256]{2,1,0:T(4,128)(2,1)S(1)}, u32[]{:S(2)}, u32[]{:S(2)}) collective-permute-start(bf16[3,4,256]{2,1,0:T(4,128)(2,1)S(1)} %get-tuple-element.44), channel_id=1, source_target_pairs={{0,16},{8,48},{16,80},{24,112},{32,144},{40,176},{48,208},{56,240}... | collective-permute-start | bytes 18440 | tf_op jit(solution)/shard_map/ppermute | solution.py:202
  140.0 3.2 %collective-permute-start.7 = (bf16[3,4,256]{2,1,0:T(4,128)(2,1)S(1)}, bf16[3,4,256]{2,1,0:T(4,128)(2,1)S(1)}, u32[]{:S(2)}, u32[]{:S(2)}) collective-permute-start(bf16[3,4,256]{2,1,0:T(4,128)(2,1)S(1)} %get-tuple-element.45), channel_id=1, source_target_pairs={{0,8},{8,40},{16,72},{24,104},{32,136},{40,168},{48,200},{56,232},... | collective-permute-start | bytes 18440 | tf_op jit(solution)/shard_map/ppermute | solution.py:202
  143.2 6.5 %collective-permute-start.6 = (bf16[3,4,256]{2,1,0:T(4,128)(2,1)S(1)}, bf16[3,4,256]{2,1,0:T(4,128)(2,1)S(1)}, u32[]{:S(2)}, u32[]{:S(2)}) collective-permute-start(bf16[3,4,256]{2,1,0:T(4,128)(2,1)S(1)} %get-tuple-element.42), channel_id=1, source_target_pairs={{0,0},{8,32},{16,64},{24,96},{32,128},{40,160},{48,192},{56,224},{... | collective-permute-start | bytes 18440 | tf_op jit(solution)/shard_map/ppermute | solution.py:202
  150.6 2.9 %collective-permute-start.17 = (bf16[384,512]{1,0:T(8,128)(2,1)}, bf16[384,512]{1,0:T(8,128)(2,1)S(1)}, u32[]{:S(2)}, u32[]{:S(2)}) collective-permute-start(bf16[384,512]{1,0:T(8,128)(2,1)} %slice.182), channel_id=1, source_target_pairs={{0,7},{1,0},{2,1},{3,2},{4,3},{5,4},{6,5},{7,6},{8,15},{9,8},{10,9... | collective-permute-start | bytes 1179656 | tf_op jit(solution)/shard_map/ppermute | solution.py:60
  153.6 1.8 slice.181
  155.4 24.3 %all-gather.4.cloned.1.call-done = bf16[4096,512]{1,0:T(8,128)(2,1)} async-done(((bf16[128,512]{1,0:T(8,128)(2,1)}), bf16[4096,512]{1,0:T(8,128)(2,1)}) %all-gather.4.cloned.1.call-update) | async-done | bytes 4194320 | tf_op jit(solution)/shard_map/all_gather | solution.py:110
  179.8 2.1 fusion.12
  181.8 1.9 fusion.14
  183.8 1.8 fusion.16
  185.5 1.8 fusion.18
  188.0 1.8 fusion.20
  189.8 1.6 fusion.2
  193.1 3.8 %collective-permute-start.21 = (bf16[3,4,256]{2,1,0:T(4,128)(2,1)S(1)}, bf16[3,4,256]{2,1,0:T(4,128)(2,1)S(1)}, u32[]{:S(2)}, u32[]{:S(2)}) collective-permute-start(bf16[3,4,256]{2,1,0:T(4,128)(2,1)S(1)} %squeeze.124), channel_id=1, source_target_pairs={{24,0},{56,8},{88,16},{120,24},{152,32},{184,40},{216,48},{248,56}... | collective-permute-start | bytes 18440 | tf_op jit(solution)/shard_map/ppermute | solution.py:214
  196.9 2.5 %collective-permute-start.20 = (bf16[3,4,256]{2,1,0:T(4,128)(2,1)S(1)}, bf16[3,4,256]{2,1,0:T(4,128)(2,1)S(1)}, u32[]{:S(2)}, u32[]{:S(2)}) collective-permute-start(bf16[3,4,256]{2,1,0:T(4,128)(2,1)S(1)} %squeeze.123), channel_id=1, source_target_pairs={{16,0},{48,8},{80,16},{112,24},{144,32},{176,40},{208,48},{240,56}... | collective-permute-start | bytes 18440 | tf_op jit(solution)/shard_map/ppermute | solution.py:214
  199.4 2.0 collective-permute-start.19
  201.5 6.1 %collective-permute-start.18 = (bf16[3,4,256]{2,1,0:T(4,128)(2,1)S(1)}, bf16[3,4,256]{2,1,0:T(4,128)(2,1)S(1)}, u32[]{:S(2)}, u32[]{:S(2)}) collective-permute-start(bf16[3,4,256]{2,1,0:T(4,128)(2,1)S(1)} %squeeze.121), channel_id=1, source_target_pairs={{0,0},{32,8},{64,16},{96,24},{128,32},{160,40},{192,48},{224,56},{... | collective-permute-start | bytes 18440 | tf_op jit(solution)/shard_map/ppermute | solution.py:214
  (161 shorter events, 28.3 us)
Async XLA Ops:
  7.2 46.0 %copy-start = (bf16[256,4096]{1,0:T(8,128)(2,1)S(1)}, bf16[256,4096]{1,0:T(8,128)(2,1)}, u32[]{:S(2)}) copy-start(bf16[256,4096]{1,0:T(8,128)(2,1)} %param.25) | copy-start | bytes 6291460
  7.2 119.6 %all-gather.6.cloned.1.call-start = ((), (), s32[]{:S(2)}) async-start(), calls=%async_computation.1 | async-start | bytes 3538944 | tf_op jit(solution)/shard_map/all_gather | solution.py:185
  9.4 4.7 %copy-start.3 = (bf16[4096,256]{1,0:T(8,128)(2,1)S(1)}, bf16[4096,256]{1,0:T(8,128)(2,1)}, u32[]{:S(2)}) copy-start(bf16[4096,256]{1,0:T(8,128)(2,1)} %param.23) | copy-start | bytes 6291460
  11.9 7.3 %copy-start.9 = (bf16[16,32,256]{2,1,0:T(8,128)(2,1)S(1)}, bf16[16,32,256]{2,1,0:T(8,128)(2,1)}, u32[]{:S(2)}) copy-start(bf16[16,32,256]{2,1,0:T(8,128)(2,1)} %param.32) | copy-start | bytes 786436
  11.9 7.3 %copy-start.10 = (bf16[16,32,256]{2,1,0:T(8,128)(2,1)S(1)}, bf16[16,32,256]{2,1,0:T(8,128)(2,1)}, u32[]{:S(2)}) copy-start(bf16[16,32,256]{2,1,0:T(8,128)(2,1)} %param.31) | copy-start | bytes 786436
  14.1 9.7 %copy-start.12 = (s32[3,512]{1,0:T(4,128)S(1)}, s32[3,512]{1,0:T(4,128)}, u32[]{:S(2)}) copy-start(s32[3,512]{1,0:T(4,128)} %param.33) | copy-start | bytes 18436
  14.6 21.1 %collective-permute-start.3 = (bf16[2,3,16,256]{3,2,0,1:T(8,128)(2,1)S(1)}, bf16[2,3,16,256]{3,2,0,1:T(8,128)(2,1)S(1)}, u32[]{:S(2)}, u32[]{:S(2)}) collective-permute-start(bf16[2,3,16,256]{3,2,0,1:T(8,128)(2,1)S(1)} %pad_maximum_fusion.4), channel_id=1, source_target_pairs={{64,0},{72,8},{80,16},{88,24},{96,32},{104,40},{112,48},{120,56},{... | collective-permute-start | bytes 147464 | tf_op jit(solution)/shard_map/ppermute | solution.py:34
  18.2 17.6 %collective-permute-start.4 = (bf16[2,3,16,256]{3,2,0,1:T(8,128)(2,1)S(1)}, bf16[2,3,16,256]{3,2,0,1:T(8,128)(2,1)S(1)}, u32[]{:S(2)}, u32[]{:S(2)}) collective-permute-start(bf16[2,3,16,256]{3,2,0,1:T(8,128)(2,1)S(1)} %pad_maximum_fusion.4), channel_id=1, source_target_pairs={{128,0},{136,8},{144,16},{152,24},{160,32},{168,40},{176,48},{184,... | collective-permute-start | bytes 147464 | tf_op jit(solution)/shard_map/ppermute | solution.py:34
  18.5 17.3 %collective-permute-start.5 = (bf16[2,3,16,256]{3,2,0,1:T(8,128)(2,1)S(1)}, bf16[2,3,16,256]{3,2,0,1:T(8,128)(2,1)S(1)}, u32[]{:S(2)}, u32[]{:S(2)}) collective-permute-start(bf16[2,3,16,256]{3,2,0,1:T(8,128)(2,1)S(1)} %pad_maximum_fusion.4), channel_id=1, source_target_pairs={{192,0},{200,8},{208,16},{216,24},{224,32},{232,40},{240,48},{248,... | collective-permute-start | bytes 147464 | tf_op jit(solution)/shard_map/ppermute | solution.py:34
  20.4 15.7 %collective-permute-start = (bf16[2,16,32,256]{3,1,2,0:T(8,128)(2,1)}, bf16[2,16,32,256]{3,1,2,0:T(8,128)(2,1)}, u32[]{:S(2)}, u32[]{:S(2)}) collective-permute-start(bf16[2,16,32,256]{3,1,2,0:T(8,128)(2,1)} %pad_maximum_fusion.2), channel_id=1, source_target_pairs={{64,0},{72,8},{80,16},{88,24},{96,32},{104,40},{112,48},{120,56},{... | collective-permute-start | bytes 1572872 | tf_op jit(solution)/shard_map/ppermute | solution.py:34
  22.3 13.7 %collective-permute-start.1 = (bf16[2,16,32,256]{3,1,2,0:T(8,128)(2,1)}, bf16[2,16,32,256]{3,1,2,0:T(8,128)(2,1)}, u32[]{:S(2)}, u32[]{:S(2)}) collective-permute-start(bf16[2,16,32,256]{3,1,2,0:T(8,128)(2,1)} %pad_maximum_fusion.2), channel_id=1, source_target_pairs={{128,0},{136,8},{144,16},{152,24},{160,32},{168,40},{176,48},{184,... | collective-permute-start | bytes 1572872 | tf_op jit(solution)/shard_map/ppermute | solution.py:34
  35.7 12.9 %collective-permute-start.2 = (bf16[2,16,32,256]{3,1,2,0:T(8,128)(2,1)}, bf16[2,16,32,256]{3,1,2,0:T(8,128)(2,1)S(1)}, u32[]{:S(2)}, u32[]{:S(2)}) collective-permute-start(bf16[2,16,32,256]{3,1,2,0:T(8,128)(2,1)} %pad_maximum_fusion.2), channel_id=1, source_target_pairs={{192,0},{200,8},{208,16},{216,24},{224,32},{232,40},{240,48},{248,... | collective-permute-start | bytes 1572872 | tf_op jit(solution)/shard_map/ppermute | solution.py:34
  52.2 3.0 %copy-start.6 = (bf16[768,512]{1,0:T(8,128)(2,1)S(1)}, bf16[768,512]{1,0:T(8,128)(2,1)}, u32[]{:S(2)}) copy-start(bf16[768,512]{1,0:T(8,128)(2,1)} %param.29) | copy-start | bytes 2359300
  54.4 74.8 %copy-start.1 = (bf16[3,16,4096]{2,1,0:T(8,128)(2,1)S(1)}, bf16[3,16,4096]{2,1,0:T(8,128)(2,1)}, u32[]{:S(2)}) copy-start(bf16[3,16,4096]{2,1,0:T(8,128)(2,1)} %param.18) | copy-start | bytes 1179652
  54.4 125.4 %all-gather.4.cloned.1.call-start = ((), (), s32[]{:S(2)}) async-start(), calls=%async_computation | async-start | bytes 4325376 | tf_op jit(solution)/shard_map/all_gather | solution.py:110
  55.2 25.8 %collective-permute-start.11 = (bf16[768,512]{1,0:T(8,128)(2,1)S(1)}, bf16[768,512]{1,0:T(8,128)(2,1)}, u32[]{:S(2)}, u32[]{:S(2)}) collective-permute-start(bf16[768,512]{1,0:T(8,128)(2,1)S(1)} %copy-done.6), channel_id=1, source_target_pairs={{0,7},{1,0},{2,1},{3,2},{4,3},{5,4},{6,5},{7,6},{8,15},{9,8},{10,9... | collective-permute-start | bytes 2359304 | tf_op jit(solution)/shard_map/ppermute | solution.py:55
  60.8 23.7 %collective-permute-start.10 = (bf16[768,512]{1,0:T(8,128)(2,1)S(1)}, bf16[768,512]{1,0:T(8,128)(2,1)}, u32[]{:S(2)}, u32[]{:S(2)}) collective-permute-start(bf16[768,512]{1,0:T(8,128)(2,1)S(1)} %copy-done.6), channel_id=1, source_target_pairs={{0,1},{1,2},{2,3},{3,4},{4,5},{5,6},{6,7},{7,0},{8,9},{9,10},{10,1... | collective-permute-start | bytes 2359304 | tf_op jit(solution)/shard_map/ppermute | solution.py:54
  81.0 36.4 %collective-permute-start.13 = (bf16[768,512]{1,0:T(8,128)(2,1)}, bf16[768,512]{1,0:T(8,128)(2,1)}, u32[]{:S(2)}, u32[]{:S(2)}) collective-permute-start(bf16[768,512]{1,0:T(8,128)(2,1)} %collective-permute-done.11), channel_id=1, source_target_pairs={{0,7},{1,0},{2,1},{3,2},{4,3},{5,4},{6,5},{7,6},{8,15},{9,8},{10,9... | collective-permute-start | bytes 2359304 | tf_op jit(solution)/shard_map/ppermute | solution.py:55
  84.5 36.3 %collective-permute-start.12 = (bf16[768,512]{1,0:T(8,128)(2,1)}, bf16[768,512]{1,0:T(8,128)(2,1)}, u32[]{:S(2)}, u32[]{:S(2)}) collective-permute-start(bf16[768,512]{1,0:T(8,128)(2,1)} %collective-permute-done.10), channel_id=1, source_target_pairs={{0,1},{1,2},{2,3},{3,4},{4,5},{5,6},{6,7},{7,0},{8,9},{9,10},{10,1... | collective-permute-start | bytes 2359304 | tf_op jit(solution)/shard_map/ppermute | solution.py:54
  117.3 25.9 %collective-permute-start.15 = (bf16[768,512]{1,0:T(8,128)(2,1)}, bf16[768,512]{1,0:T(8,128)(2,1)S(1)}, u32[]{:S(2)}, u32[]{:S(2)}) collective-permute-start(bf16[768,512]{1,0:T(8,128)(2,1)} %collective-permute-done.13), channel_id=1, source_target_pairs={{0,7},{1,0},{2,1},{3,2},{4,3},{5,4},{6,5},{7,6},{8,15},{9,8},{10,9... | collective-permute-start | bytes 2359304 | tf_op jit(solution)/shard_map/ppermute | solution.py:55
  120.7 29.9 %collective-permute-start.14 = (bf16[768,512]{1,0:T(8,128)(2,1)}, bf16[768,512]{1,0:T(8,128)(2,1)}, u32[]{:S(2)}, u32[]{:S(2)}) collective-permute-start(bf16[768,512]{1,0:T(8,128)(2,1)} %collective-permute-done.12), channel_id=1, source_target_pairs={{0,1},{1,2},{2,3},{3,4},{4,5},{5,6},{6,7},{7,0},{8,9},{9,10},{10,1... | collective-permute-start | bytes 2359304 | tf_op jit(solution)/shard_map/ppermute | solution.py:54
  131.3 24.0 %collective-permute-start.9 = (bf16[3,4,256]{2,1,0:T(4,128)(2,1)S(1)}, bf16[3,4,256]{2,1,0:T(4,128)(2,1)S(1)}, u32[]{:S(2)}, u32[]{:S(2)}) collective-permute-start(bf16[3,4,256]{2,1,0:T(4,128)(2,1)S(1)} %get-tuple-element.43), channel_id=1, source_target_pairs={{0,24},{8,56},{16,88},{24,120},{32,152},{40,184},{48,216},{56,248}... | collective-permute-start | bytes 18440 | tf_op jit(solution)/shard_map/ppermute | solution.py:202
  135.7 19.7 %collective-permute-start.8 = (bf16[3,4,256]{2,1,0:T(4,128)(2,1)S(1)}, bf16[3,4,256]{2,1,0:T(4,128)(2,1)S(1)}, u32[]{:S(2)}, u32[]{:S(2)}) collective-permute-start(bf16[3,4,256]{2,1,0:T(4,128)(2,1)S(1)} %get-tuple-element.44), channel_id=1, source_target_pairs={{0,16},{8,48},{16,80},{24,112},{32,144},{40,176},{48,208},{56,240}... | collective-permute-start | bytes 18440 | tf_op jit(solution)/shard_map/ppermute | solution.py:202
  140.0 15.4 %collective-permute-start.7 = (bf16[3,4,256]{2,1,0:T(4,128)(2,1)S(1)}, bf16[3,4,256]{2,1,0:T(4,128)(2,1)S(1)}, u32[]{:S(2)}, u32[]{:S(2)}) collective-permute-start(bf16[3,4,256]{2,1,0:T(4,128)(2,1)S(1)} %get-tuple-element.45), channel_id=1, source_target_pairs={{0,8},{8,40},{16,72},{24,104},{32,136},{40,168},{48,200},{56,232},... | collective-permute-start | bytes 18440 | tf_op jit(solution)/shard_map/ppermute | solution.py:202
  143.2 12.2 %collective-permute-start.6 = (bf16[3,4,256]{2,1,0:T(4,128)(2,1)S(1)}, bf16[3,4,256]{2,1,0:T(4,128)(2,1)S(1)}, u32[]{:S(2)}, u32[]{:S(2)}) collective-permute-start(bf16[3,4,256]{2,1,0:T(4,128)(2,1)S(1)} %get-tuple-element.42), channel_id=1, source_target_pairs={{0,0},{8,32},{16,64},{24,96},{32,128},{40,160},{48,192},{56,224},{... | collective-permute-start | bytes 18440 | tf_op jit(solution)/shard_map/ppermute | solution.py:202
  150.6 39.1 %collective-permute-start.17 = (bf16[384,512]{1,0:T(8,128)(2,1)}, bf16[384,512]{1,0:T(8,128)(2,1)S(1)}, u32[]{:S(2)}, u32[]{:S(2)}) collective-permute-start(bf16[384,512]{1,0:T(8,128)(2,1)} %slice.182), channel_id=1, source_target_pairs={{0,7},{1,0},{2,1},{3,2},{4,3},{5,4},{6,5},{7,6},{8,15},{9,8},{10,9... | collective-permute-start | bytes 1179656 | tf_op jit(solution)/shard_map/ppermute | solution.py:60
  155.4 34.4 %collective-permute-start.16 = (bf16[384,512]{1,0:T(8,128)(2,1)}, bf16[384,512]{1,0:T(8,128)(2,1)}, u32[]{:S(2)}, u32[]{:S(2)}) collective-permute-start(bf16[384,512]{1,0:T(8,128)(2,1)} %slice.181), channel_id=1, source_target_pairs={{0,1},{1,2},{2,3},{3,4},{4,5},{5,6},{6,7},{7,0},{8,9},{9,10},{10,1... | collective-permute-start | bytes 1179656 | tf_op jit(solution)/shard_map/ppermute | solution.py:59
  179.8 4.0 %copy-start.2 = (bf16[4096,512]{1,0:T(8,128)(2,1)S(1)}, bf16[4096,512]{1,0:T(8,128)(2,1)}, u32[]{:S(2)}) copy-start(bf16[4096,512]{1,0:T(8,128)(2,1)} %all-gather.4.cloned.1.call-done) | copy-start | bytes 12582916
  193.1 14.5 %collective-permute-start.21 = (bf16[3,4,256]{2,1,0:T(4,128)(2,1)S(1)}, bf16[3,4,256]{2,1,0:T(4,128)(2,1)S(1)}, u32[]{:S(2)}, u32[]{:S(2)}) collective-permute-start(bf16[3,4,256]{2,1,0:T(4,128)(2,1)S(1)} %squeeze.124), channel_id=1, source_target_pairs={{24,0},{56,8},{88,16},{120,24},{152,32},{184,40},{216,48},{248,56}... | collective-permute-start | bytes 18440 | tf_op jit(solution)/shard_map/ppermute | solution.py:214
  196.9 10.7 %collective-permute-start.20 = (bf16[3,4,256]{2,1,0:T(4,128)(2,1)S(1)}, bf16[3,4,256]{2,1,0:T(4,128)(2,1)S(1)}, u32[]{:S(2)}, u32[]{:S(2)}) collective-permute-start(bf16[3,4,256]{2,1,0:T(4,128)(2,1)S(1)} %squeeze.123), channel_id=1, source_target_pairs={{16,0},{48,8},{80,16},{112,24},{144,32},{176,40},{208,48},{240,56}... | collective-permute-start | bytes 18440 | tf_op jit(solution)/shard_map/ppermute | solution.py:214
  199.4 8.2 %collective-permute-start.19 = (bf16[3,4,256]{2,1,0:T(4,128)(2,1)S(1)}, bf16[3,4,256]{2,1,0:T(4,128)(2,1)S(1)}, u32[]{:S(2)}, u32[]{:S(2)}) collective-permute-start(bf16[3,4,256]{2,1,0:T(4,128)(2,1)S(1)} %squeeze.122), channel_id=1, source_target_pairs={{8,0},{40,8},{72,16},{104,24},{136,32},{168,40},{200,48},{232,56},... | collective-permute-start | bytes 18440 | tf_op jit(solution)/shard_map/ppermute | solution.py:214
  201.5 6.9 %collective-permute-start.18 = (bf16[3,4,256]{2,1,0:T(4,128)(2,1)S(1)}, bf16[3,4,256]{2,1,0:T(4,128)(2,1)S(1)}, u32[]{:S(2)}, u32[]{:S(2)}) collective-permute-start(bf16[3,4,256]{2,1,0:T(4,128)(2,1)S(1)} %squeeze.121), channel_id=1, source_target_pairs={{0,0},{32,8},{64,16},{96,24},{128,32},{160,40},{192,48},{224,56},{... | collective-permute-start | bytes 18440 | tf_op jit(solution)/shard_map/ppermute | solution.py:214
  (11 other events, 21.0 us)
Sparse Core Ops, SparseCore 0:
  54.5 72.2 all-gather.5
  129.3 50.4 all-gather.3

commit v6 on v5

--- a/solution.py
+++ b/solution.py
@@ -60,6 +60,25 @@
         bottom = lax.ppermute(from_right[half:], axis, left)
         last = jnp.concatenate([top, bottom], axis=0)
         total = total + partial(last, count // 2)
+    return total
+
+
+def ring_sum(block, axis):
+    count = lax.axis_size(axis)
+    right = [(i, (i + 1) % count) for i in range(count)]
+    left = [(i, (i - 1) % count) for i in range(count)]
+    total = block.astype(jnp.float32)
+    from_left = block
+    from_right = block
+    for _ in range(1, count // 2):
+        from_left = lax.ppermute(from_left, axis, right)
+        from_right = lax.ppermute(from_right, axis, left)
+        total = total + from_left.astype(jnp.float32) + from_right.astype(jnp.float32)
+    if count % 2 == 0 and count > 1:
+        half = block.shape[0] // 2
+        top = lax.ppermute(from_left[:half], axis, right)
+        bottom = lax.ppermute(from_right[half:], axis, left)
+        total = total + jnp.concatenate([top, bottom], axis=0).astype(jnp.float32)
     return total
 
 
@@ -182,8 +201,7 @@
         contexts.append((summed / totals).astype(jnp.bfloat16))
     self_context = jnp.stack(contexts).reshape(steps * row_count, head_width)
     partial_out = jnp.dot(self_context, self_wo, preferred_element_type=jnp.float32)
-    every_part = lax.all_gather(partial_out.astype(jnp.bfloat16), "head", axis=0, tiled=False)
-    summed_out = jnp.sum(every_part.astype(jnp.float32), axis=0)
+    summed_out = ring_sum(partial_out.astype(jnp.bfloat16), "head")
     residual = hidden_in + summed_out.reshape(hidden_in.shape)
     normed_cross = rms_scaled(residual, cross_gain).astype(jnp.bfloat16)
     cross_query = jnp.dot(

time: 220 us -> 187 us (0.85); the launches traced: 216 us -> 186 us
  waiting for transfers between devices: 96.6 us -> 45.4 us
  starting transfers between devices: 56.5 us -> 75.1 us
  other arithmetic: 14 us -> 16.5 us
    ppermute x3, waiting for transfers between devices: 52.3 us -> 0.01 us  [ring_project(): from_right = lax.ppermute(from_right, axis, left)]
    ppermute x0 -> x8, waiting for transfers between devices: none -> 32.2 us  [the longest x3 29.3 us: ring_sum(): from_right = lax.ppermute(from_right, axis, left)]
    all_gather x1, waiting for transfers between devices: 24.3 us -> 0.01 us  [shards(): full_weights = lax.all_gather(cross_wkv, 'hyp', axis=0, tiled=True)]
    ppermute x0 -> x8, starting transfers between devices: none -> 15.3 us  [the longest x3 11.8 us: ring_sum(): from_right = lax.ppermute(from_right, axis, left)]
    all_gather x1 -> x0, waiting for transfers between devices: 6.04 us -> none  [shards(): lax.all_gather(partial_out.astype(jnp.bfloat16), 'head', axis=0, tiled=Fa...]
    ppermute x4, starting transfers between devices: 18.3 us -> 22.3 us  [shards(): sent.append(lax.ppermute(piece, 'hyp', route))]
    ppermute x6, waiting for transfers between devices: 12.6 us -> 9.56 us  [beam_copies(): copies.append(lax.ppermute(block, 'hyp', route))]
    ppermute x1, starting transfers between devices: 2.94 us -> 0.01 us  [ring_project(): bottom = lax.ppermute(from_right[half:], axis, left)]
  transfers between devices with their start and end apart: 24 -> 31, of which waited for: 6 -> 8; matrix products, arithmetic and copies ran while one was open for 13% -> 20% of each run, Pallas kernels for 0% -> 0%
where the time goes in v6:
time: 187 us; the launch traced here: 186 us
  starting transfers between devices  75.1 us (40%)
  waiting for transfers between devices  45.4 us (24%)
  matrix products  20.9 us (11%)
  other arithmetic  16.5 us (9%)
  between operations  15.7 us (8%)
  local copies, waits for them, and re-layouts  12.6 us (7%)
    ppermute x3, waiting for transfers between devices, ring_sum(): from_right = lax.ppermute(from_right, axis, left)  29.3 us
    ppermute x4, starting transfers between devices, shards(): sent.append(lax.ppermute(piece, 'hyp', route))  22.3 us
    ppermute x4, starting transfers between devices, shards(): back.append(lax.ppermute(answer[shift], 'hyp', route))  17.3 us
    dot_general x8, matrix products, partial(): return jnp.dot(piece, w, preferred_element_type=jnp.float32)  12.4 us
    ppermute x3, starting transfers between devices, ring_sum(): from_right = lax.ppermute(from_right, axis, left)  11.8 us
    ppermute x3, starting transfers between devices, ring_project(): from_right = lax.ppermute(from_right, axis, left)  10.5 us
    ppermute x6, waiting for transfers between devices, beam_copies(): copies.append(lax.ppermute(block, 'hyp', route))  9.56 us
    ppermute x6, starting transfers between devices, beam_copies(): copies.append(lax.ppermute(block, 'hyp', route))  8.15 us
  transfers between devices with their start and end apart: 31, of which 8 were waited for; matrix products, arithmetic and copies ran while one was open for 20% of the time, Pallas kernels for 0%

profile of v6, /device:TPU:1, one launch (start us, length us, event | category | flops | bytes accessed | tf_op | source)
XLA Modules:
  0.0 186.3 jit_solution(3499635144603889853)
XLA Ops:
  11.9 2.1 %convolution_convert_fusion.3 = bf16[48,256]{1,0:T(8,128)(2,1)S(1)} fusion(bf16[48,4096]{1,0:T(8,128)(2,1)S(1)} %bitcast.289, bf16[4096,256]{1,0:T(8,128)(2,1)} %param.24), kind=kOutput, calls=%fused_computation.14 | convolution fusion | flops 100675584 | bytes 2514944 | tf_op jit(solution)/shard_map/dot_general | solution.py:150
  14.6 3.6 %collective-permute-start.3 = (bf16[2,3,16,256]{3,2,0,1:T(8,128)(2,1)S(1)}, bf16[2,3,16,256]{3,2,0,1:T(8,128)(2,1)S(1)}, u32[]{:S(2)}, u32[]{:S(2)}) collective-permute-start(bf16[2,3,16,256]{3,2,0,1:T(8,128)(2,1)S(1)} %pad_maximum_fusion.4), channel_id=1, source_target_pairs={{64,0},{72,8},{80,16},{88,24},{96,32},{104,40},{112,48},{120,56},{... | collective-permute-start | bytes 147464 | tf_op jit(solution)/shard_map/ppermute | solution.py:34
  20.4 2.0 %collective-permute-start = (bf16[2,16,32,256]{3,1,2,0:T(8,128)(2,1)}, bf16[2,16,32,256]{3,1,2,0:T(8,128)(2,1)}, u32[]{:S(2)}, u32[]{:S(2)}) collective-permute-start(bf16[2,16,32,256]{3,1,2,0:T(8,128)(2,1)} %pad_maximum_fusion.2), channel_id=1, source_target_pairs={{64,0},{72,8},{80,16},{88,24},{96,32},{104,40},{112,48},{120,56},{... | collective-permute-start | bytes 1572872 | tf_op jit(solution)/shard_map/ppermute | solution.py:34
  36.6 2.1 %convolution_convert_fusion.5 = bf16[48,256]{1,0:T(8,128)(2,1)S(1)} fusion(bf16[48,4096]{1,0:T(8,128)(2,1)S(1)} %bitcast.291, bf16[4096,256]{1,0:T(8,128)(2,1)} %param.22), kind=kOutput, calls=%fused_computation.16 | convolution fusion | flops 100675584 | bytes 2514944 | tf_op jit(solution)/shard_map/dot_general | solution.py:148
  38.8 5.7 %collective-permute-start.19 = (bf16[768,512]{1,0:T(8,128)(2,1)S(1)}, bf16[768,512]{1,0:T(8,128)(2,1)}, u32[]{:S(2)}, u32[]{:S(2)}) collective-permute-start(bf16[768,512]{1,0:T(8,128)(2,1)S(1)} %copy-done.8), channel_id=1, source_target_pairs={{0,7},{1,0},{2,1},{3,2},{4,3},{5,4},{6,5},{7,6},{8,15},{9,8},{10,9... | collective-permute-start | bytes 2359304 | tf_op jit(solution)/shard_map/ppermute | solution.py:55
  44.8 9.5 %collective-permute-done.2 = bf16[2,16,32,256]{3,1,2,0:T(8,128)(2,1)S(1)} collective-permute-done((bf16[2,16,32,256]{3,1,2,0:T(8,128)(2,1)}, bf16[2,16,32,256]{3,1,2,0:T(8,128)(2,1)S(1)}, u32[]{:S(2)}, u32[]{:S(2)}) %collective-permute-start.2) | collective-permute-done | bytes 524320 | tf_op jit(solution)/shard_map/ppermute | solution.py:34
  59.2 4.7 %collective-permute-start.7 = (bf16[48,4096]{1,0:T(8,128)(2,1)S(1)}, bf16[48,4096]{1,0:T(8,128)(2,1)S(1)}, u32[]{:S(2)}, u32[]{:S(2)}) collective-permute-start(bf16[48,4096]{1,0:T(8,128)(2,1)S(1)} %convolution_convert_fusion), channel_id=1, source_target_pairs={{0,7},{1,0},{2,1},{3,2},{4,3},{5,4},{6,5},{7,6},{8,15},{9,8},{10,9... | collective-permute-start | bytes 1179656 | tf_op jit(solution)/shard_map/ppermute | solution.py:75
  63.9 5.9 %collective-permute-done.7 = bf16[48,4096]{1,0:T(8,128)(2,1)S(1)} collective-permute-done((bf16[48,4096]{1,0:T(8,128)(2,1)S(1)}, bf16[48,4096]{1,0:T(8,128)(2,1)S(1)}, u32[]{:S(2)}, u32[]{:S(2)}) %collective-permute-start.7) | collective-permute-done | bytes 393248 | tf_op jit(solution)/shard_map/ppermute | solution.py:75
  69.8 3.5 %collective-permute-start.9 = (bf16[48,4096]{1,0:T(8,128)(2,1)S(1)}, bf16[48,4096]{1,0:T(8,128)(2,1)}, u32[]{:S(2)}, u32[]{:S(2)}) collective-permute-start(bf16[48,4096]{1,0:T(8,128)(2,1)S(1)} %collective-permute-done.7), channel_id=1, source_target_pairs={{0,7},{1,0},{2,1},{3,2},{4,3},{5,4},{6,5},{7,6},{8,15},{9,8},{10,9... | collective-permute-start | bytes 1179656 | tf_op jit(solution)/shard_map/ppermute | solution.py:75
  73.3 2.7 %collective-permute-start.21 = (bf16[768,512]{1,0:T(8,128)(2,1)}, bf16[768,512]{1,0:T(8,128)(2,1)}, u32[]{:S(2)}, u32[]{:S(2)}) collective-permute-start(bf16[768,512]{1,0:T(8,128)(2,1)} %collective-permute-done.19), channel_id=1, source_target_pairs={{0,7},{1,0},{2,1},{3,2},{4,3},{5,4},{6,5},{7,6},{8,15},{9,8},{10,9... | collective-permute-start | bytes 2359304 | tf_op jit(solution)/shard_map/ppermute | solution.py:55
  76.0 2.4 %collective-permute-done.9 = bf16[48,4096]{1,0:T(8,128)(2,1)} collective-permute-done((bf16[48,4096]{1,0:T(8,128)(2,1)S(1)}, bf16[48,4096]{1,0:T(8,128)(2,1)}, u32[]{:S(2)}, u32[]{:S(2)}) %collective-permute-start.9) | collective-permute-done | bytes 393248 | tf_op jit(solution)/shard_map/ppermute | solution.py:75
  78.4 3.5 %collective-permute-start.11 = (bf16[48,4096]{1,0:T(8,128)(2,1)}, bf16[48,4096]{1,0:T(8,128)(2,1)S(1)}, u32[]{:S(2)}, u32[]{:S(2)}) collective-permute-start(bf16[48,4096]{1,0:T(8,128)(2,1)} %collective-permute-done.9), channel_id=1, source_target_pairs={{0,7},{1,0},{2,1},{3,2},{4,3},{5,4},{6,5},{7,6},{8,15},{9,8},{10,9... | collective-permute-start | bytes 1179656 | tf_op jit(solution)/shard_map/ppermute | solution.py:75
  82.8 21.0 %collective-permute-done.11 = bf16[48,4096]{1,0:T(8,128)(2,1)S(1)} collective-permute-done((bf16[48,4096]{1,0:T(8,128)(2,1)}, bf16[48,4096]{1,0:T(8,128)(2,1)S(1)}, u32[]{:S(2)}, u32[]{:S(2)}) %collective-permute-start.11) | collective-permute-done | bytes 393248 | tf_op jit(solution)/shard_map/ppermute | solution.py:75
  103.8 3.4 %collective-permute-start.13 = (bf16[24,4096]{1,0:T(8,128)(2,1)S(1)}, bf16[24,4096]{1,0:T(8,128)(2,1)S(1)}, u32[]{:S(2)}, u32[]{:S(2)}) collective-permute-start(bf16[24,4096]{1,0:T(8,128)(2,1)S(1)} %slice.190), channel_id=1, source_target_pairs={{0,7},{1,0},{2,1},{3,2},{4,3},{5,4},{6,5},{7,6},{8,15},{9,8},{10,9... | collective-permute-start | bytes 589832 | tf_op jit(solution)/shard_map/ppermute | solution.py:80
  108.0 2.2 %collective-permute-start.23 = (bf16[768,512]{1,0:T(8,128)(2,1)}, bf16[768,512]{1,0:T(8,128)(2,1)S(1)}, u32[]{:S(2)}, u32[]{:S(2)}) collective-permute-start(bf16[768,512]{1,0:T(8,128)(2,1)} %collective-permute-done.21), channel_id=1, source_target_pairs={{0,7},{1,0},{2,1},{3,2},{4,3},{5,4},{6,5},{7,6},{8,15},{9,8},{10,9... | collective-permute-start | bytes 2359304 | tf_op jit(solution)/shard_map/ppermute | solution.py:55
  110.2 2.9 %collective-permute-done.12 = bf16[24,4096]{1,0:T(8,128)(2,1)S(1)} collective-permute-done((bf16[24,4096]{1,0:T(8,128)(2,1)S(1)}, bf16[24,4096]{1,0:T(8,128)(2,1)S(1)}, u32[]{:S(2)}, u32[]{:S(2)}) %collective-permute-start.12) | collective-permute-done | bytes 196640 | tf_op jit(solution)/shard_map/ppermute | solution.py:79
  113.1 2.0 %convert_add_fusion = f32[48,4096]{1,0:T(8,128)S(1)} fusion(bf16[48,4096]{1,0:T(8,128)(2,1)} %copy-done.6, bf16[48,4096]{1,0:T(8,128)(2,1)} %copy-done.7, bf16[48,4096]{1,0:T(8,128)(2,1)} %collective-permute-done.9, bf16[48,4096]{1,0:T(8,128)(2,1)} %collective-permute-done.8, bf16[48,4096]{1,0:T(8,128)(2,1)} %copy-done.10, bf16[48,4096]{1,0:T(8,128)(2,1)} %copy-done.11, ...), kind=kLoop, calls=%fused_computation.23 | loop fusion | flops 3538944 | bytes 3932160 | tf_op jit(solution)/shard_map/add | solution.py:81
  117.2 5.1 %collective-permute-start.17 = (bf16[3,4,256]{2,1,0:T(4,128)(2,1)S(1)}, bf16[3,4,256]{2,1,0:T(4,128)(2,1)S(1)}, u32[]{:S(2)}, u32[]{:S(2)}) collective-permute-start(bf16[3,4,256]{2,1,0:T(4,128)(2,1)S(1)} %get-tuple-element.43), channel_id=1, source_target_pairs={{0,24},{8,56},{16,88},{24,120},{32,152},{40,184},{48,216},{56,248}... | collective-permute-start | bytes 18440 | tf_op jit(solution)/shard_map/ppermute | solution.py:220
  122.3 7.5 %collective-permute-start.16 = (bf16[3,4,256]{2,1,0:T(4,128)(2,1)S(1)}, bf16[3,4,256]{2,1,0:T(4,128)(2,1)S(1)}, u32[]{:S(2)}, u32[]{:S(2)}) collective-permute-start(bf16[3,4,256]{2,1,0:T(4,128)(2,1)S(1)} %get-tuple-element.44), channel_id=1, source_target_pairs={{0,16},{8,48},{16,80},{24,112},{32,144},{40,176},{48,208},{56,240}... | collective-permute-start | bytes 18440 | tf_op jit(solution)/shard_map/ppermute | solution.py:220
  129.8 2.8 %collective-permute-start.15 = (bf16[3,4,256]{2,1,0:T(4,128)(2,1)S(1)}, bf16[3,4,256]{2,1,0:T(4,128)(2,1)S(1)}, u32[]{:S(2)}, u32[]{:S(2)}) collective-permute-start(bf16[3,4,256]{2,1,0:T(4,128)(2,1)S(1)} %get-tuple-element.45), channel_id=1, source_target_pairs={{0,8},{8,40},{16,72},{24,104},{32,136},{40,168},{48,200},{56,232},... | collective-permute-start | bytes 18440 | tf_op jit(solution)/shard_map/ppermute | solution.py:220
  132.6 6.9 %collective-permute-start.14 = (bf16[3,4,256]{2,1,0:T(4,128)(2,1)S(1)}, bf16[3,4,256]{2,1,0:T(4,128)(2,1)S(1)}, u32[]{:S(2)}, u32[]{:S(2)}) collective-permute-start(bf16[3,4,256]{2,1,0:T(4,128)(2,1)S(1)} %get-tuple-element.42), channel_id=1, source_target_pairs={{0,0},{8,32},{16,64},{24,96},{32,128},{40,160},{48,192},{56,224},{... | collective-permute-start | bytes 18440 | tf_op jit(solution)/shard_map/ppermute | solution.py:220
  141.2 1.8 slice.191
  144.4 2.1 %fusion.12 = f32[512,768]{1,0:T(8,128)S(1)} fusion(bf16[768,512]{1,0:T(8,128)(2,1)} %collective-permute-done.22, bf16[4096,512]{1,0:T(8,128)(2,1)} %all-gather.2.cloned.1.call-done, s32[]{:T(128)S(6)} %select_n.409), kind=kOutput, calls=%fused_computation.36 | convolution fusion | flops 402653184 | bytes 2883588 | tf_op jit(solution)/shard_map/dot_general | solution.py:48
  146.5 1.9 %fusion.14 = f32[512,768]{1,0:T(8,128)S(1)} fusion(bf16[768,512]{1,0:T(8,128)(2,1)} %collective-permute-done.21, bf16[4096,512]{1,0:T(8,128)(2,1)} %all-gather.2.cloned.1.call-done, s32[]{:T(128)S(6)} %select_n.407), kind=kOutput, calls=%fused_computation.38 | convolution fusion | flops 402653184 | bytes 2883588 | tf_op jit(solution)/shard_map/dot_general | solution.py:48
  148.4 1.8 fusion.16
  150.2 1.8 fusion.18
  152.7 1.8 fusion.20
  157.7 7.6 %collective-permute-start.29 = (bf16[3,4,256]{2,1,0:T(4,128)(2,1)S(1)}, bf16[3,4,256]{2,1,0:T(4,128)(2,1)S(1)}, u32[]{:S(2)}, u32[]{:S(2)}) collective-permute-start(bf16[3,4,256]{2,1,0:T(4,128)(2,1)S(1)} %squeeze.124), channel_id=1, source_target_pairs={{24,0},{56,8},{88,16},{120,24},{152,32},{184,40},{216,48},{248,56}... | collective-permute-start | bytes 18440 | tf_op jit(solution)/shard_map/ppermute | solution.py:232
  165.3 4.4 %collective-permute-start.28 = (bf16[3,4,256]{2,1,0:T(4,128)(2,1)S(1)}, bf16[3,4,256]{2,1,0:T(4,128)(2,1)S(1)}, u32[]{:S(2)}, u32[]{:S(2)}) collective-permute-start(bf16[3,4,256]{2,1,0:T(4,128)(2,1)S(1)} %squeeze.123), channel_id=1, source_target_pairs={{16,0},{48,8},{80,16},{112,24},{144,32},{176,40},{208,48},{240,56}... | collective-permute-start | bytes 18440 | tf_op jit(solution)/shard_map/ppermute | solution.py:232
  169.7 1.9 %collective-permute-start.27 = (bf16[3,4,256]{2,1,0:T(4,128)(2,1)S(1)}, bf16[3,4,256]{2,1,0:T(4,128)(2,1)S(1)}, u32[]{:S(2)}, u32[]{:S(2)}) collective-permute-start(bf16[3,4,256]{2,1,0:T(4,128)(2,1)S(1)} %squeeze.122), channel_id=1, source_target_pairs={{8,0},{40,8},{72,16},{104,24},{136,32},{168,40},{200,48},{232,56},... | collective-permute-start | bytes 18440 | tf_op jit(solution)/shard_map/ppermute | solution.py:232
  171.6 3.4 %collective-permute-start.26 = (bf16[3,4,256]{2,1,0:T(4,128)(2,1)S(1)}, bf16[3,4,256]{2,1,0:T(4,128)(2,1)S(1)}, u32[]{:S(2)}, u32[]{:S(2)}) collective-permute-start(bf16[3,4,256]{2,1,0:T(4,128)(2,1)S(1)} %squeeze.121), channel_id=1, source_target_pairs={{0,0},{32,8},{64,16},{96,24},{128,32},{160,40},{192,48},{224,56},{... | collective-permute-start | bytes 18440 | tf_op jit(solution)/shard_map/ppermute | solution.py:232
  175.6 2.5 %collective-permute-done.26 = bf16[3,4,256]{2,1,0:T(4,128)(2,1)S(1)} collective-permute-done((bf16[3,4,256]{2,1,0:T(4,128)(2,1)S(1)}, bf16[3,4,256]{2,1,0:T(4,128)(2,1)S(1)}, u32[]{:S(2)}, u32[]{:S(2)}) %collective-permute-start.26) | collective-permute-done | bytes 6176 | tf_op jit(solution)/shard_map/ppermute | solution.py:232
  (184 shorter events, 38.1 us)
Async XLA Ops:
  7.2 51.5 %copy-start = (bf16[256,4096]{1,0:T(8,128)(2,1)S(1)}, bf16[256,4096]{1,0:T(8,128)(2,1)}, u32[]{:S(2)}) copy-start(bf16[256,4096]{1,0:T(8,128)(2,1)} %param.25) | copy-start | bytes 6291460
  7.2 137.2 %all-gather.2.cloned.1.call-start = ((), (), s32[]{:S(2)}) async-start(), calls=%async_computation | async-start | bytes 4325376 | tf_op jit(solution)/shard_map/all_gather | solution.py:129
  14.6 24.1 %collective-permute-start.3 = (bf16[2,3,16,256]{3,2,0,1:T(8,128)(2,1)S(1)}, bf16[2,3,16,256]{3,2,0,1:T(8,128)(2,1)S(1)}, u32[]{:S(2)}, u32[]{:S(2)}) collective-permute-start(bf16[2,3,16,256]{3,2,0,1:T(8,128)(2,1)S(1)} %pad_maximum_fusion.4), channel_id=1, source_target_pairs={{64,0},{72,8},{80,16},{88,24},{96,32},{104,40},{112,48},{120,56},{... | collective-permute-start | bytes 147464 | tf_op jit(solution)/shard_map/ppermute | solution.py:34
  18.2 20.6 %collective-permute-start.4 = (bf16[2,3,16,256]{3,2,0,1:T(8,128)(2,1)S(1)}, bf16[2,3,16,256]{3,2,0,1:T(8,128)(2,1)S(1)}, u32[]{:S(2)}, u32[]{:S(2)}) collective-permute-start(bf16[2,3,16,256]{3,2,0,1:T(8,128)(2,1)S(1)} %pad_maximum_fusion.4), channel_id=1, source_target_pairs={{128,0},{136,8},{144,16},{152,24},{160,32},{168,40},{176,48},{184,... | collective-permute-start | bytes 147464 | tf_op jit(solution)/shard_map/ppermute | solution.py:34
  18.5 26.0 %collective-permute-start.5 = (bf16[2,3,16,256]{3,2,0,1:T(8,128)(2,1)S(1)}, bf16[2,3,16,256]{3,2,0,1:T(8,128)(2,1)S(1)}, u32[]{:S(2)}, u32[]{:S(2)}) collective-permute-start(bf16[2,3,16,256]{3,2,0,1:T(8,128)(2,1)S(1)} %pad_maximum_fusion.4), channel_id=1, source_target_pairs={{192,0},{200,8},{208,16},{216,24},{224,32},{232,40},{240,48},{248,... | collective-permute-start | bytes 147464 | tf_op jit(solution)/shard_map/ppermute | solution.py:34
  20.4 24.4 %collective-permute-start = (bf16[2,16,32,256]{3,1,2,0:T(8,128)(2,1)}, bf16[2,16,32,256]{3,1,2,0:T(8,128)(2,1)}, u32[]{:S(2)}, u32[]{:S(2)}) collective-permute-start(bf16[2,16,32,256]{3,1,2,0:T(8,128)(2,1)} %pad_maximum_fusion.2), channel_id=1, source_target_pairs={{64,0},{72,8},{80,16},{88,24},{96,32},{104,40},{112,48},{120,56},{... | collective-permute-start | bytes 1572872 | tf_op jit(solution)/shard_map/ppermute | solution.py:34
  22.4 22.4 %collective-permute-start.1 = (bf16[2,16,32,256]{3,1,2,0:T(8,128)(2,1)}, bf16[2,16,32,256]{3,1,2,0:T(8,128)(2,1)}, u32[]{:S(2)}, u32[]{:S(2)}) collective-permute-start(bf16[2,16,32,256]{3,1,2,0:T(8,128)(2,1)} %pad_maximum_fusion.2), channel_id=1, source_target_pairs={{128,0},{136,8},{144,16},{152,24},{160,32},{168,40},{176,48},{184,... | collective-permute-start | bytes 1572872 | tf_op jit(solution)/shard_map/ppermute | solution.py:34
  38.7 15.6 %collective-permute-start.2 = (bf16[2,16,32,256]{3,1,2,0:T(8,128)(2,1)}, bf16[2,16,32,256]{3,1,2,0:T(8,128)(2,1)S(1)}, u32[]{:S(2)}, u32[]{:S(2)}) collective-permute-start(bf16[2,16,32,256]{3,1,2,0:T(8,128)(2,1)} %pad_maximum_fusion.2), channel_id=1, source_target_pairs={{192,0},{200,8},{208,16},{216,24},{224,32},{232,40},{240,48},{248,... | collective-permute-start | bytes 1572872 | tf_op jit(solution)/shard_map/ppermute | solution.py:34
  38.8 34.5 %collective-permute-start.19 = (bf16[768,512]{1,0:T(8,128)(2,1)S(1)}, bf16[768,512]{1,0:T(8,128)(2,1)}, u32[]{:S(2)}, u32[]{:S(2)}) collective-permute-start(bf16[768,512]{1,0:T(8,128)(2,1)S(1)} %copy-done.8), channel_id=1, source_target_pairs={{0,7},{1,0},{2,1},{3,2},{4,3},{5,4},{6,5},{7,6},{8,15},{9,8},{10,9... | collective-permute-start | bytes 2359304 | tf_op jit(solution)/shard_map/ppermute | solution.py:55
  44.5 31.5 %collective-permute-start.18 = (bf16[768,512]{1,0:T(8,128)(2,1)S(1)}, bf16[768,512]{1,0:T(8,128)(2,1)}, u32[]{:S(2)}, u32[]{:S(2)}) collective-permute-start(bf16[768,512]{1,0:T(8,128)(2,1)S(1)} %copy-done.8), channel_id=1, source_target_pairs={{0,1},{1,2},{2,3},{3,4},{4,5},{5,6},{6,7},{7,0},{8,9},{9,10},{10,1... | collective-permute-start | bytes 2359304 | tf_op jit(solution)/shard_map/ppermute | solution.py:54
  59.2 10.6 %collective-permute-start.7 = (bf16[48,4096]{1,0:T(8,128)(2,1)S(1)}, bf16[48,4096]{1,0:T(8,128)(2,1)S(1)}, u32[]{:S(2)}, u32[]{:S(2)}) collective-permute-start(bf16[48,4096]{1,0:T(8,128)(2,1)S(1)} %convolution_convert_fusion), channel_id=1, source_target_pairs={{0,7},{1,0},{2,1},{3,2},{4,3},{5,4},{6,5},{7,6},{8,15},{9,8},{10,9... | collective-permute-start | bytes 1179656 | tf_op jit(solution)/shard_map/ppermute | solution.py:75
  63.9 9.4 %collective-permute-start.6 = (bf16[48,4096]{1,0:T(8,128)(2,1)S(1)}, bf16[48,4096]{1,0:T(8,128)(2,1)S(1)}, u32[]{:S(2)}, u32[]{:S(2)}) collective-permute-start(bf16[48,4096]{1,0:T(8,128)(2,1)S(1)} %convolution_convert_fusion), channel_id=1, source_target_pairs={{0,1},{1,2},{2,3},{3,4},{4,5},{5,6},{6,7},{7,0},{8,9},{9,10},{10,1... | collective-permute-start | bytes 1179656 | tf_op jit(solution)/shard_map/ppermute | solution.py:74
  69.8 8.6 %collective-permute-start.9 = (bf16[48,4096]{1,0:T(8,128)(2,1)S(1)}, bf16[48,4096]{1,0:T(8,128)(2,1)}, u32[]{:S(2)}, u32[]{:S(2)}) collective-permute-start(bf16[48,4096]{1,0:T(8,128)(2,1)S(1)} %collective-permute-done.7), channel_id=1, source_target_pairs={{0,7},{1,0},{2,1},{3,2},{4,3},{5,4},{6,5},{7,6},{8,15},{9,8},{10,9... | collective-permute-start | bytes 1179656 | tf_op jit(solution)/shard_map/ppermute | solution.py:75
  73.3 8.6 %collective-permute-start.8 = (bf16[48,4096]{1,0:T(8,128)(2,1)S(1)}, bf16[48,4096]{1,0:T(8,128)(2,1)}, u32[]{:S(2)}, u32[]{:S(2)}) collective-permute-start(bf16[48,4096]{1,0:T(8,128)(2,1)S(1)} %collective-permute-done.6), channel_id=1, source_target_pairs={{0,1},{1,2},{2,3},{3,4},{4,5},{5,6},{6,7},{7,0},{8,9},{9,10},{10,1... | collective-permute-start | bytes 1179656 | tf_op jit(solution)/shard_map/ppermute | solution.py:74
  73.3 34.7 %collective-permute-start.21 = (bf16[768,512]{1,0:T(8,128)(2,1)}, bf16[768,512]{1,0:T(8,128)(2,1)}, u32[]{:S(2)}, u32[]{:S(2)}) collective-permute-start(bf16[768,512]{1,0:T(8,128)(2,1)} %collective-permute-done.19), channel_id=1, source_target_pairs={{0,7},{1,0},{2,1},{3,2},{4,3},{5,4},{6,5},{7,6},{8,15},{9,8},{10,9... | collective-permute-start | bytes 2359304 | tf_op jit(solution)/shard_map/ppermute | solution.py:55
  76.0 34.2 %collective-permute-start.20 = (bf16[768,512]{1,0:T(8,128)(2,1)}, bf16[768,512]{1,0:T(8,128)(2,1)}, u32[]{:S(2)}, u32[]{:S(2)}) collective-permute-start(bf16[768,512]{1,0:T(8,128)(2,1)} %collective-permute-done.18), channel_id=1, source_target_pairs={{0,1},{1,2},{2,3},{3,4},{4,5},{5,6},{6,7},{7,0},{8,9},{9,10},{10,1... | collective-permute-start | bytes 2359304 | tf_op jit(solution)/shard_map/ppermute | solution.py:54
  78.4 25.4 %collective-permute-start.11 = (bf16[48,4096]{1,0:T(8,128)(2,1)}, bf16[48,4096]{1,0:T(8,128)(2,1)S(1)}, u32[]{:S(2)}, u32[]{:S(2)}) collective-permute-start(bf16[48,4096]{1,0:T(8,128)(2,1)} %collective-permute-done.9), channel_id=1, source_target_pairs={{0,7},{1,0},{2,1},{3,2},{4,3},{5,4},{6,5},{7,6},{8,15},{9,8},{10,9... | collective-permute-start | bytes 1179656 | tf_op jit(solution)/shard_map/ppermute | solution.py:75
  82.0 25.3 %collective-permute-start.10 = (bf16[48,4096]{1,0:T(8,128)(2,1)}, bf16[48,4096]{1,0:T(8,128)(2,1)S(1)}, u32[]{:S(2)}, u32[]{:S(2)}) collective-permute-start(bf16[48,4096]{1,0:T(8,128)(2,1)} %collective-permute-done.8), channel_id=1, source_target_pairs={{0,1},{1,2},{2,3},{3,4},{4,5},{5,6},{6,7},{7,0},{8,9},{9,10},{10,1... | collective-permute-start | bytes 1179656 | tf_op jit(solution)/shard_map/ppermute | solution.py:74
  103.8 6.3 %collective-permute-start.13 = (bf16[24,4096]{1,0:T(8,128)(2,1)S(1)}, bf16[24,4096]{1,0:T(8,128)(2,1)S(1)}, u32[]{:S(2)}, u32[]{:S(2)}) collective-permute-start(bf16[24,4096]{1,0:T(8,128)(2,1)S(1)} %slice.190), channel_id=1, source_target_pairs={{0,7},{1,0},{2,1},{3,2},{4,3},{5,4},{6,5},{7,6},{8,15},{9,8},{10,9... | collective-permute-start | bytes 589832 | tf_op jit(solution)/shard_map/ppermute | solution.py:80
  107.3 5.8 %collective-permute-start.12 = (bf16[24,4096]{1,0:T(8,128)(2,1)S(1)}, bf16[24,4096]{1,0:T(8,128)(2,1)S(1)}, u32[]{:S(2)}, u32[]{:S(2)}) collective-permute-start(bf16[24,4096]{1,0:T(8,128)(2,1)S(1)} %slice.189), channel_id=1, source_target_pairs={{0,1},{1,2},{2,3},{3,4},{4,5},{5,6},{6,7},{7,0},{8,9},{9,10},{10,1... | collective-permute-start | bytes 589832 | tf_op jit(solution)/shard_map/ppermute | solution.py:79
  108.0 32.3 %collective-permute-start.23 = (bf16[768,512]{1,0:T(8,128)(2,1)}, bf16[768,512]{1,0:T(8,128)(2,1)S(1)}, u32[]{:S(2)}, u32[]{:S(2)}) collective-permute-start(bf16[768,512]{1,0:T(8,128)(2,1)} %collective-permute-done.21), channel_id=1, source_target_pairs={{0,7},{1,0},{2,1},{3,2},{4,3},{5,4},{6,5},{7,6},{8,15},{9,8},{10,9... | collective-permute-start | bytes 2359304 | tf_op jit(solution)/shard_map/ppermute | solution.py:55
  110.2 31.0 %collective-permute-start.22 = (bf16[768,512]{1,0:T(8,128)(2,1)}, bf16[768,512]{1,0:T(8,128)(2,1)}, u32[]{:S(2)}, u32[]{:S(2)}) collective-permute-start(bf16[768,512]{1,0:T(8,128)(2,1)} %collective-permute-done.20), channel_id=1, source_target_pairs={{0,1},{1,2},{2,3},{3,4},{4,5},{5,6},{6,7},{7,0},{8,9},{9,10},{10,1... | collective-permute-start | bytes 2359304 | tf_op jit(solution)/shard_map/ppermute | solution.py:54
  117.2 15.4 %collective-permute-start.17 = (bf16[3,4,256]{2,1,0:T(4,128)(2,1)S(1)}, bf16[3,4,256]{2,1,0:T(4,128)(2,1)S(1)}, u32[]{:S(2)}, u32[]{:S(2)}) collective-permute-start(bf16[3,4,256]{2,1,0:T(4,128)(2,1)S(1)} %get-tuple-element.43), channel_id=1, source_target_pairs={{0,24},{8,56},{16,88},{24,120},{32,152},{40,184},{48,216},{56,248}... | collective-permute-start | bytes 18440 | tf_op jit(solution)/shard_map/ppermute | solution.py:220
  122.3 17.3 %collective-permute-start.16 = (bf16[3,4,256]{2,1,0:T(4,128)(2,1)S(1)}, bf16[3,4,256]{2,1,0:T(4,128)(2,1)S(1)}, u32[]{:S(2)}, u32[]{:S(2)}) collective-permute-start(bf16[3,4,256]{2,1,0:T(4,128)(2,1)S(1)} %get-tuple-element.44), channel_id=1, source_target_pairs={{0,16},{8,48},{16,80},{24,112},{32,144},{40,176},{48,208},{56,240}... | collective-permute-start | bytes 18440 | tf_op jit(solution)/shard_map/ppermute | solution.py:220
  129.8 9.9 %collective-permute-start.15 = (bf16[3,4,256]{2,1,0:T(4,128)(2,1)S(1)}, bf16[3,4,256]{2,1,0:T(4,128)(2,1)S(1)}, u32[]{:S(2)}, u32[]{:S(2)}) collective-permute-start(bf16[3,4,256]{2,1,0:T(4,128)(2,1)S(1)} %get-tuple-element.45), channel_id=1, source_target_pairs={{0,8},{8,40},{16,72},{24,104},{32,136},{40,168},{48,200},{56,232},... | collective-permute-start | bytes 18440 | tf_op jit(solution)/shard_map/ppermute | solution.py:220
  132.6 7.7 %collective-permute-start.14 = (bf16[3,4,256]{2,1,0:T(4,128)(2,1)S(1)}, bf16[3,4,256]{2,1,0:T(4,128)(2,1)S(1)}, u32[]{:S(2)}, u32[]{:S(2)}) collective-permute-start(bf16[3,4,256]{2,1,0:T(4,128)(2,1)S(1)} %get-tuple-element.42), channel_id=1, source_target_pairs={{0,0},{8,32},{16,64},{24,96},{32,128},{40,160},{48,192},{56,224},{... | collective-permute-start | bytes 18440 | tf_op jit(solution)/shard_map/ppermute | solution.py:220
  141.2 13.3 %collective-permute-start.25 = (bf16[384,512]{1,0:T(8,128)(2,1)}, bf16[384,512]{1,0:T(8,128)(2,1)S(1)}, u32[]{:S(2)}, u32[]{:S(2)}) collective-permute-start(bf16[384,512]{1,0:T(8,128)(2,1)} %slice.192), channel_id=1, source_target_pairs={{0,7},{1,0},{2,1},{3,2},{4,3},{5,4},{6,5},{7,6},{8,15},{9,8},{10,9... | collective-permute-start | bytes 1179656 | tf_op jit(solution)/shard_map/ppermute | solution.py:60
  142.9 11.5 %collective-permute-start.24 = (bf16[384,512]{1,0:T(8,128)(2,1)}, bf16[384,512]{1,0:T(8,128)(2,1)}, u32[]{:S(2)}, u32[]{:S(2)}) collective-permute-start(bf16[384,512]{1,0:T(8,128)(2,1)} %slice.191), channel_id=1, source_target_pairs={{0,1},{1,2},{2,3},{3,4},{4,5},{5,6},{6,7},{7,0},{8,9},{9,10},{10,1... | collective-permute-start | bytes 1179656 | tf_op jit(solution)/shard_map/ppermute | solution.py:59
  157.7 17.4 %collective-permute-start.29 = (bf16[3,4,256]{2,1,0:T(4,128)(2,1)S(1)}, bf16[3,4,256]{2,1,0:T(4,128)(2,1)S(1)}, u32[]{:S(2)}, u32[]{:S(2)}) collective-permute-start(bf16[3,4,256]{2,1,0:T(4,128)(2,1)S(1)} %squeeze.124), channel_id=1, source_target_pairs={{24,0},{56,8},{88,16},{120,24},{152,32},{184,40},{216,48},{248,56}... | collective-permute-start | bytes 18440 | tf_op jit(solution)/shard_map/ppermute | solution.py:232
  165.3 9.8 %collective-permute-start.28 = (bf16[3,4,256]{2,1,0:T(4,128)(2,1)S(1)}, bf16[3,4,256]{2,1,0:T(4,128)(2,1)S(1)}, u32[]{:S(2)}, u32[]{:S(2)}) collective-permute-start(bf16[3,4,256]{2,1,0:T(4,128)(2,1)S(1)} %squeeze.123), channel_id=1, source_target_pairs={{16,0},{48,8},{80,16},{112,24},{144,32},{176,40},{208,48},{240,56}... | collective-permute-start | bytes 18440 | tf_op jit(solution)/shard_map/ppermute | solution.py:232
  169.7 5.9 %collective-permute-start.27 = (bf16[3,4,256]{2,1,0:T(4,128)(2,1)S(1)}, bf16[3,4,256]{2,1,0:T(4,128)(2,1)S(1)}, u32[]{:S(2)}, u32[]{:S(2)}) collective-permute-start(bf16[3,4,256]{2,1,0:T(4,128)(2,1)S(1)} %squeeze.122), channel_id=1, source_target_pairs={{8,0},{40,8},{72,16},{104,24},{136,32},{168,40},{200,48},{232,56},... | collective-permute-start | bytes 18440 | tf_op jit(solution)/shard_map/ppermute | solution.py:232
  171.6 6.5 %collective-permute-start.26 = (bf16[3,4,256]{2,1,0:T(4,128)(2,1)S(1)}, bf16[3,4,256]{2,1,0:T(4,128)(2,1)S(1)}, u32[]{:S(2)}, u32[]{:S(2)}) collective-permute-start(bf16[3,4,256]{2,1,0:T(4,128)(2,1)S(1)} %squeeze.121), channel_id=1, source_target_pairs={{0,0},{32,8},{64,16},{96,24},{128,32},{160,40},{192,48},{224,56},{... | collective-permute-start | bytes 18440 | tf_op jit(solution)/shard_map/ppermute | solution.py:232
  (22 other events, 128.5 us)
Sparse Core Ops, SparseCore 0:
  23.9 58.4 all-gather.1

commit v7 on v6

--- a/solution.py
+++ b/solution.py
@@ -201,7 +201,12 @@
         contexts.append((summed / totals).astype(jnp.bfloat16))
     self_context = jnp.stack(contexts).reshape(steps * row_count, head_width)
     partial_out = jnp.dot(self_context, self_wo, preferred_element_type=jnp.float32)
-    summed_out = ring_sum(partial_out.astype(jnp.bfloat16), "head")
+    parts = partial_out.astype(jnp.bfloat16)
+    split = (steps - 1) * row_count
+    every_part = lax.all_gather(parts[:split], "head", axis=0, tiled=False)
+    early_sum = jnp.sum(every_part.astype(jnp.float32), axis=0)
+    late_sum = ring_sum(parts[split:], "head")
+    summed_out = jnp.concatenate([early_sum, late_sum], axis=0)
     residual = hidden_in + summed_out.reshape(hidden_in.shape)
     normed_cross = rms_scaled(residual, cross_gain).astype(jnp.bfloat16)
     cross_query = jnp.dot(

time: 187 us -> 207 us (1.11); the launches traced: 186 us -> 204 us
  waiting for transfers between devices: 45.4 us -> 56.9 us
  local copies, waits for them, and re-layouts: 12.6 us -> 15.2 us
  starting transfers between devices: 75.1 us -> 77.3 us
    ppermute x3, waiting for transfers between devices: 0.01 us -> 7.04 us  [ring_project(): from_right = lax.ppermute(from_right, axis, left)]
    ppermute x4, starting transfers between devices: 22.3 us -> 29.1 us  [shards(): sent.append(lax.ppermute(piece, 'hyp', route))]
    ppermute x4, starting transfers between devices: 17.3 us -> 12.4 us  [shards(): back.append(lax.ppermute(answer[shift], 'hyp', route))]
    ppermute x6, waiting for transfers between devices: 9.56 us -> 12.6 us  [beam_copies(): copies.append(lax.ppermute(block, 'hyp', route))]
    ppermute x1, starting transfers between devices: 0.01 us -> 2.89 us  [ring_project(): bottom = lax.ppermute(from_right[half:], axis, left)]
  transfers between devices with their start and end apart: 31 -> 32, of which waited for: 8 -> 10; matrix products, arithmetic and copies ran while one was open for 20% -> 17% of each run, Pallas kernels for 0% -> 0%
where the time goes in v7:
time: 207 us; the launch traced here: 204 us
  starting transfers between devices  77.3 us (37%)
  waiting for transfers between devices  56.9 us (27%)
  matrix products  20.9 us (10%)
  other arithmetic  17.9 us (9%)
  between operations  15.7 us (8%)
  local copies, waits for them, and re-layouts  15.2 us (7%)
    ppermute x3, waiting for transfers between devices, ring_sum(): from_right = lax.ppermute(from_right, axis, left)  31 us
    ppermute x4, starting transfers between devices, shards(): sent.append(lax.ppermute(piece, 'hyp', route))  29.1 us
    ppermute x6, waiting for transfers between devices, beam_copies(): copies.append(lax.ppermute(block, 'hyp', route))  12.6 us
    ppermute x4, starting transfers between devices, shards(): back.append(lax.ppermute(answer[shift], 'hyp', route))  12.4 us
    dot_general x8, matrix products, partial(): return jnp.dot(piece, w, preferred_element_type=jnp.float32)  12.4 us
    ppermute x3, starting transfers between devices, ring_project(): from_right = lax.ppermute(from_right, axis, left)  11.5 us
    ppermute x3, starting transfers between devices, ring_sum(): from_right = lax.ppermute(from_right, axis, left)  9.79 us
    ppermute x6, starting transfers between devices, beam_copies(): copies.append(lax.ppermute(block, 'hyp', route))  8.15 us
  transfers between devices with their start and end apart: 32, of which 10 were waited for; matrix products, arithmetic and copies ran while one was open for 17% of the time, Pallas kernels for 0%

profile of v7, /device:TPU:1, one launch (start us, length us, event | category | flops | bytes accessed | tf_op | source)
XLA Modules:
  0.0 203.9 jit_solution(2964979926057936688)
XLA Ops:
  11.9 2.1 %convolution_convert_fusion.3 = bf16[48,256]{1,0:T(8,128)(2,1)S(1)} fusion(bf16[48,4096]{1,0:T(8,128)(2,1)S(1)} %bitcast.291, bf16[4096,256]{1,0:T(8,128)(2,1)} %param.24), kind=kOutput, calls=%fused_computation.15 | convolution fusion | flops 100675584 | bytes 2514944 | tf_op jit(solution)/shard_map/dot_general | solution.py:150
  14.6 3.6 %collective-permute-start.3 = (bf16[2,3,16,256]{3,2,0,1:T(8,128)(2,1)S(1)}, bf16[2,3,16,256]{3,2,0,1:T(8,128)(2,1)S(1)}, u32[]{:S(2)}, u32[]{:S(2)}) collective-permute-start(bf16[2,3,16,256]{3,2,0,1:T(8,128)(2,1)S(1)} %pad_maximum_fusion.5), channel_id=1, source_target_pairs={{64,0},{72,8},{80,16},{88,24},{96,32},{104,40},{112,48},{120,56},{... | collective-permute-start | bytes 147464 | tf_op jit(solution)/shard_map/ppermute | solution.py:34
  20.4 2.0 collective-permute-start
  36.5 2.1 %convolution_convert_fusion.5 = bf16[48,256]{1,0:T(8,128)(2,1)S(1)} fusion(bf16[48,4096]{1,0:T(8,128)(2,1)S(1)} %bitcast.293, bf16[4096,256]{1,0:T(8,128)(2,1)} %param.22), kind=kOutput, calls=%fused_computation.17 | convolution fusion | flops 100675584 | bytes 2514944 | tf_op jit(solution)/shard_map/dot_general | solution.py:148
  39.0 12.5 %collective-permute-done.2 = bf16[2,16,32,256]{3,1,2,0:T(8,128)(2,1)S(1)} collective-permute-done((bf16[2,16,32,256]{3,1,2,0:T(8,128)(2,1)}, bf16[2,16,32,256]{3,1,2,0:T(8,128)(2,1)S(1)}, u32[]{:S(2)}, u32[]{:S(2)}) %collective-permute-start.2) | collective-permute-done | bytes 524320 | tf_op jit(solution)/shard_map/ppermute | solution.py:34
  58.1 5.7 %collective-permute-start.19 = (bf16[768,512]{1,0:T(8,128)(2,1)S(1)}, bf16[768,512]{1,0:T(8,128)(2,1)}, u32[]{:S(2)}, u32[]{:S(2)}) collective-permute-start(bf16[768,512]{1,0:T(8,128)(2,1)S(1)} %copy-done.6), channel_id=1, source_target_pairs={{0,7},{1,0},{2,1},{3,2},{4,3},{5,4},{6,5},{7,6},{8,15},{9,8},{10,9... | collective-permute-start | bytes 2359304 | tf_op jit(solution)/shard_map/ppermute | solution.py:55
  63.8 2.7 %collective-permute-start.7 = (bf16[16,4096]{1,0:T(8,128)(2,1)S(1)}, bf16[16,4096]{1,0:T(8,128)(2,1)}, u32[]{:S(2)}, u32[]{:S(2)}) collective-permute-start(bf16[16,4096]{1,0:T(8,128)(2,1)S(1)} %slice.198), channel_id=1, source_target_pairs={{0,7},{1,0},{2,1},{3,2},{4,3},{5,4},{6,5},{7,6},{8,15},{9,8},{10,9... | collective-permute-start | bytes 393224 | tf_op jit(solution)/shard_map/ppermute | solution.py:75
  66.5 22.3 %collective-permute-done.7 = bf16[16,4096]{1,0:T(8,128)(2,1)} collective-permute-done((bf16[16,4096]{1,0:T(8,128)(2,1)S(1)}, bf16[16,4096]{1,0:T(8,128)(2,1)}, u32[]{:S(2)}, u32[]{:S(2)}) %collective-permute-start.7) | collective-permute-done | bytes 131104 | tf_op jit(solution)/shard_map/ppermute | solution.py:75
  88.9 3.6 %collective-permute-start.9 = (bf16[16,4096]{1,0:T(8,128)(2,1)}, bf16[16,4096]{1,0:T(8,128)(2,1)}, u32[]{:S(2)}, u32[]{:S(2)}) collective-permute-start(bf16[16,4096]{1,0:T(8,128)(2,1)} %collective-permute-done.7), channel_id=1, source_target_pairs={{0,7},{1,0},{2,1},{3,2},{4,3},{5,4},{6,5},{7,6},{8,15},{9,8},{10,9... | collective-permute-start | bytes 393224 | tf_op jit(solution)/shard_map/ppermute | solution.py:75
  93.1 5.4 %collective-permute-done.9 = bf16[16,4096]{1,0:T(8,128)(2,1)} collective-permute-done((bf16[16,4096]{1,0:T(8,128)(2,1)}, bf16[16,4096]{1,0:T(8,128)(2,1)}, u32[]{:S(2)}, u32[]{:S(2)}) %collective-permute-start.9) | collective-permute-done | bytes 131104 | tf_op jit(solution)/shard_map/ppermute | solution.py:75
  98.6 3.4 %collective-permute-start.11 = (bf16[16,4096]{1,0:T(8,128)(2,1)}, bf16[16,4096]{1,0:T(8,128)(2,1)}, u32[]{:S(2)}, u32[]{:S(2)}) collective-permute-start(bf16[16,4096]{1,0:T(8,128)(2,1)} %collective-permute-done.9), channel_id=1, source_target_pairs={{0,7},{1,0},{2,1},{3,2},{4,3},{5,4},{6,5},{7,6},{8,15},{9,8},{10,9... | collective-permute-start | bytes 393224 | tf_op jit(solution)/shard_map/ppermute | solution.py:75
  103.5 3.2 %collective-permute-done.11 = bf16[16,4096]{1,0:T(8,128)(2,1)} collective-permute-done((bf16[16,4096]{1,0:T(8,128)(2,1)}, bf16[16,4096]{1,0:T(8,128)(2,1)}, u32[]{:S(2)}, u32[]{:S(2)}) %collective-permute-start.11) | collective-permute-done | bytes 131104 | tf_op jit(solution)/shard_map/ppermute | solution.py:75
  107.6 3.4 %collective-permute-start.13 = (bf16[8,4096]{1,0:T(8,128)(2,1)S(1)}, bf16[8,4096]{1,0:T(8,128)(2,1)S(1)}, u32[]{:S(2)}, u32[]{:S(2)}) collective-permute-start(bf16[8,4096]{1,0:T(8,128)(2,1)S(1)} %slice.200), channel_id=1, source_target_pairs={{0,7},{1,0},{2,1},{3,2},{4,3},{5,4},{6,5},{7,6},{8,15},{9,8},{10,9... | collective-permute-start | bytes 196616 | tf_op jit(solution)/shard_map/ppermute | solution.py:80
  111.9 2.7 %collective-permute-start.21 = (bf16[768,512]{1,0:T(8,128)(2,1)}, bf16[768,512]{1,0:T(8,128)(2,1)}, u32[]{:S(2)}, u32[]{:S(2)}) collective-permute-start(bf16[768,512]{1,0:T(8,128)(2,1)} %collective-permute-done.19), channel_id=1, source_target_pairs={{0,7},{1,0},{2,1},{3,2},{4,3},{5,4},{6,5},{7,6},{8,15},{9,8},{10,9... | collective-permute-start | bytes 2359304 | tf_op jit(solution)/shard_map/ppermute | solution.py:55
  117.6 7.0 %collective-permute-done.21 = bf16[768,512]{1,0:T(8,128)(2,1)} collective-permute-done((bf16[768,512]{1,0:T(8,128)(2,1)}, bf16[768,512]{1,0:T(8,128)(2,1)}, u32[]{:S(2)}, u32[]{:S(2)}) %collective-permute-start.21) | collective-permute-done | bytes 786464 | tf_op jit(solution)/shard_map/ppermute | solution.py:55
  124.6 3.1 %collective-permute-start.23 = (bf16[768,512]{1,0:T(8,128)(2,1)}, bf16[768,512]{1,0:T(8,128)(2,1)S(1)}, u32[]{:S(2)}, u32[]{:S(2)}) collective-permute-start(bf16[768,512]{1,0:T(8,128)(2,1)} %collective-permute-done.21), channel_id=1, source_target_pairs={{0,7},{1,0},{2,1},{3,2},{4,3},{5,4},{6,5},{7,6},{8,15},{9,8},{10,9... | collective-permute-start | bytes 2359304 | tf_op jit(solution)/shard_map/ppermute | solution.py:55
  128.0 2.0 convert_reduce_fusion
  132.2 5.0 %collective-permute-start.17 = (bf16[3,4,256]{2,1,0:T(4,128)(2,1)S(1)}, bf16[3,4,256]{2,1,0:T(4,128)(2,1)S(1)}, u32[]{:S(2)}, u32[]{:S(2)}) collective-permute-start(bf16[3,4,256]{2,1,0:T(4,128)(2,1)S(1)} %get-tuple-element.43), channel_id=1, source_target_pairs={{0,24},{8,56},{16,88},{24,120},{32,152},{40,184},{48,216},{56,248}... | collective-permute-start | bytes 18440 | tf_op jit(solution)/shard_map/ppermute | solution.py:225
  137.1 14.0 %collective-permute-start.16 = (bf16[3,4,256]{2,1,0:T(4,128)(2,1)S(1)}, bf16[3,4,256]{2,1,0:T(4,128)(2,1)S(1)}, u32[]{:S(2)}, u32[]{:S(2)}) collective-permute-start(bf16[3,4,256]{2,1,0:T(4,128)(2,1)S(1)} %get-tuple-element.44), channel_id=1, source_target_pairs={{0,16},{8,48},{16,80},{24,112},{32,144},{40,176},{48,208},{56,240}... | collective-permute-start | bytes 18440 | tf_op jit(solution)/shard_map/ppermute | solution.py:225
  151.1 1.9 collective-permute-start.15
  153.1 8.2 %collective-permute-start.14 = (bf16[3,4,256]{2,1,0:T(4,128)(2,1)S(1)}, bf16[3,4,256]{2,1,0:T(4,128)(2,1)S(1)}, u32[]{:S(2)}, u32[]{:S(2)}) collective-permute-start(bf16[3,4,256]{2,1,0:T(4,128)(2,1)S(1)} %get-tuple-element.42), channel_id=1, source_target_pairs={{0,0},{8,32},{16,64},{24,96},{32,128},{40,160},{48,192},{56,224},{... | collective-permute-start | bytes 18440 | tf_op jit(solution)/shard_map/ppermute | solution.py:225
  162.2 2.9 %collective-permute-start.25 = (bf16[384,512]{1,0:T(8,128)(2,1)}, bf16[384,512]{1,0:T(8,128)(2,1)S(1)}, u32[]{:S(2)}, u32[]{:S(2)}) collective-permute-start(bf16[384,512]{1,0:T(8,128)(2,1)} %slice.202), channel_id=1, source_target_pairs={{0,7},{1,0},{2,1},{3,2},{4,3},{5,4},{6,5},{7,6},{8,15},{9,8},{10,9... | collective-permute-start | bytes 1179656 | tf_op jit(solution)/shard_map/ppermute | solution.py:60
  165.0 1.8 slice.201
  167.0 2.1 %fusion.12 = f32[512,768]{1,0:T(8,128)S(1)} fusion(bf16[768,512]{1,0:T(8,128)(2,1)} %collective-permute-done.22, bf16[4096,512]{1,0:T(8,128)(2,1)} %all-gather.4.cloned.1.call-done, s32[]{:T(128)S(6)} %select_n.409), kind=kOutput, calls=%fused_computation.37 | convolution fusion | flops 402653184 | bytes 2883588 | tf_op jit(solution)/shard_map/dot_general | solution.py:48
  169.0 1.9 fusion.14
  172.7 1.8 fusion.18
  175.2 1.8 fusion.20
  180.3 4.8 %collective-permute-start.29 = (bf16[3,4,256]{2,1,0:T(4,128)(2,1)S(1)}, bf16[3,4,256]{2,1,0:T(4,128)(2,1)S(1)}, u32[]{:S(2)}, u32[]{:S(2)}) collective-permute-start(bf16[3,4,256]{2,1,0:T(4,128)(2,1)S(1)} %squeeze.124), channel_id=1, source_target_pairs={{24,0},{56,8},{88,16},{120,24},{152,32},{184,40},{216,48},{248,56}... | collective-permute-start | bytes 18440 | tf_op jit(solution)/shard_map/ppermute | solution.py:237
  185.1 2.2 %collective-permute-start.28 = (bf16[3,4,256]{2,1,0:T(4,128)(2,1)S(1)}, bf16[3,4,256]{2,1,0:T(4,128)(2,1)S(1)}, u32[]{:S(2)}, u32[]{:S(2)}) collective-permute-start(bf16[3,4,256]{2,1,0:T(4,128)(2,1)S(1)} %squeeze.123), channel_id=1, source_target_pairs={{16,0},{48,8},{80,16},{112,24},{144,32},{176,40},{208,48},{240,56}... | collective-permute-start | bytes 18440 | tf_op jit(solution)/shard_map/ppermute | solution.py:237
  187.3 1.9 collective-permute-start.27
  189.2 3.5 %collective-permute-start.26 = (bf16[3,4,256]{2,1,0:T(4,128)(2,1)S(1)}, bf16[3,4,256]{2,1,0:T(4,128)(2,1)S(1)}, u32[]{:S(2)}, u32[]{:S(2)}) collective-permute-start(bf16[3,4,256]{2,1,0:T(4,128)(2,1)S(1)} %squeeze.121), channel_id=1, source_target_pairs={{0,0},{32,8},{64,16},{96,24},{128,32},{160,40},{192,48},{224,56},{... | collective-permute-start | bytes 18440 | tf_op jit(solution)/shard_map/ppermute | solution.py:237
  193.2 2.5 %collective-permute-done.26 = bf16[3,4,256]{2,1,0:T(4,128)(2,1)S(1)} collective-permute-done((bf16[3,4,256]{2,1,0:T(4,128)(2,1)S(1)}, bf16[3,4,256]{2,1,0:T(4,128)(2,1)S(1)}, u32[]{:S(2)}, u32[]{:S(2)}) %collective-permute-start.26) | collective-permute-done | bytes 6176 | tf_op jit(solution)/shard_map/ppermute | solution.py:237
  (185 shorter events, 44.9 us)
Async XLA Ops:
  7.2 120.8 %all-gather.6.cloned.1.call-start = ((), (), s32[]{:S(2)}) async-start(), calls=%async_computation.1 | async-start | bytes 2359296 | tf_op jit(solution)/shard_map/all_gather | solution.py:206
  14.6 24.1 %collective-permute-start.3 = (bf16[2,3,16,256]{3,2,0,1:T(8,128)(2,1)S(1)}, bf16[2,3,16,256]{3,2,0,1:T(8,128)(2,1)S(1)}, u32[]{:S(2)}, u32[]{:S(2)}) collective-permute-start(bf16[2,3,16,256]{3,2,0,1:T(8,128)(2,1)S(1)} %pad_maximum_fusion.5), channel_id=1, source_target_pairs={{64,0},{72,8},{80,16},{88,24},{96,32},{104,40},{112,48},{120,56},{... | collective-permute-start | bytes 147464 | tf_op jit(solution)/shard_map/ppermute | solution.py:34
  18.2 20.6 %collective-permute-start.4 = (bf16[2,3,16,256]{3,2,0,1:T(8,128)(2,1)S(1)}, bf16[2,3,16,256]{3,2,0,1:T(8,128)(2,1)S(1)}, u32[]{:S(2)}, u32[]{:S(2)}) collective-permute-start(bf16[2,3,16,256]{3,2,0,1:T(8,128)(2,1)S(1)} %pad_maximum_fusion.5), channel_id=1, source_target_pairs={{128,0},{136,8},{144,16},{152,24},{160,32},{168,40},{176,48},{184,... | collective-permute-start | bytes 147464 | tf_op jit(solution)/shard_map/ppermute | solution.py:34
  18.5 20.2 %collective-permute-start.5 = (bf16[2,3,16,256]{3,2,0,1:T(8,128)(2,1)S(1)}, bf16[2,3,16,256]{3,2,0,1:T(8,128)(2,1)S(1)}, u32[]{:S(2)}, u32[]{:S(2)}) collective-permute-start(bf16[2,3,16,256]{3,2,0,1:T(8,128)(2,1)S(1)} %pad_maximum_fusion.5), channel_id=1, source_target_pairs={{192,0},{200,8},{208,16},{216,24},{224,32},{232,40},{240,48},{248,... | collective-permute-start | bytes 147464 | tf_op jit(solution)/shard_map/ppermute | solution.py:34
  20.4 18.6 %collective-permute-start = (bf16[2,16,32,256]{3,1,2,0:T(8,128)(2,1)}, bf16[2,16,32,256]{3,1,2,0:T(8,128)(2,1)}, u32[]{:S(2)}, u32[]{:S(2)}) collective-permute-start(bf16[2,16,32,256]{3,1,2,0:T(8,128)(2,1)} %pad_maximum_fusion.3), channel_id=1, source_target_pairs={{64,0},{72,8},{80,16},{88,24},{96,32},{104,40},{112,48},{120,56},{... | collective-permute-start | bytes 1572872 | tf_op jit(solution)/shard_map/ppermute | solution.py:34
  22.4 16.6 %collective-permute-start.1 = (bf16[2,16,32,256]{3,1,2,0:T(8,128)(2,1)}, bf16[2,16,32,256]{3,1,2,0:T(8,128)(2,1)}, u32[]{:S(2)}, u32[]{:S(2)}) collective-permute-start(bf16[2,16,32,256]{3,1,2,0:T(8,128)(2,1)} %pad_maximum_fusion.3), channel_id=1, source_target_pairs={{128,0},{136,8},{144,16},{152,24},{160,32},{168,40},{176,48},{184,... | collective-permute-start | bytes 1572872 | tf_op jit(solution)/shard_map/ppermute | solution.py:34
  38.6 12.9 %collective-permute-start.2 = (bf16[2,16,32,256]{3,1,2,0:T(8,128)(2,1)}, bf16[2,16,32,256]{3,1,2,0:T(8,128)(2,1)S(1)}, u32[]{:S(2)}, u32[]{:S(2)}) collective-permute-start(bf16[2,16,32,256]{3,1,2,0:T(8,128)(2,1)} %pad_maximum_fusion.3), channel_id=1, source_target_pairs={{192,0},{200,8},{208,16},{216,24},{224,32},{232,40},{240,48},{248,... | collective-permute-start | bytes 1572872 | tf_op jit(solution)/shard_map/ppermute | solution.py:34
  57.3 109.6 %all-gather.4.cloned.1.call-start = ((), (), s32[]{:S(2)}) async-start(), calls=%async_computation | async-start | bytes 4325376 | tf_op jit(solution)/shard_map/all_gather | solution.py:129
  58.1 53.8 %collective-permute-start.19 = (bf16[768,512]{1,0:T(8,128)(2,1)S(1)}, bf16[768,512]{1,0:T(8,128)(2,1)}, u32[]{:S(2)}, u32[]{:S(2)}) collective-permute-start(bf16[768,512]{1,0:T(8,128)(2,1)S(1)} %copy-done.6), channel_id=1, source_target_pairs={{0,7},{1,0},{2,1},{3,2},{4,3},{5,4},{6,5},{7,6},{8,15},{9,8},{10,9... | collective-permute-start | bytes 2359304 | tf_op jit(solution)/shard_map/ppermute | solution.py:55
  63.7 50.9 %collective-permute-start.18 = (bf16[768,512]{1,0:T(8,128)(2,1)S(1)}, bf16[768,512]{1,0:T(8,128)(2,1)}, u32[]{:S(2)}, u32[]{:S(2)}) collective-permute-start(bf16[768,512]{1,0:T(8,128)(2,1)S(1)} %copy-done.6), channel_id=1, source_target_pairs={{0,1},{1,2},{2,3},{3,4},{4,5},{5,6},{6,7},{7,0},{8,9},{9,10},{10,1... | collective-permute-start | bytes 2359304 | tf_op jit(solution)/shard_map/ppermute | solution.py:54
  63.8 25.1 %collective-permute-start.7 = (bf16[16,4096]{1,0:T(8,128)(2,1)S(1)}, bf16[16,4096]{1,0:T(8,128)(2,1)}, u32[]{:S(2)}, u32[]{:S(2)}) collective-permute-start(bf16[16,4096]{1,0:T(8,128)(2,1)S(1)} %slice.198), channel_id=1, source_target_pairs={{0,7},{1,0},{2,1},{3,2},{4,3},{5,4},{6,5},{7,6},{8,15},{9,8},{10,9... | collective-permute-start | bytes 393224 | tf_op jit(solution)/shard_map/ppermute | solution.py:75
  66.5 26.0 %collective-permute-start.6 = (bf16[16,4096]{1,0:T(8,128)(2,1)S(1)}, bf16[16,4096]{1,0:T(8,128)(2,1)S(1)}, u32[]{:S(2)}, u32[]{:S(2)}) collective-permute-start(bf16[16,4096]{1,0:T(8,128)(2,1)S(1)} %slice.198), channel_id=1, source_target_pairs={{0,1},{1,2},{2,3},{3,4},{4,5},{5,6},{6,7},{7,0},{8,9},{9,10},{10,1... | collective-permute-start | bytes 393224 | tf_op jit(solution)/shard_map/ppermute | solution.py:74
  88.9 9.7 %collective-permute-start.9 = (bf16[16,4096]{1,0:T(8,128)(2,1)}, bf16[16,4096]{1,0:T(8,128)(2,1)}, u32[]{:S(2)}, u32[]{:S(2)}) collective-permute-start(bf16[16,4096]{1,0:T(8,128)(2,1)} %collective-permute-done.7), channel_id=1, source_target_pairs={{0,7},{1,0},{2,1},{3,2},{4,3},{5,4},{6,5},{7,6},{8,15},{9,8},{10,9... | collective-permute-start | bytes 393224 | tf_op jit(solution)/shard_map/ppermute | solution.py:75
  93.1 9.6 %collective-permute-start.8 = (bf16[16,4096]{1,0:T(8,128)(2,1)S(1)}, bf16[16,4096]{1,0:T(8,128)(2,1)}, u32[]{:S(2)}, u32[]{:S(2)}) collective-permute-start(bf16[16,4096]{1,0:T(8,128)(2,1)S(1)} %collective-permute-done.6), channel_id=1, source_target_pairs={{0,1},{1,2},{2,3},{3,4},{4,5},{5,6},{6,7},{7,0},{8,9},{9,10},{10,1... | collective-permute-start | bytes 393224 | tf_op jit(solution)/shard_map/ppermute | solution.py:74
  98.6 8.2 %collective-permute-start.11 = (bf16[16,4096]{1,0:T(8,128)(2,1)}, bf16[16,4096]{1,0:T(8,128)(2,1)}, u32[]{:S(2)}, u32[]{:S(2)}) collective-permute-start(bf16[16,4096]{1,0:T(8,128)(2,1)} %collective-permute-done.9), channel_id=1, source_target_pairs={{0,7},{1,0},{2,1},{3,2},{4,3},{5,4},{6,5},{7,6},{8,15},{9,8},{10,9... | collective-permute-start | bytes 393224 | tf_op jit(solution)/shard_map/ppermute | solution.py:75
  102.8 8.3 %collective-permute-start.10 = (bf16[16,4096]{1,0:T(8,128)(2,1)}, bf16[16,4096]{1,0:T(8,128)(2,1)}, u32[]{:S(2)}, u32[]{:S(2)}) collective-permute-start(bf16[16,4096]{1,0:T(8,128)(2,1)} %collective-permute-done.8), channel_id=1, source_target_pairs={{0,1},{1,2},{2,3},{3,4},{4,5},{5,6},{6,7},{7,0},{8,9},{9,10},{10,1... | collective-permute-start | bytes 393224 | tf_op jit(solution)/shard_map/ppermute | solution.py:74
  107.6 7.0 %collective-permute-start.13 = (bf16[8,4096]{1,0:T(8,128)(2,1)S(1)}, bf16[8,4096]{1,0:T(8,128)(2,1)S(1)}, u32[]{:S(2)}, u32[]{:S(2)}) collective-permute-start(bf16[8,4096]{1,0:T(8,128)(2,1)S(1)} %slice.200), channel_id=1, source_target_pairs={{0,7},{1,0},{2,1},{3,2},{4,3},{5,4},{6,5},{7,6},{8,15},{9,8},{10,9... | collective-permute-start | bytes 196616 | tf_op jit(solution)/shard_map/ppermute | solution.py:80
  111.9 4.3 %collective-permute-start.12 = (bf16[8,4096]{1,0:T(8,128)(2,1)S(1)}, bf16[8,4096]{1,0:T(8,128)(2,1)S(1)}, u32[]{:S(2)}, u32[]{:S(2)}) collective-permute-start(bf16[8,4096]{1,0:T(8,128)(2,1)S(1)} %slice.199), channel_id=1, source_target_pairs={{0,1},{1,2},{2,3},{3,4},{4,5},{5,6},{6,7},{7,0},{8,9},{9,10},{10,1... | collective-permute-start | bytes 196616 | tf_op jit(solution)/shard_map/ppermute | solution.py:79
  111.9 12.7 %collective-permute-start.21 = (bf16[768,512]{1,0:T(8,128)(2,1)}, bf16[768,512]{1,0:T(8,128)(2,1)}, u32[]{:S(2)}, u32[]{:S(2)}) collective-permute-start(bf16[768,512]{1,0:T(8,128)(2,1)} %collective-permute-done.19), channel_id=1, source_target_pairs={{0,7},{1,0},{2,1},{3,2},{4,3},{5,4},{6,5},{7,6},{8,15},{9,8},{10,9... | collective-permute-start | bytes 2359304 | tf_op jit(solution)/shard_map/ppermute | solution.py:55
  114.7 13.4 %collective-permute-start.20 = (bf16[768,512]{1,0:T(8,128)(2,1)}, bf16[768,512]{1,0:T(8,128)(2,1)}, u32[]{:S(2)}, u32[]{:S(2)}) collective-permute-start(bf16[768,512]{1,0:T(8,128)(2,1)} %collective-permute-done.18), channel_id=1, source_target_pairs={{0,1},{1,2},{2,3},{3,4},{4,5},{5,6},{6,7},{7,0},{8,9},{9,10},{10,1... | collective-permute-start | bytes 2359304 | tf_op jit(solution)/shard_map/ppermute | solution.py:54
  124.6 28.5 %collective-permute-start.23 = (bf16[768,512]{1,0:T(8,128)(2,1)}, bf16[768,512]{1,0:T(8,128)(2,1)S(1)}, u32[]{:S(2)}, u32[]{:S(2)}) collective-permute-start(bf16[768,512]{1,0:T(8,128)(2,1)} %collective-permute-done.21), channel_id=1, source_target_pairs={{0,7},{1,0},{2,1},{3,2},{4,3},{5,4},{6,5},{7,6},{8,15},{9,8},{10,9... | collective-permute-start | bytes 2359304 | tf_op jit(solution)/shard_map/ppermute | solution.py:55
  128.0 34.1 %collective-permute-start.22 = (bf16[768,512]{1,0:T(8,128)(2,1)}, bf16[768,512]{1,0:T(8,128)(2,1)}, u32[]{:S(2)}, u32[]{:S(2)}) collective-permute-start(bf16[768,512]{1,0:T(8,128)(2,1)} %collective-permute-done.20), channel_id=1, source_target_pairs={{0,1},{1,2},{2,3},{3,4},{4,5},{5,6},{6,7},{7,0},{8,9},{9,10},{10,1... | collective-permute-start | bytes 2359304 | tf_op jit(solution)/shard_map/ppermute | solution.py:54
  132.2 34.7 %collective-permute-start.17 = (bf16[3,4,256]{2,1,0:T(4,128)(2,1)S(1)}, bf16[3,4,256]{2,1,0:T(4,128)(2,1)S(1)}, u32[]{:S(2)}, u32[]{:S(2)}) collective-permute-start(bf16[3,4,256]{2,1,0:T(4,128)(2,1)S(1)} %get-tuple-element.43), channel_id=1, source_target_pairs={{0,24},{8,56},{16,88},{24,120},{32,152},{40,184},{48,216},{56,248}... | collective-permute-start | bytes 18440 | tf_op jit(solution)/shard_map/ppermute | solution.py:225
  137.1 29.7 %collective-permute-start.16 = (bf16[3,4,256]{2,1,0:T(4,128)(2,1)S(1)}, bf16[3,4,256]{2,1,0:T(4,128)(2,1)S(1)}, u32[]{:S(2)}, u32[]{:S(2)}) collective-permute-start(bf16[3,4,256]{2,1,0:T(4,128)(2,1)S(1)} %get-tuple-element.44), channel_id=1, source_target_pairs={{0,16},{8,48},{16,80},{24,112},{32,144},{40,176},{48,208},{56,240}... | collective-permute-start | bytes 18440 | tf_op jit(solution)/shard_map/ppermute | solution.py:225
  151.1 15.7 %collective-permute-start.15 = (bf16[3,4,256]{2,1,0:T(4,128)(2,1)S(1)}, bf16[3,4,256]{2,1,0:T(4,128)(2,1)S(1)}, u32[]{:S(2)}, u32[]{:S(2)}) collective-permute-start(bf16[3,4,256]{2,1,0:T(4,128)(2,1)S(1)} %get-tuple-element.45), channel_id=1, source_target_pairs={{0,8},{8,40},{16,72},{24,104},{32,136},{40,168},{48,200},{56,232},... | collective-permute-start | bytes 18440 | tf_op jit(solution)/shard_map/ppermute | solution.py:225
  153.1 13.8 %collective-permute-start.14 = (bf16[3,4,256]{2,1,0:T(4,128)(2,1)S(1)}, bf16[3,4,256]{2,1,0:T(4,128)(2,1)S(1)}, u32[]{:S(2)}, u32[]{:S(2)}) collective-permute-start(bf16[3,4,256]{2,1,0:T(4,128)(2,1)S(1)} %get-tuple-element.42), channel_id=1, source_target_pairs={{0,0},{8,32},{16,64},{24,96},{32,128},{40,160},{48,192},{56,224},{... | collective-permute-start | bytes 18440 | tf_op jit(solution)/shard_map/ppermute | solution.py:225
  162.2 14.8 %collective-permute-start.25 = (bf16[384,512]{1,0:T(8,128)(2,1)}, bf16[384,512]{1,0:T(8,128)(2,1)S(1)}, u32[]{:S(2)}, u32[]{:S(2)}) collective-permute-start(bf16[384,512]{1,0:T(8,128)(2,1)} %slice.202), channel_id=1, source_target_pairs={{0,7},{1,0},{2,1},{3,2},{4,3},{5,4},{6,5},{7,6},{8,15},{9,8},{10,9... | collective-permute-start | bytes 1179656 | tf_op jit(solution)/shard_map/ppermute | solution.py:60
  166.8 10.1 %collective-permute-start.24 = (bf16[384,512]{1,0:T(8,128)(2,1)}, bf16[384,512]{1,0:T(8,128)(2,1)}, u32[]{:S(2)}, u32[]{:S(2)}) collective-permute-start(bf16[384,512]{1,0:T(8,128)(2,1)} %slice.201), channel_id=1, source_target_pairs={{0,1},{1,2},{2,3},{3,4},{4,5},{5,6},{6,7},{7,0},{8,9},{9,10},{10,1... | collective-permute-start | bytes 1179656 | tf_op jit(solution)/shard_map/ppermute | solution.py:59
  180.3 12.5 %collective-permute-start.29 = (bf16[3,4,256]{2,1,0:T(4,128)(2,1)S(1)}, bf16[3,4,256]{2,1,0:T(4,128)(2,1)S(1)}, u32[]{:S(2)}, u32[]{:S(2)}) collective-permute-start(bf16[3,4,256]{2,1,0:T(4,128)(2,1)S(1)} %squeeze.124), channel_id=1, source_target_pairs={{24,0},{56,8},{88,16},{120,24},{152,32},{184,40},{216,48},{248,56}... | collective-permute-start | bytes 18440 | tf_op jit(solution)/shard_map/ppermute | solution.py:237
  185.1 7.7 %collective-permute-start.28 = (bf16[3,4,256]{2,1,0:T(4,128)(2,1)S(1)}, bf16[3,4,256]{2,1,0:T(4,128)(2,1)S(1)}, u32[]{:S(2)}, u32[]{:S(2)}) collective-permute-start(bf16[3,4,256]{2,1,0:T(4,128)(2,1)S(1)} %squeeze.123), channel_id=1, source_target_pairs={{16,0},{48,8},{80,16},{112,24},{144,32},{176,40},{208,48},{240,56}... | collective-permute-start | bytes 18440 | tf_op jit(solution)/shard_map/ppermute | solution.py:237
  187.3 5.9 %collective-permute-start.27 = (bf16[3,4,256]{2,1,0:T(4,128)(2,1)S(1)}, bf16[3,4,256]{2,1,0:T(4,128)(2,1)S(1)}, u32[]{:S(2)}, u32[]{:S(2)}) collective-permute-start(bf16[3,4,256]{2,1,0:T(4,128)(2,1)S(1)} %squeeze.122), channel_id=1, source_target_pairs={{8,0},{40,8},{72,16},{104,24},{136,32},{168,40},{200,48},{232,56},... | collective-permute-start | bytes 18440 | tf_op jit(solution)/shard_map/ppermute | solution.py:237
  189.2 6.5 %collective-permute-start.26 = (bf16[3,4,256]{2,1,0:T(4,128)(2,1)S(1)}, bf16[3,4,256]{2,1,0:T(4,128)(2,1)S(1)}, u32[]{:S(2)}, u32[]{:S(2)}) collective-permute-start(bf16[3,4,256]{2,1,0:T(4,128)(2,1)S(1)} %squeeze.121), channel_id=1, source_target_pairs={{0,0},{32,8},{64,16},{96,24},{128,32},{160,40},{192,48},{224,56},{... | collective-permute-start | bytes 18440 | tf_op jit(solution)/shard_map/ppermute | solution.py:237
  (20 other events, 113.0 us)
Sparse Core Ops, SparseCore 0:
  57.4 51.8 all-gather.5
  111.9 49.9 all-gather.3

commit v8 on v5

--- a/solution.py
+++ b/solution.py
@@ -200,18 +200,16 @@
         ]
         piece = lax.dynamic_index_in_dim(by_doc, (my_beam + shift) % BEAMS, 1, keepdims=False)
         sent.append(lax.ppermute(piece, "hyp", route))
-    doc_queries = jnp.stack(sent).reshape(BEAMS * steps * TARGETS, head_width)
-    answer = cross_attend(doc_queries, cross_keys, cross_values, doc_length, scaling)
-    answer = answer.reshape(BEAMS, steps, TARGETS, head_width)
-
     back = []
     for shift in range(BEAMS):
+        message = sent[shift].reshape(steps * TARGETS, head_width)
+        answer = cross_attend(message, cross_keys, cross_values, doc_length, scaling)
         route = [
             (slot * docs_here + (beam + shift) % BEAMS, beam * group_size + slot)
             for beam in range(BEAMS)
             for slot in range(group_size)
         ]
-        back.append(lax.ppermute(answer[shift], "hyp", route))
+        back.append(lax.ppermute(answer.reshape(steps, TARGETS, head_width), "hyp", route))
     back = jnp.stack(back)
     order = (jnp.arange(docs_here, dtype=jnp.int32) - my_beam) % BEAMS
     by_k = jnp.take(back, order, axis=0)

time: 220 us -> 222 us (level)
  transfers between devices with their start and end apart: 24 -> 24, of which waited for: 6 -> 6; matrix products, arithmetic and copies ran while one was open for 13% -> 14% of each run, Pallas kernels for 0% -> 0%
where the time goes in v8:
time: 222 us; the launch traced here: 219 us
  waiting for transfers between devices  96.6 us (44%)
  starting transfers between devices  56.5 us (25%)
  matrix products  23.1 us (10%)
  between operations  15.7 us (7%)
  other arithmetic  14.5 us (7%)
  local copies, waits for them, and re-layouts  12.3 us (6%)
    ppermute x3, waiting for transfers between devices, ring_project(): from_right = lax.ppermute(from_right, axis, left)  52.3 us
    all_gather x1, waiting for transfers between devices, shards(): full_weights = lax.all_gather(cross_wkv, 'hyp', axis=0, tiled=True)  24.3 us
    ppermute x4, starting transfers between devices, shards(): sent.append(lax.ppermute(piece, 'hyp', route))  18.3 us
    ppermute x4, starting transfers between devices, shards(): lax.ppermute(answer.reshape(steps, TARGETS, head_width), 'hyp', route)  14.4 us
    ppermute x3, starting transfers between devices, ring_project(): from_right = lax.ppermute(from_right, axis, left)  12.6 us
    ppermute x6, waiting for transfers between devices, beam_copies(): copies.append(lax.ppermute(block, 'hyp', route))  12.6 us
    dot_general x8, matrix products, partial(): return jnp.dot(piece, w, preferred_element_type=jnp.float32)  12.4 us
    ppermute x6, starting transfers between devices, beam_copies(): copies.append(lax.ppermute(block, 'hyp', route))  8.15 us
  transfers between devices with their start and end apart: 24, of which 6 were waited for; matrix products, arithmetic and copies ran while one was open for 14% of the time, Pallas kernels for 0%

profile of v8, /device:TPU:1, one launch (start us, length us, event | category | flops | bytes accessed | tf_op | source)
XLA Modules:
  0.0 218.7 jit_solution(18371828452863911195)
XLA Ops:
  9.4 1.3 multiply_reduce_fusion.1
  11.9 2.1 convolution_convert_fusion.2
  14.6 3.6 %collective-permute-start.3 = (bf16[2,3,16,256]{3,2,0,1:T(8,128)(2,1)S(1)}, bf16[2,3,16,256]{3,2,0,1:T(8,128)(2,1)S(1)}, u32[]{:S(2)}, u32[]{:S(2)}) collective-permute-start(bf16[2,3,16,256]{3,2,0,1:T(8,128)(2,1)S(1)} %pad_maximum_fusion.4), channel_id=1, source_target_pairs={{64,0},{72,8},{80,16},{88,24},{96,32},{104,40},{112,48},{120,56},{... | collective-permute-start | bytes 147464 | tf_op jit(solution)/shard_map/ppermute | solution.py:34
  20.4 2.0 collective-permute-start
  22.4 1.4 collective-permute-start.1
  33.4 2.1 convolution_convert_fusion.4
  35.9 12.5 %collective-permute-done.2 = bf16[2,16,32,256]{3,1,2,0:T(8,128)(2,1)S(1)} collective-permute-done((bf16[2,16,32,256]{3,1,2,0:T(8,128)(2,1)}, bf16[2,16,32,256]{3,1,2,0:T(8,128)(2,1)S(1)}, u32[]{:S(2)}, u32[]{:S(2)}) %collective-permute-start.2) | collective-permute-done | bytes 524320 | tf_op jit(solution)/shard_map/ppermute | solution.py:34
  48.4 1.5 select_select_fusion.2
  55.0 5.7 %collective-permute-start.8 = (bf16[768,512]{1,0:T(8,128)(2,1)S(1)}, bf16[768,512]{1,0:T(8,128)(2,1)}, u32[]{:S(2)}, u32[]{:S(2)}) collective-permute-start(bf16[768,512]{1,0:T(8,128)(2,1)S(1)} %copy-done.8), channel_id=1, source_target_pairs={{0,7},{1,0},{2,1},{3,2},{4,3},{5,4},{6,5},{7,6},{8,15},{9,8},{10,9... | collective-permute-start | bytes 2359304 | tf_op jit(solution)/shard_map/ppermute | solution.py:55
  60.7 20.1 %collective-permute-done.8 = bf16[768,512]{1,0:T(8,128)(2,1)} collective-permute-done((bf16[768,512]{1,0:T(8,128)(2,1)S(1)}, bf16[768,512]{1,0:T(8,128)(2,1)}, u32[]{:S(2)}, u32[]{:S(2)}) %collective-permute-start.8) | collective-permute-done | bytes 786464 | tf_op jit(solution)/shard_map/ppermute | solution.py:55
  80.8 3.5 %collective-permute-start.10 = (bf16[768,512]{1,0:T(8,128)(2,1)}, bf16[768,512]{1,0:T(8,128)(2,1)}, u32[]{:S(2)}, u32[]{:S(2)}) collective-permute-start(bf16[768,512]{1,0:T(8,128)(2,1)} %collective-permute-done.8), channel_id=1, source_target_pairs={{0,7},{1,0},{2,1},{3,2},{4,3},{5,4},{6,5},{7,6},{8,15},{9,8},{10,9... | collective-permute-start | bytes 2359304 | tf_op jit(solution)/shard_map/ppermute | solution.py:55
  85.0 32.1 %collective-permute-done.10 = bf16[768,512]{1,0:T(8,128)(2,1)} collective-permute-done((bf16[768,512]{1,0:T(8,128)(2,1)}, bf16[768,512]{1,0:T(8,128)(2,1)}, u32[]{:S(2)}, u32[]{:S(2)}) %collective-permute-start.10) | collective-permute-done | bytes 786464 | tf_op jit(solution)/shard_map/ppermute | solution.py:55
  117.2 3.4 %collective-permute-start.12 = (bf16[768,512]{1,0:T(8,128)(2,1)}, bf16[768,512]{1,0:T(8,128)(2,1)S(1)}, u32[]{:S(2)}, u32[]{:S(2)}) collective-permute-start(bf16[768,512]{1,0:T(8,128)(2,1)} %collective-permute-done.10), channel_id=1, source_target_pairs={{0,7},{1,0},{2,1},{3,2},{4,3},{5,4},{6,5},{7,6},{8,15},{9,8},{10,9... | collective-permute-start | bytes 2359304 | tf_op jit(solution)/shard_map/ppermute | solution.py:55
  120.6 6.0 %all-gather.6.cloned.1.call-done = bf16[384,4096]{1,0:T(8,128)(2,1)} async-done(((bf16[48,4096]{1,0:T(8,128)(2,1)}), bf16[384,4096]{1,0:T(8,128)(2,1)}) %all-gather.6.cloned.1.call-update) | async-done | bytes 3145744 | tf_op jit(solution)/shard_map/all_gather | solution.py:185
  126.6 2.4 %convert_reduce_fusion = f32[48,4096]{1,0:T(8,128)S(1)} fusion(bf16[8,48,4096]{2,1,0:T(8,128)(2,1)} %bitcast.313), kind=kLoop, calls=%fused_computation.7 | loop fusion | flops 2949120 | bytes 3932160 | tf_op jit(solution)/shard_map/reduce_sum | solution.py:186
  131.2 4.3 %collective-permute-start.20 = (bf16[3,4,256]{2,1,0:T(4,128)(2,1)S(1)}, bf16[3,4,256]{2,1,0:T(4,128)(2,1)S(1)}, u32[]{:S(2)}, u32[]{:S(2)}) collective-permute-start(bf16[3,4,256]{2,1,0:T(4,128)(2,1)S(1)} %get-tuple-element.39), channel_id=1, source_target_pairs={{0,24},{8,56},{16,88},{24,120},{32,152},{40,184},{48,216},{56,248}... | collective-permute-start | bytes 18440 | tf_op jit(solution)/shard_map/ppermute | solution.py:202
  135.5 4.3 %collective-permute-start.18 = (bf16[3,4,256]{2,1,0:T(4,128)(2,1)S(1)}, bf16[3,4,256]{2,1,0:T(4,128)(2,1)S(1)}, u32[]{:S(2)}, u32[]{:S(2)}) collective-permute-start(bf16[3,4,256]{2,1,0:T(4,128)(2,1)S(1)} %get-tuple-element.40), channel_id=1, source_target_pairs={{0,16},{8,48},{16,80},{24,112},{32,144},{40,176},{48,208},{56,240}... | collective-permute-start | bytes 18440 | tf_op jit(solution)/shard_map/ppermute | solution.py:202
  139.8 3.2 %collective-permute-start.16 = (bf16[3,4,256]{2,1,0:T(4,128)(2,1)S(1)}, bf16[3,4,256]{2,1,0:T(4,128)(2,1)S(1)}, u32[]{:S(2)}, u32[]{:S(2)}) collective-permute-start(bf16[3,4,256]{2,1,0:T(4,128)(2,1)S(1)} %get-tuple-element.41), channel_id=1, source_target_pairs={{0,8},{8,40},{16,72},{24,104},{32,136},{40,168},{48,200},{56,232},... | collective-permute-start | bytes 18440 | tf_op jit(solution)/shard_map/ppermute | solution.py:202
  143.1 6.5 %collective-permute-start.6 = (bf16[3,4,256]{2,1,0:T(4,128)(2,1)S(1)}, bf16[3,4,256]{2,1,0:T(4,128)(2,1)S(1)}, u32[]{:S(2)}, u32[]{:S(2)}) collective-permute-start(bf16[3,4,256]{2,1,0:T(4,128)(2,1)S(1)} %get-tuple-element.38), channel_id=1, source_target_pairs={{0,0},{8,32},{16,64},{24,96},{32,128},{40,160},{48,192},{56,224},{... | collective-permute-start | bytes 18440 | tf_op jit(solution)/shard_map/ppermute | solution.py:202
  150.5 2.9 %collective-permute-start.14 = (bf16[384,512]{1,0:T(8,128)(2,1)}, bf16[384,512]{1,0:T(8,128)(2,1)S(1)}, u32[]{:S(2)}, u32[]{:S(2)}) collective-permute-start(bf16[384,512]{1,0:T(8,128)(2,1)} %slice.162), channel_id=1, source_target_pairs={{0,7},{1,0},{2,1},{3,2},{4,3},{5,4},{6,5},{7,6},{8,15},{9,8},{10,9... | collective-permute-start | bytes 1179656 | tf_op jit(solution)/shard_map/ppermute | solution.py:60
  153.4 1.8 slice.161
  155.3 24.3 %all-gather.4.cloned.1.call-done = bf16[4096,512]{1,0:T(8,128)(2,1)} async-done(((bf16[128,512]{1,0:T(8,128)(2,1)}), bf16[4096,512]{1,0:T(8,128)(2,1)}) %all-gather.4.cloned.1.call-update) | async-done | bytes 4194320 | tf_op jit(solution)/shard_map/all_gather | solution.py:110
  179.6 2.1 fusion.15
  181.7 1.9 fusion.17
  183.6 1.8 fusion.19
  185.4 1.8 fusion.21
  187.9 1.8 fusion.23
  189.7 1.7 fusion.5
  193.0 3.8 %collective-permute-start.21 = (bf16[3,4,256]{2,1,0:T(4,128)(2,1)S(1)}, bf16[3,4,256]{2,1,0:T(4,128)(2,1)S(1)}, u32[]{:S(2)}, u32[]{:S(2)}) collective-permute-start(bf16[3,4,256]{2,1,0:T(4,128)(2,1)S(1)} %reshape.480), channel_id=1, source_target_pairs={{24,0},{56,8},{88,16},{120,24},{152,32},{184,40},{216,48},{248,56}... | collective-permute-start | bytes 18440 | tf_op jit(solution)/shard_map/ppermute | solution.py:212
  197.6 2.5 %collective-permute-start.19 = (bf16[3,4,256]{2,1,0:T(4,128)(2,1)S(1)}, bf16[3,4,256]{2,1,0:T(4,128)(2,1)S(1)}, u32[]{:S(2)}, u32[]{:S(2)}) collective-permute-start(bf16[3,4,256]{2,1,0:T(4,128)(2,1)S(1)} %reshape.478), channel_id=1, source_target_pairs={{16,0},{48,8},{80,16},{112,24},{144,32},{176,40},{208,48},{240,56}... | collective-permute-start | bytes 18440 | tf_op jit(solution)/shard_map/ppermute | solution.py:212
  200.8 2.0 collective-permute-start.17
  203.6 6.1 %collective-permute-start.15 = (bf16[3,4,256]{2,1,0:T(4,128)(2,1)S(1)}, bf16[3,4,256]{2,1,0:T(4,128)(2,1)S(1)}, u32[]{:S(2)}, u32[]{:S(2)}) collective-permute-start(bf16[3,4,256]{2,1,0:T(4,128)(2,1)S(1)} %reshape.474), channel_id=1, source_target_pairs={{0,0},{32,8},{64,16},{96,24},{128,32},{160,40},{192,48},{224,56},{... | collective-permute-start | bytes 18440 | tf_op jit(solution)/shard_map/ppermute | solution.py:212
  (175 shorter events, 30.4 us)
Async XLA Ops:
  7.2 45.8 %copy-start = (bf16[256,4096]{1,0:T(8,128)(2,1)S(1)}, bf16[256,4096]{1,0:T(8,128)(2,1)}, u32[]{:S(2)}) copy-start(bf16[256,4096]{1,0:T(8,128)(2,1)} %param.25) | copy-start | bytes 6291460
  7.2 119.4 %all-gather.6.cloned.1.call-start = ((), (), s32[]{:S(2)}) async-start(), calls=%async_computation.1 | async-start | bytes 3538944 | tf_op jit(solution)/shard_map/all_gather | solution.py:185
  9.4 4.7 %copy-start.3 = (bf16[4096,256]{1,0:T(8,128)(2,1)S(1)}, bf16[4096,256]{1,0:T(8,128)(2,1)}, u32[]{:S(2)}) copy-start(bf16[4096,256]{1,0:T(8,128)(2,1)} %param.23) | copy-start | bytes 6291460
  11.9 7.3 %copy-start.11 = (bf16[16,32,256]{2,1,0:T(8,128)(2,1)S(1)}, bf16[16,32,256]{2,1,0:T(8,128)(2,1)}, u32[]{:S(2)}) copy-start(bf16[16,32,256]{2,1,0:T(8,128)(2,1)} %param.32) | copy-start | bytes 786436
  11.9 7.3 %copy-start.12 = (bf16[16,32,256]{2,1,0:T(8,128)(2,1)S(1)}, bf16[16,32,256]{2,1,0:T(8,128)(2,1)}, u32[]{:S(2)}) copy-start(bf16[16,32,256]{2,1,0:T(8,128)(2,1)} %param.31) | copy-start | bytes 786436
  14.1 9.7 %copy-start.14 = (s32[3,512]{1,0:T(4,128)S(1)}, s32[3,512]{1,0:T(4,128)}, u32[]{:S(2)}) copy-start(s32[3,512]{1,0:T(4,128)} %param.33) | copy-start | bytes 18436
  14.6 21.0 %collective-permute-start.3 = (bf16[2,3,16,256]{3,2,0,1:T(8,128)(2,1)S(1)}, bf16[2,3,16,256]{3,2,0,1:T(8,128)(2,1)S(1)}, u32[]{:S(2)}, u32[]{:S(2)}) collective-permute-start(bf16[2,3,16,256]{3,2,0,1:T(8,128)(2,1)S(1)} %pad_maximum_fusion.4), channel_id=1, source_target_pairs={{64,0},{72,8},{80,16},{88,24},{96,32},{104,40},{112,48},{120,56},{... | collective-permute-start | bytes 147464 | tf_op jit(solution)/shard_map/ppermute | solution.py:34
  18.2 17.4 %collective-permute-start.4 = (bf16[2,3,16,256]{3,2,0,1:T(8,128)(2,1)S(1)}, bf16[2,3,16,256]{3,2,0,1:T(8,128)(2,1)S(1)}, u32[]{:S(2)}, u32[]{:S(2)}) collective-permute-start(bf16[2,3,16,256]{3,2,0,1:T(8,128)(2,1)S(1)} %pad_maximum_fusion.4), channel_id=1, source_target_pairs={{128,0},{136,8},{144,16},{152,24},{160,32},{168,40},{176,48},{184,... | collective-permute-start | bytes 147464 | tf_op jit(solution)/shard_map/ppermute | solution.py:34
  18.5 17.1 %collective-permute-start.5 = (bf16[2,3,16,256]{3,2,0,1:T(8,128)(2,1)S(1)}, bf16[2,3,16,256]{3,2,0,1:T(8,128)(2,1)S(1)}, u32[]{:S(2)}, u32[]{:S(2)}) collective-permute-start(bf16[2,3,16,256]{3,2,0,1:T(8,128)(2,1)S(1)} %pad_maximum_fusion.4), channel_id=1, source_target_pairs={{192,0},{200,8},{208,16},{216,24},{224,32},{232,40},{240,48},{248,... | collective-permute-start | bytes 147464 | tf_op jit(solution)/shard_map/ppermute | solution.py:34
  20.4 15.5 %collective-permute-start = (bf16[2,16,32,256]{3,1,2,0:T(8,128)(2,1)}, bf16[2,16,32,256]{3,1,2,0:T(8,128)(2,1)}, u32[]{:S(2)}, u32[]{:S(2)}) collective-permute-start(bf16[2,16,32,256]{3,1,2,0:T(8,128)(2,1)} %pad_maximum_fusion.2), channel_id=1, source_target_pairs={{64,0},{72,8},{80,16},{88,24},{96,32},{104,40},{112,48},{120,56},{... | collective-permute-start | bytes 1572872 | tf_op jit(solution)/shard_map/ppermute | solution.py:34
  22.4 13.5 %collective-permute-start.1 = (bf16[2,16,32,256]{3,1,2,0:T(8,128)(2,1)}, bf16[2,16,32,256]{3,1,2,0:T(8,128)(2,1)}, u32[]{:S(2)}, u32[]{:S(2)}) collective-permute-start(bf16[2,16,32,256]{3,1,2,0:T(8,128)(2,1)} %pad_maximum_fusion.2), channel_id=1, source_target_pairs={{128,0},{136,8},{144,16},{152,24},{160,32},{168,40},{176,48},{184,... | collective-permute-start | bytes 1572872 | tf_op jit(solution)/shard_map/ppermute | solution.py:34
  35.5 12.9 %collective-permute-start.2 = (bf16[2,16,32,256]{3,1,2,0:T(8,128)(2,1)}, bf16[2,16,32,256]{3,1,2,0:T(8,128)(2,1)S(1)}, u32[]{:S(2)}, u32[]{:S(2)}) collective-permute-start(bf16[2,16,32,256]{3,1,2,0:T(8,128)(2,1)} %pad_maximum_fusion.2), channel_id=1, source_target_pairs={{192,0},{200,8},{208,16},{216,24},{224,32},{232,40},{240,48},{248,... | collective-permute-start | bytes 1572872 | tf_op jit(solution)/shard_map/ppermute | solution.py:34
  54.2 74.8 %copy-start.1 = (bf16[3,16,4096]{2,1,0:T(8,128)(2,1)S(1)}, bf16[3,16,4096]{2,1,0:T(8,128)(2,1)}, u32[]{:S(2)}) copy-start(bf16[3,16,4096]{2,1,0:T(8,128)(2,1)} %param.18) | copy-start | bytes 1179652
  54.3 125.4 %all-gather.4.cloned.1.call-start = ((), (), s32[]{:S(2)}) async-start(), calls=%async_computation | async-start | bytes 4325376 | tf_op jit(solution)/shard_map/all_gather | solution.py:110
  55.0 25.8 %collective-permute-start.8 = (bf16[768,512]{1,0:T(8,128)(2,1)S(1)}, bf16[768,512]{1,0:T(8,128)(2,1)}, u32[]{:S(2)}, u32[]{:S(2)}) collective-permute-start(bf16[768,512]{1,0:T(8,128)(2,1)S(1)} %copy-done.8), channel_id=1, source_target_pairs={{0,7},{1,0},{2,1},{3,2},{4,3},{5,4},{6,5},{7,6},{8,15},{9,8},{10,9... | collective-permute-start | bytes 2359304 | tf_op jit(solution)/shard_map/ppermute | solution.py:55
  60.7 23.7 %collective-permute-start.7 = (bf16[768,512]{1,0:T(8,128)(2,1)S(1)}, bf16[768,512]{1,0:T(8,128)(2,1)}, u32[]{:S(2)}, u32[]{:S(2)}) collective-permute-start(bf16[768,512]{1,0:T(8,128)(2,1)S(1)} %copy-done.8), channel_id=1, source_target_pairs={{0,1},{1,2},{2,3},{3,4},{4,5},{5,6},{6,7},{7,0},{8,9},{9,10},{10,1... | collective-permute-start | bytes 2359304 | tf_op jit(solution)/shard_map/ppermute | solution.py:54
  80.8 36.4 %collective-permute-start.10 = (bf16[768,512]{1,0:T(8,128)(2,1)}, bf16[768,512]{1,0:T(8,128)(2,1)}, u32[]{:S(2)}, u32[]{:S(2)}) collective-permute-start(bf16[768,512]{1,0:T(8,128)(2,1)} %collective-permute-done.8), channel_id=1, source_target_pairs={{0,7},{1,0},{2,1},{3,2},{4,3},{5,4},{6,5},{7,6},{8,15},{9,8},{10,9... | collective-permute-start | bytes 2359304 | tf_op jit(solution)/shard_map/ppermute | solution.py:55
  84.3 36.3 %collective-permute-start.9 = (bf16[768,512]{1,0:T(8,128)(2,1)}, bf16[768,512]{1,0:T(8,128)(2,1)}, u32[]{:S(2)}, u32[]{:S(2)}) collective-permute-start(bf16[768,512]{1,0:T(8,128)(2,1)} %collective-permute-done.7), channel_id=1, source_target_pairs={{0,1},{1,2},{2,3},{3,4},{4,5},{5,6},{6,7},{7,0},{8,9},{9,10},{10,1... | collective-permute-start | bytes 2359304 | tf_op jit(solution)/shard_map/ppermute | solution.py:54
  117.2 25.9 %collective-permute-start.12 = (bf16[768,512]{1,0:T(8,128)(2,1)}, bf16[768,512]{1,0:T(8,128)(2,1)S(1)}, u32[]{:S(2)}, u32[]{:S(2)}) collective-permute-start(bf16[768,512]{1,0:T(8,128)(2,1)} %collective-permute-done.10), channel_id=1, source_target_pairs={{0,7},{1,0},{2,1},{3,2},{4,3},{5,4},{6,5},{7,6},{8,15},{9,8},{10,9... | collective-permute-start | bytes 2359304 | tf_op jit(solution)/shard_map/ppermute | solution.py:55
  120.6 29.9 %collective-permute-start.11 = (bf16[768,512]{1,0:T(8,128)(2,1)}, bf16[768,512]{1,0:T(8,128)(2,1)}, u32[]{:S(2)}, u32[]{:S(2)}) collective-permute-start(bf16[768,512]{1,0:T(8,128)(2,1)} %collective-permute-done.9), channel_id=1, source_target_pairs={{0,1},{1,2},{2,3},{3,4},{4,5},{5,6},{6,7},{7,0},{8,9},{9,10},{10,1... | collective-permute-start | bytes 2359304 | tf_op jit(solution)/shard_map/ppermute | solution.py:54
  131.2 24.0 %collective-permute-start.20 = (bf16[3,4,256]{2,1,0:T(4,128)(2,1)S(1)}, bf16[3,4,256]{2,1,0:T(4,128)(2,1)S(1)}, u32[]{:S(2)}, u32[]{:S(2)}) collective-permute-start(bf16[3,4,256]{2,1,0:T(4,128)(2,1)S(1)} %get-tuple-element.39), channel_id=1, source_target_pairs={{0,24},{8,56},{16,88},{24,120},{32,152},{40,184},{48,216},{56,248}... | collective-permute-start | bytes 18440 | tf_op jit(solution)/shard_map/ppermute | solution.py:202
  135.5 19.7 %collective-permute-start.18 = (bf16[3,4,256]{2,1,0:T(4,128)(2,1)S(1)}, bf16[3,4,256]{2,1,0:T(4,128)(2,1)S(1)}, u32[]{:S(2)}, u32[]{:S(2)}) collective-permute-start(bf16[3,4,256]{2,1,0:T(4,128)(2,1)S(1)} %get-tuple-element.40), channel_id=1, source_target_pairs={{0,16},{8,48},{16,80},{24,112},{32,144},{40,176},{48,208},{56,240}... | collective-permute-start | bytes 18440 | tf_op jit(solution)/shard_map/ppermute | solution.py:202
  139.8 15.5 %collective-permute-start.16 = (bf16[3,4,256]{2,1,0:T(4,128)(2,1)S(1)}, bf16[3,4,256]{2,1,0:T(4,128)(2,1)S(1)}, u32[]{:S(2)}, u32[]{:S(2)}) collective-permute-start(bf16[3,4,256]{2,1,0:T(4,128)(2,1)S(1)} %get-tuple-element.41), channel_id=1, source_target_pairs={{0,8},{8,40},{16,72},{24,104},{32,136},{40,168},{48,200},{56,232},... | collective-permute-start | bytes 18440 | tf_op jit(solution)/shard_map/ppermute | solution.py:202
  143.0 38.6 %copy-start.5 = (bf16[768,512]{1,0:T(8,128)(2,1)}, bf16[768,512]{1,0:T(8,128)(2,1)S(1)}, u32[]{:S(2)}) copy-start(bf16[768,512]{1,0:T(8,128)(2,1)S(1)} %collective-permute-done.12) | copy-start | bytes 2359300
  143.1 12.2 %collective-permute-start.6 = (bf16[3,4,256]{2,1,0:T(4,128)(2,1)S(1)}, bf16[3,4,256]{2,1,0:T(4,128)(2,1)S(1)}, u32[]{:S(2)}, u32[]{:S(2)}) collective-permute-start(bf16[3,4,256]{2,1,0:T(4,128)(2,1)S(1)} %get-tuple-element.38), channel_id=1, source_target_pairs={{0,0},{8,32},{16,64},{24,96},{32,128},{40,160},{48,192},{56,224},{... | collective-permute-start | bytes 18440 | tf_op jit(solution)/shard_map/ppermute | solution.py:202
  150.5 39.2 %collective-permute-start.14 = (bf16[384,512]{1,0:T(8,128)(2,1)}, bf16[384,512]{1,0:T(8,128)(2,1)S(1)}, u32[]{:S(2)}, u32[]{:S(2)}) collective-permute-start(bf16[384,512]{1,0:T(8,128)(2,1)} %slice.162), channel_id=1, source_target_pairs={{0,7},{1,0},{2,1},{3,2},{4,3},{5,4},{6,5},{7,6},{8,15},{9,8},{10,9... | collective-permute-start | bytes 1179656 | tf_op jit(solution)/shard_map/ppermute | solution.py:60
  155.2 34.4 %collective-permute-start.13 = (bf16[384,512]{1,0:T(8,128)(2,1)}, bf16[384,512]{1,0:T(8,128)(2,1)}, u32[]{:S(2)}, u32[]{:S(2)}) collective-permute-start(bf16[384,512]{1,0:T(8,128)(2,1)} %slice.161), channel_id=1, source_target_pairs={{0,1},{1,2},{2,3},{3,4},{4,5},{5,6},{6,7},{7,0},{8,9},{9,10},{10,1... | collective-permute-start | bytes 1179656 | tf_op jit(solution)/shard_map/ppermute | solution.py:59
  179.6 4.0 %copy-start.2 = (bf16[4096,512]{1,0:T(8,128)(2,1)S(1)}, bf16[4096,512]{1,0:T(8,128)(2,1)}, u32[]{:S(2)}) copy-start(bf16[4096,512]{1,0:T(8,128)(2,1)} %all-gather.4.cloned.1.call-done) | copy-start | bytes 12582916
  193.0 16.8 %collective-permute-start.21 = (bf16[3,4,256]{2,1,0:T(4,128)(2,1)S(1)}, bf16[3,4,256]{2,1,0:T(4,128)(2,1)S(1)}, u32[]{:S(2)}, u32[]{:S(2)}) collective-permute-start(bf16[3,4,256]{2,1,0:T(4,128)(2,1)S(1)} %reshape.480), channel_id=1, source_target_pairs={{24,0},{56,8},{88,16},{120,24},{152,32},{184,40},{216,48},{248,56}... | collective-permute-start | bytes 18440 | tf_op jit(solution)/shard_map/ppermute | solution.py:212
  197.6 12.2 %collective-permute-start.19 = (bf16[3,4,256]{2,1,0:T(4,128)(2,1)S(1)}, bf16[3,4,256]{2,1,0:T(4,128)(2,1)S(1)}, u32[]{:S(2)}, u32[]{:S(2)}) collective-permute-start(bf16[3,4,256]{2,1,0:T(4,128)(2,1)S(1)} %reshape.478), channel_id=1, source_target_pairs={{16,0},{48,8},{80,16},{112,24},{144,32},{176,40},{208,48},{240,56}... | collective-permute-start | bytes 18440 | tf_op jit(solution)/shard_map/ppermute | solution.py:212
  200.8 9.0 %collective-permute-start.17 = (bf16[3,4,256]{2,1,0:T(4,128)(2,1)S(1)}, bf16[3,4,256]{2,1,0:T(4,128)(2,1)S(1)}, u32[]{:S(2)}, u32[]{:S(2)}) collective-permute-start(bf16[3,4,256]{2,1,0:T(4,128)(2,1)S(1)} %reshape.476), channel_id=1, source_target_pairs={{8,0},{40,8},{72,16},{104,24},{136,32},{168,40},{200,48},{232,56},... | collective-permute-start | bytes 18440 | tf_op jit(solution)/shard_map/ppermute | solution.py:212
  203.6 6.9 %collective-permute-start.15 = (bf16[3,4,256]{2,1,0:T(4,128)(2,1)S(1)}, bf16[3,4,256]{2,1,0:T(4,128)(2,1)S(1)}, u32[]{:S(2)}, u32[]{:S(2)}) collective-permute-start(bf16[3,4,256]{2,1,0:T(4,128)(2,1)S(1)} %reshape.474), channel_id=1, source_target_pairs={{0,0},{32,8},{64,16},{96,24},{128,32},{160,40},{192,48},{224,56},{... | collective-permute-start | bytes 18440 | tf_op jit(solution)/shard_map/ppermute | solution.py:212
  (13 other events, 25.7 us)
Sparse Core Ops, SparseCore 0:
  54.4 72.2 all-gather.5
  129.2 50.4 all-gather.3
